TPU v7x, 128 devices: a whole 4x4x4 slice. The times are simulated.
128 devices in a mesh: pair: 16 (over y_lo, x, core), col: 8 (over y_hi, z).
Axes of the slice: x: 4, y: 4 (y_hi: 2, y_lo: 2; y = y_hi * 2 + y_lo), z: 4, core: 2. Of those that a mesh axis runs over, the one named last changes fastest.
Arguments:
- tmatrix: bfloat16 [16, 2, 4096, 4096], P('pair', None, None, 'col'), may hold values from -0.046875 to 0.046875
- translation: bfloat16 [16, 2, 4096, 4096], P('pair', None, None, 'col'), may hold values from -0.0625 to 0.0625
- incident: bfloat16 [16, 4096, 256], P('pair', 'col'), may hold values from -6 to 6
- farfield: bfloat16 [2, 2048, 4096], P(None, None, 'col'), may hold values from -0.0625 to 0.0625
- centres: int32 [16, 3], replicated, may hold values from -8 to 8
Outputs:
- amplitude: float32 [16, 2048, 128], P('pair', 'col')
All inputs are finite; a program needn't handle non-finite values.
Results may differ from a plain program's by a relative error of at most 0.034.
Values may be sent and summed in bfloat16 or wider, within the bound.
No kernel may reach another device: no remote copies, remote signals or barrier semaphores. Data moves between devices by JAX's collectives and lax.ppermute only.
A program may use at most 128 MiB of HBM per device.

v0:
```python
import math

import jax
import jax.numpy as jnp
from jax import lax
from jax.sharding import PartitionSpec as P

ITERS = 3
LEVEL = 2


def partner(value, axis, bit):
    mask = 2**bit
    pairs = [(source, source ^ mask) for source in range(lax.axis_size(axis))]
    return lax.ppermute(value, axis, pairs)


def turned_block(vector):
    half_width = vector.shape[1] // 2
    return jnp.concatenate([-vector[:, half_width:], vector[:, :half_width]], axis=1)


def rotate(field, phase):
    half_width = field.shape[1] // 2
    cosine = jnp.cos(phase)[:, None]
    sine = jnp.sin(phase)[:, None]
    real_part = field[:, :half_width]
    imag_part = field[:, half_width:]
    return jnp.concatenate(
        [cosine * real_part + sine * imag_part, cosine * imag_part - sine * real_part], axis=1
    )


def direction_phase(centre, count, total_rows):
    steps_int = jnp.arange(count, dtype=jnp.int32)
    polar = math.pi / total_rows * (steps_int.astype(jnp.float32) + 0.5)
    azimuth = 2.0 * math.pi / 97.0 * (steps_int * 40 % 97).astype(jnp.float32)
    spot = centre.astype(jnp.float32)
    return 0.7 * (
        jnp.sin(polar) * jnp.cos(azimuth) * spot[0]
        + jnp.sin(polar) * jnp.sin(azimuth) * spot[1]
        + jnp.cos(polar) * spot[2]
    )


def pick_half(vector, column_half, half_width):
    full_width = vector.shape[1] // 2
    real_part = lax.dynamic_slice_in_dim(vector, column_half * half_width, half_width, 1)
    imag_part = lax.dynamic_slice_in_dim(
        vector, full_width + column_half * half_width, half_width, 1
    )
    return jnp.concatenate([real_part, imag_part], axis=1)


def column_sums(operands):
    pieces = []
    for matrix, vector in operands:
        turned = turned_block(vector)
        real_rows = matrix[0]
        imag_rows = matrix[1]
        pieces.append(
            jnp.dot(real_rows, vector, preferred_element_type=jnp.float32)
            + jnp.dot(imag_rows, turned, preferred_element_type=jnp.float32)
        )
    return lax.psum_scatter(
        pieces[0].astype(jnp.bfloat16), "col", scatter_dimension=0, tiled=True
    ).astype(jnp.float32)


def far_sums(farfield, members):
    total_rows = farfield.shape[1]
    count = total_rows // lax.axis_size("col") * lax.axis_size("col")
    real_rows = farfield[0]
    imag_rows = farfield[1]
    summed = None
    for coeffs, centre in members:
        field = jnp.dot(real_rows, coeffs, preferred_element_type=jnp.float32) + jnp.dot(
            imag_rows, turned_block(coeffs), preferred_element_type=jnp.float32
        )
        turned_field = rotate(field, direction_phase(centre, count, total_rows))
        summed = turned_field
    return lax.psum_scatter(
        summed.astype(jnp.bfloat16), "col", scatter_dimension=0, tiled=True
    ).astype(jnp.float32)


def on_device(tmatrix, translation, incident, farfield, centres):
    pair_index = lax.axis_index("pair")
    column_half = jnp.bitwise_and(jnp.right_shift(pair_index, LEVEL), 1)
    own_centre = lax.dynamic_index_in_dim(centres, pair_index, 0, keepdims=False)
    own_matrix = tmatrix[0]
    own_coupling = translation[0]
    own_incident = incident[0]
    full_width = own_incident.shape[1] // 2
    half_width = full_width // 2
    coeffs = column_sums([(own_matrix, own_incident)]).astype(jnp.bfloat16)
    for iteration in range(ITERS):
        partner_coeffs = partner(coeffs, "pair", LEVEL)
        driven = (
            own_incident.astype(jnp.float32) + column_sums([(own_coupling, partner_coeffs)])
        ).astype(jnp.bfloat16)
        coeffs = column_sums([(own_matrix, driven)]).astype(jnp.bfloat16)
    own_field = far_sums(farfield, [(coeffs, own_centre)])
    outgoing = pick_half(own_field, 1 - column_half, half_width)
    incoming = partner(outgoing.astype(jnp.bfloat16), "pair", LEVEL).astype(outgoing.dtype)
    amplitude = pick_half(own_field, column_half, half_width) + incoming
    return amplitude[None]


def solution(mesh):
    return jax.shard_map(
        on_device,
        mesh=mesh,
        in_specs=(
            P("pair", None, None, "col"),
            P("pair", None, None, "col"),
            P("pair", "col", None),
            P(None, None, "col"),
            P(),
        ),
        out_specs=P("pair", "col", None),
        check_vma=False,
    )
```

profile of v0, /device:TPU:0, one launch (start us, length us, event | category | flops | bytes accessed | tf_op | source)
XLA Modules:
  0.0 715.3 jit_solution(11287860804193688039)
XLA Ops:
  6.5 1.1 copy.6
  7.7 3.6 fusion.33
  11.3 1.1 copy-done
  12.4 2.6 fusion.1
  15.1 79.0 %reduce-scatter.9.cloned.1.call-done = bf16[512,256]{1,0:T(8,128)(2,1)} async-done(((bf16[4096,256]{1,0:T(8,128)(2,1)}), bf16[512,256]{1,0:T(8,128)(2,1)}) %reduce-scatter.9.cloned.1.call-update) | async-done | bytes 262160 | tf_op jit(solution)/shard_map/reduce_scatter | solution.py:65
  94.1 3.0 collective-permute-start
  97.0 5.3 collective-permute-done
  102.3 3.5 fusion.18
  105.9 4.8 fusion.13
  110.7 0.0 reduce-scatter.13.cloned.1.call-start
  110.8 75.2 %reduce-scatter.11.cloned.1.call-done = bf16[512,256]{0,1:T(8,128)(2,1)} async-done(((bf16[4096,256]{0,1:T(8,128)(2,1)}), bf16[512,256]{0,1:T(8,128)(2,1)}) %reduce-scatter.11.cloned.1.call-update) | async-done | bytes 262160 | tf_op jit(solution)/shard_map/reduce_scatter | solution.py:65
  186.0 1.0 fusion.55
  187.0 3.5 fusion.31
  190.5 4.8 fusion.12
  195.4 75.2 %reduce-scatter.13.cloned.1.call-done = bf16[512,256]{0,1:T(8,128)(2,1)} async-done(((bf16[4096,256]{0,1:T(8,128)(2,1)}), bf16[512,256]{0,1:T(8,128)(2,1)}) %reduce-scatter.13.cloned.1.call-update) | async-done | bytes 262160 | tf_op jit(solution)/shard_map/reduce_scatter | solution.py:65
  270.6 3.0 collective-permute-start.1
  273.5 5.3 collective-permute-done.1
  278.8 3.5 fusion.16
  282.3 4.8 fusion.11
  287.2 0.2 reduce-scatter.17.cloned.1.call-start
  287.4 75.0 %reduce-scatter.15.cloned.1.call-done = bf16[512,256]{0,1:T(8,128)(2,1)} async-done(((bf16[4096,256]{0,1:T(8,128)(2,1)}), bf16[512,256]{0,1:T(8,128)(2,1)}) %reduce-scatter.15.cloned.1.call-update) | async-done | bytes 262160 | tf_op jit(solution)/shard_map/reduce_scatter | solution.py:65
  362.4 1.0 fusion.56
  363.4 3.5 fusion.29
  366.9 4.8 fusion.10
  371.8 75.2 %reduce-scatter.17.cloned.1.call-done = bf16[512,256]{0,1:T(8,128)(2,1)} async-done(((bf16[4096,256]{0,1:T(8,128)(2,1)}), bf16[512,256]{0,1:T(8,128)(2,1)}) %reduce-scatter.17.cloned.1.call-update) | async-done | bytes 262160 | tf_op jit(solution)/shard_map/reduce_scatter | solution.py:65
  447.0 3.0 collective-permute-start.2
  450.0 5.3 collective-permute-done.2
  455.3 3.5 fusion.14
  458.8 4.8 fusion.9
  463.6 0.0 reduce-scatter.21.cloned.1.call-start
  463.7 75.2 %reduce-scatter.19.cloned.1.call-done = bf16[512,256]{0,1:T(8,128)(2,1)} async-done(((bf16[4096,256]{0,1:T(8,128)(2,1)}), bf16[512,256]{0,1:T(8,128)(2,1)}) %reduce-scatter.19.cloned.1.call-update) | async-done | bytes 262160 | tf_op jit(solution)/shard_map/reduce_scatter | solution.py:65
  538.8 1.0 fusion.57
  539.9 3.5 fusion.27
  543.4 4.8 fusion.8
  548.3 0.1 dynamic-slice_convert_fusion.2
  548.4 0.6 fusion.114
  549.0 2.1 fusion.104
  551.0 72.4 %reduce-scatter.21.cloned.1.call-done = bf16[512,256]{0,1:T(8,128)(2,1)} async-done(((bf16[4096,256]{0,1:T(8,128)(2,1)}), bf16[512,256]{0,1:T(8,128)(2,1)}) %reduce-scatter.21.cloned.1.call-update) | async-done | bytes 262160 | tf_op jit(solution)/shard_map/reduce_scatter | solution.py:65
  623.4 1.1 slice_negate_fusion
  624.5 2.6 fusion.51
  627.2 0.7 fusion.41
  628.0 0.3 add_convert_fusion
  628.2 1.1 pad_maximum_fusion
  629.4 71.5 %reduce-scatter.23.cloned.1.call-done = bf16[256,256]{0,1:T(8,128)(2,1)} async-done(((bf16[2048,256]{0,1:T(8,128)(2,1)}), bf16[256,256]{0,1:T(8,128)(2,1)}) %reduce-scatter.23.cloned.1.call-update) | async-done | bytes 131088 | tf_op jit(solution)/shard_map/reduce_scatter | solution.py:82
  700.9 0.9 convert_element_type.131
  701.9 3.0 collective-permute-start.3
  704.9 2.8 collective-permute-done.3
  707.7 0.8 copy.8
  (29 shorter events, 0.5 us)
Async XLA Ops:
  6.5 87.5 %reduce-scatter.9.cloned.1.call-start = ((), (), s32[]{:S(2)}) async-start(), calls=%async_computation.8 | async-start | bytes 2359296 | tf_op jit(solution)/shard_map/reduce_scatter | solution.py:65
  7.7 4.7 copy-start
  15.0 170.9 %reduce-scatter.11.cloned.1.call-start = ((), (), s32[]{:S(2)}) async-start(), calls=%async_computation.9 | async-start | bytes 2359296 | tf_op jit(solution)/shard_map/reduce_scatter | solution.py:65
  94.1 8.2 %collective-permute-start = (bf16[512,256]{1,0:T(8,128)(2,1)}, bf16[512,256]{1,0:T(8,128)(2,1)S(1)}, u32[]{:S(2)}, u32[]{:S(2)}) collective-permute-start(bf16[512,256]{1,0:T(8,128)(2,1)} %reduce-scatter.9.cloned.1.call-done), channel_id=1, source_target_pairs={{0,32},{8,40},{16,48},{24,56},{32,0},{40,8},{48,16},{56,24},{64,96... | collective-permute-start | bytes 786440 | tf_op jit(solution)/shard_map/ppermute | solution.py:15
  110.7 159.8 %reduce-scatter.13.cloned.1.call-start = ((), (), s32[]{:S(2)}) async-start(), calls=%async_computation.10 | async-start | bytes 2359296 | tf_op jit(solution)/shard_map/reduce_scatter | solution.py:65
  195.3 167.1 %reduce-scatter.15.cloned.1.call-start = ((), (), s32[]{:S(2)}) async-start(), calls=%async_computation.11 | async-start | bytes 2359296 | tf_op jit(solution)/shard_map/reduce_scatter | solution.py:65
  270.6 8.2 %collective-permute-start.1 = (bf16[512,256]{0,1:T(8,128)(2,1)}, bf16[512,256]{0,1:T(8,128)(2,1)S(1)}, u32[]{:S(2)}, u32[]{:S(2)}) collective-permute-start(bf16[512,256]{0,1:T(8,128)(2,1)} %reduce-scatter.13.cloned.1.call-done), channel_id=1, source_target_pairs={{0,32},{8,40},{16,48},{24,56},{32,0},{40,8},{48,16},{56,24},{64,96... | collective-permute-start | bytes 786440 | tf_op jit(solution)/shard_map/ppermute | solution.py:15
  287.2 159.9 %reduce-scatter.17.cloned.1.call-start = ((), (), s32[]{:S(2)}) async-start(), calls=%async_computation.12 | async-start | bytes 2359296 | tf_op jit(solution)/shard_map/reduce_scatter | solution.py:65
  371.8 167.1 %reduce-scatter.19.cloned.1.call-start = ((), (), s32[]{:S(2)}) async-start(), calls=%async_computation.13 | async-start | bytes 2359296 | tf_op jit(solution)/shard_map/reduce_scatter | solution.py:65
  447.0 8.3 %collective-permute-start.2 = (bf16[512,256]{0,1:T(8,128)(2,1)}, bf16[512,256]{0,1:T(8,128)(2,1)S(1)}, u32[]{:S(2)}, u32[]{:S(2)}) collective-permute-start(bf16[512,256]{0,1:T(8,128)(2,1)} %reduce-scatter.17.cloned.1.call-done), channel_id=1, source_target_pairs={{0,32},{8,40},{16,48},{24,56},{32,0},{40,8},{48,16},{56,24},{64,96... | collective-permute-start | bytes 786440 | tf_op jit(solution)/shard_map/ppermute | solution.py:15
  463.6 159.8 %reduce-scatter.21.cloned.1.call-start = ((), (), s32[]{:S(2)}) async-start(), calls=%async_computation.14 | async-start | bytes 2359296 | tf_op jit(solution)/shard_map/reduce_scatter | solution.py:65
  543.4 4.9 copy-start.2
  548.2 152.7 %reduce-scatter.23.cloned.1.call-start = ((), (), s32[]{:S(2)}) async-start(), calls=%async_computation.15 | async-start | bytes 1179648 | tf_op jit(solution)/shard_map/reduce_scatter | solution.py:82
  623.4 3.8 copy-start.1
  701.9 5.8 collective-permute-start.3
Sparse Core Ops, SparseCore 0:
  15.2 78.8 reduce-scatter.8
  110.8 75.0 reduce-scatter.10
  195.5 75.0 reduce-scatter.12
  287.3 75.0 reduce-scatter.14
  371.9 75.0 reduce-scatter.16
  463.7 75.0 reduce-scatter.18
  548.3 75.0 reduce-scatter.20
  629.5 71.3 reduce-scatter.22
where the time goes:
time: 716 us; the launch traced here: 715 us
  waiting for transfers between devices  617 us (86%)
  matrix products  59.4 us (8%)
  between operations  13.7 us (2%)
  starting transfers between devices  12.4 us (2%)
  other arithmetic  8.81 us (1%)
    reduce_scatter x7, waiting for transfers between devices, column_sums(): lax.psum_scatter(pieces[0].astype(jnp.bfloat16), 'col', scatter_dimension...  527 us
    reduce_scatter x1, waiting for transfers between devices, far_sums(): lax.psum_scatter(summed.astype(jnp.bfloat16), 'col', scatter_dimension=0,...  71.5 us
    dot_general x7, matrix products, column_sums(): jnp.dot(real_rows, vector, preferred_element_type=jnp.float32)  28.5 us
    dot_general x7, matrix products, column_sums(): jnp.dot(imag_rows, turned, preferred_element_type=jnp.float32)  27.5 us
    ppermute x4, waiting for transfers between devices, partner(): return lax.ppermute(value, axis, pairs)  18.6 us
  transfers between devices with their start and end apart: 12, of which 12 were waited for; matrix products, arithmetic and copies ran while one was open for 0% of the time, Pallas kernels for 0%

commit v1 on v0

--- a/solution.py
+++ b/solution.py
@@ -52,58 +52,52 @@
     return jnp.concatenate([real_part, imag_part], axis=1)
 
 
-def column_sums(operands):
-    pieces = []
-    for matrix, vector in operands:
-        turned = turned_block(vector)
-        real_rows = matrix[0]
-        imag_rows = matrix[1]
-        pieces.append(
-            jnp.dot(real_rows, vector, preferred_element_type=jnp.float32)
-            + jnp.dot(imag_rows, turned, preferred_element_type=jnp.float32)
-        )
-    return lax.psum_scatter(
-        pieces[0].astype(jnp.bfloat16), "col", scatter_dimension=0, tiled=True
-    ).astype(jnp.float32)
+def col_sum(partial):
+    count = lax.axis_size("col")
+    rows, width = partial.shape
+    blocks = partial.astype(jnp.bfloat16).reshape(count, rows // count, width)
+    received = lax.all_to_all(blocks, "col", 0, 0)
+    return jnp.sum(received.astype(jnp.float32), axis=0)
 
 
-def far_sums(farfield, members):
-    total_rows = farfield.shape[1]
-    count = total_rows // lax.axis_size("col") * lax.axis_size("col")
-    real_rows = farfield[0]
-    imag_rows = farfield[1]
-    summed = None
-    for coeffs, centre in members:
-        field = jnp.dot(real_rows, coeffs, preferred_element_type=jnp.float32) + jnp.dot(
-            imag_rows, turned_block(coeffs), preferred_element_type=jnp.float32
-        )
-        turned_field = rotate(field, direction_phase(centre, count, total_rows))
-        summed = turned_field
-    return lax.psum_scatter(
-        summed.astype(jnp.bfloat16), "col", scatter_dimension=0, tiled=True
-    ).astype(jnp.float32)
+def product(matrix, vector):
+    return jnp.dot(matrix[0], vector, preferred_element_type=jnp.float32) + jnp.dot(
+        matrix[1], turned_block(vector), preferred_element_type=jnp.float32
+    )
 
 
 def on_device(tmatrix, translation, incident, farfield, centres):
     pair_index = lax.axis_index("pair")
     column_half = jnp.bitwise_and(jnp.right_shift(pair_index, LEVEL), 1)
     own_centre = lax.dynamic_index_in_dim(centres, pair_index, 0, keepdims=False)
+    other_centre = lax.dynamic_index_in_dim(
+        centres, jnp.bitwise_xor(pair_index, 2**LEVEL), 0, keepdims=False
+    )
     own_matrix = tmatrix[0]
     own_coupling = translation[0]
     own_incident = incident[0]
     full_width = own_incident.shape[1] // 2
     half_width = full_width // 2
-    coeffs = column_sums([(own_matrix, own_incident)]).astype(jnp.bfloat16)
+    coeffs = col_sum(product(own_matrix, own_incident)).astype(jnp.bfloat16)
     for iteration in range(ITERS):
         partner_coeffs = partner(coeffs, "pair", LEVEL)
         driven = (
-            own_incident.astype(jnp.float32) + column_sums([(own_coupling, partner_coeffs)])
+            own_incident.astype(jnp.float32) + col_sum(product(own_coupling, partner_coeffs))
         ).astype(jnp.bfloat16)
-        coeffs = column_sums([(own_matrix, driven)]).astype(jnp.bfloat16)
-    own_field = far_sums(farfield, [(coeffs, own_centre)])
-    outgoing = pick_half(own_field, 1 - column_half, half_width)
-    incoming = partner(outgoing.astype(jnp.bfloat16), "pair", LEVEL).astype(outgoing.dtype)
-    amplitude = pick_half(own_field, column_half, half_width) + incoming
+        coeffs = col_sum(product(own_matrix, driven)).astype(jnp.bfloat16)
+    incoming = partner(pick_half(coeffs, 1 - column_half, half_width), "pair", LEVEL)
+    own_half = pick_half(coeffs, column_half, half_width)
+    total_rows = farfield.shape[1]
+    both = jnp.concatenate([own_half, incoming], axis=1)
+    both_turned = jnp.concatenate([turned_block(own_half), turned_block(incoming)], axis=1)
+    field = jnp.dot(farfield[0], both, preferred_element_type=jnp.float32) + jnp.dot(
+        farfield[1], both_turned, preferred_element_type=jnp.float32
+    )
+    width = own_half.shape[1]
+    merged = rotate(field[:, :width], direction_phase(own_centre, total_rows, total_rows)) + rotate(
+        field[:, width:], direction_phase(other_centre, total_rows, total_rows)
+    )
+    amplitude = col_sum(merged)
     return amplitude[None]
 
 

time: 716 us -> 285 us (0.40)
  waiting for transfers between devices: 617 us -> 27.3 us
  blocking collectives: 0 us -> 185 us
  matrix products: 59.4 us -> 37 us
  between operations: 13.7 us -> 0.52 us
    reduce_scatter x8 -> x0, waiting for transfers between devices: 599 us -> none  [the longest x7 527 us: column_sums(): lax.psum_scatter(pieces[0].astype(jnp.bfloat16), 'col', scatter_dimension...]
    all_to_all x0 -> x7, blocking collectives: none -> 185 us  [col_sum(): received = lax.all_to_all(blocks, 'col', 0, 0)]
    dot_general x16, matrix products: 59.4 us -> 37 us  [the longest x7 18.4 us: product(): jnp.dot(matrix[0], vector, preferred_element_type=jnp.float32)]
    all_to_all x0 -> x1, waiting for transfers between devices: none -> 12.8 us  [col_sum(): received = lax.all_to_all(blocks, 'col', 0, 0)]
  transfers between devices with their start and end apart: 12 -> 5, of which waited for: 12 -> 4; matrix products, arithmetic and copies ran while one was open for 0% -> 3% of each run, Pallas kernels for 0% -> 0%
where the time goes in v1:
time: 285 us; the launch traced here: 284 us
  blocking collectives  185 us (65%)
  matrix products  37 us (13%)
  waiting for transfers between devices  27.3 us (10%)
  starting transfers between devices  16.1 us (6%)
  other arithmetic  11.7 us (4%)
  local copies, waits for them, and re-layouts  6.27 us (2%)
    all_to_all x7, blocking collectives, col_sum(): received = lax.all_to_all(blocks, 'col', 0, 0)  185 us
    dot_general x7, matrix products, product(): jnp.dot(matrix[0], vector, preferred_element_type=jnp.float32)  18.4 us
    dot_general x7, matrix products, product(): jnp.dot(matrix[1], turned_block(vector), preferred_element_type=jnp.float32)  15.6 us
    ppermute x4, waiting for transfers between devices, partner(): return lax.ppermute(value, axis, pairs)  14.5 us
    all_to_all x1, waiting for transfers between devices, col_sum(): received = lax.all_to_all(blocks, 'col', 0, 0)  12.8 us
    ppermute x4, starting transfers between devices, partner(): return lax.ppermute(value, axis, pairs)  12.5 us
  transfers between devices with their start and end apart: 5, of which 4 were waited for; matrix products, arithmetic and copies ran while one was open for 3% of the time, Pallas kernels for 0%

profile of v1, /device:TPU:0, one launch (start us, length us, event | category | flops | bytes accessed | tf_op | source)
XLA Modules:
  0.0 284.0 jit_solution(14828228203111991098)
XLA Ops:
  0.0 1.1 copy.7
  1.1 3.6 %fusion.27 = f32[4096,256]{1,0:T(8,128)S(1)} fusion(bf16[1,2,4096,512]{3,2,1,0:T(8,128)(2,1)} %param.5, bf16[1,512,256]{2,1,0:T(8,128)(2,1)} %param.7), kind=kOutput, calls=%fused_computation.34 | convolution fusion | flops 1073741824 | bytes 8650752 | tf_op jit(solution)/shard_map/dot_general | solution.py:64
  4.8 1.1 copy-done
  5.8 1.3 fusion.1
  7.1 36.2 %all_to_all.40 = bf16[8,512,256]{2,1,0:T(8,128)(2,1)S(1)} all-to-all(bf16[8,512,256]{2,1,0:T(8,128)(2,1)S(1)} %bitcast.157), channel_id=1, replica_groups=mesh['pair'=16,'col'=8] {'col'}, dimensions={0} | all-to-all | bytes 4194304 | tf_op jit(solution)/shard_map/all_to_all | solution.py:59
  43.4 0.4 reduce_sum.90
  43.8 3.1 %collective-permute-start = (bf16[512,256]{1,0:T(8,128)(2,1)S(1)}, bf16[512,256]{1,0:T(8,128)(2,1)S(1)}, u32[]{:S(2)}, u32[]{:S(2)}) collective-permute-start(bf16[512,256]{1,0:T(8,128)(2,1)S(1)} %reduce_sum.90), channel_id=1, source_target_pairs={{0,32},{8,40},{16,48},{24,56},{32,0},{40,8},{48,16},{56,24},{64,96... | collective-permute-start | bytes 786440 | tf_op jit(solution)/shard_map/ppermute | solution.py:15
  46.9 4.8 %collective-permute-done = bf16[512,256]{1,0:T(8,128)(2,1)S(1)} collective-permute-done((bf16[512,256]{1,0:T(8,128)(2,1)S(1)}, bf16[512,256]{1,0:T(8,128)(2,1)S(1)}, u32[]{:S(2)}, u32[]{:S(2)}) %collective-permute-start) | collective-permute-done | bytes 262176 | tf_op jit(solution)/shard_map/ppermute | solution.py:15
  51.8 3.5 %fusion.12 = f32[256,4096]{1,0:T(8,128)S(1)} fusion(bf16[1,2,4096,512]{3,2,1,0:T(8,128)(2,1)} %param.6, bf16[512,128]{1,0:T(8,128)(2,1)S(1)} %get-tuple-element.27, bf16[512,128]{1,0:T(8,128)(2,1)S(1)} %get-tuple-element.26), kind=kOutput, calls=%fused_computation.19 | convolution fusion | flops 1074266112 | bytes 8650752 | tf_op jit(solution)/shard_map/dot_general | solution.py:64
  55.3 3.7 %fusion.2 = bf16[256,4096]{1,0:T(8,128)(2,1)S(1)} fusion(f32[256,4096]{1,0:T(8,128)S(1)} %fusion.12, bf16[512,256]{1,0:T(8,128)(2,1)S(1)} %collective-permute-done, bf16[1,2,4096,512]{3,2,1,0:T(8,128)(2,1)} %param.6), kind=kOutput, calls=%fused_computation.9 | convolution fusion | flops 1075838976 | bytes 10747904 | tf_op jit(solution)/shard_map/dot_general | solution.py:64
  59.1 29.8 %all_to_all.41 = bf16[8,512,256]{1,2,0:T(8,128)(2,1)S(1)} all-to-all(bf16[8,512,256]{1,2,0:T(8,128)(2,1)S(1)} %bitcast.142), channel_id=1, replica_groups=mesh['pair'=16,'col'=8] {'col'}, dimensions={0} | all-to-all | bytes 4194304 | tf_op jit(solution)/shard_map/all_to_all | solution.py:59
  88.9 0.3 convert_reduce_fusion.2
  89.3 1.3 fusion.25
  90.7 1.3 fusion.3
  92.2 28.3 %all_to_all.42 = bf16[8,512,256]{1,2,0:T(8,128)(2,1)S(1)} all-to-all(bf16[8,512,256]{1,2,0:T(8,128)(2,1)S(1)} %bitcast.143), channel_id=1, replica_groups=mesh['pair'=16,'col'=8] {'col'}, dimensions={0} | all-to-all | bytes 4194304 | tf_op jit(solution)/shard_map/all_to_all | solution.py:59
  120.5 0.4 reduce_sum.93
  120.9 3.1 %collective-permute-start.1 = (bf16[512,256]{0,1:T(8,128)(2,1)S(1)}, bf16[512,256]{0,1:T(8,128)(2,1)S(1)}, u32[]{:S(2)}, u32[]{:S(2)}) collective-permute-start(bf16[512,256]{0,1:T(8,128)(2,1)S(1)} %reduce_sum.93), channel_id=1, source_target_pairs={{0,32},{8,40},{16,48},{24,56},{32,0},{40,8},{48,16},{56,24},{64,96... | collective-permute-start | bytes 786440 | tf_op jit(solution)/shard_map/ppermute | solution.py:15
  124.0 4.8 %collective-permute-done.1 = bf16[512,256]{0,1:T(8,128)(2,1)S(1)} collective-permute-done((bf16[512,256]{0,1:T(8,128)(2,1)S(1)}, bf16[512,256]{0,1:T(8,128)(2,1)S(1)}, u32[]{:S(2)}, u32[]{:S(2)}) %collective-permute-start.1) | collective-permute-done | bytes 262176 | tf_op jit(solution)/shard_map/ppermute | solution.py:15
  128.9 3.5 %fusion.10 = f32[256,4096]{1,0:T(8,128)S(1)} fusion(bf16[1,2,4096,512]{3,2,1,0:T(8,128)(2,1)} %param.6, bf16[512,128]{0,1:T(8,128)(2,1)S(1)} %get-tuple-element.23, bf16[512,128]{0,1:T(8,128)(2,1)S(1)} %get-tuple-element.22), kind=kOutput, calls=%fused_computation.17 | convolution fusion | flops 1074266112 | bytes 8650752 | tf_op jit(solution)/shard_map/dot_general | solution.py:64
  132.4 3.6 %fusion.4 = bf16[256,4096]{1,0:T(8,128)(2,1)S(1)} fusion(f32[256,4096]{1,0:T(8,128)S(1)} %fusion.10, bf16[512,256]{0,1:T(8,128)(2,1)S(1)} %collective-permute-done.1, bf16[1,2,4096,512]{3,2,1,0:T(8,128)(2,1)} %param.6), kind=kOutput, calls=%fused_computation.11 | convolution fusion | flops 1075838976 | bytes 10747904 | tf_op jit(solution)/shard_map/dot_general | solution.py:64
  136.2 26.7 %all_to_all.43 = bf16[8,512,256]{1,2,0:T(8,128)(2,1)S(1)} all-to-all(bf16[8,512,256]{1,2,0:T(8,128)(2,1)S(1)} %bitcast.144), channel_id=1, replica_groups=mesh['pair'=16,'col'=8] {'col'}, dimensions={0} | all-to-all | bytes 4194304 | tf_op jit(solution)/shard_map/all_to_all | solution.py:59
  163.2 1.3 fusion.23
  164.6 1.3 fusion.5
  166.1 25.5 %all_to_all.44 = bf16[8,512,256]{1,2,0:T(8,128)(2,1)S(1)} all-to-all(bf16[8,512,256]{1,2,0:T(8,128)(2,1)S(1)} %bitcast.145), channel_id=1, replica_groups=mesh['pair'=16,'col'=8] {'col'}, dimensions={0} | all-to-all | bytes 4194304 | tf_op jit(solution)/shard_map/all_to_all | solution.py:59
  191.7 0.4 reduce_sum.96
  192.0 3.1 %collective-permute-start.2 = (bf16[512,256]{0,1:T(8,128)(2,1)S(1)}, bf16[512,256]{0,1:T(8,128)(2,1)S(1)}, u32[]{:S(2)}, u32[]{:S(2)}) collective-permute-start(bf16[512,256]{0,1:T(8,128)(2,1)S(1)} %reduce_sum.96), channel_id=1, source_target_pairs={{0,32},{8,40},{16,48},{24,56},{32,0},{40,8},{48,16},{56,24},{64,96... | collective-permute-start | bytes 786440 | tf_op jit(solution)/shard_map/ppermute | solution.py:15
  195.2 4.8 %collective-permute-done.2 = bf16[512,256]{0,1:T(8,128)(2,1)S(1)} collective-permute-done((bf16[512,256]{0,1:T(8,128)(2,1)S(1)}, bf16[512,256]{0,1:T(8,128)(2,1)S(1)}, u32[]{:S(2)}, u32[]{:S(2)}) %collective-permute-start.2) | collective-permute-done | bytes 262176 | tf_op jit(solution)/shard_map/ppermute | solution.py:15
  200.0 3.5 %fusion.8 = f32[256,4096]{1,0:T(8,128)S(1)} fusion(bf16[1,2,4096,512]{3,2,1,0:T(8,128)(2,1)} %param.6, bf16[512,128]{0,1:T(8,128)(2,1)S(1)} %get-tuple-element.19, bf16[512,128]{0,1:T(8,128)(2,1)S(1)} %get-tuple-element.18), kind=kOutput, calls=%fused_computation.15 | convolution fusion | flops 1074266112 | bytes 8650752 | tf_op jit(solution)/shard_map/dot_general | solution.py:64
  203.5 3.6 %fusion.6 = bf16[256,4096]{1,0:T(8,128)(2,1)S(1)} fusion(f32[256,4096]{1,0:T(8,128)S(1)} %fusion.8, bf16[512,256]{0,1:T(8,128)(2,1)S(1)} %collective-permute-done.2, bf16[1,2,4096,512]{3,2,1,0:T(8,128)(2,1)} %param.6), kind=kOutput, calls=%fused_computation.13 | convolution fusion | flops 1075838976 | bytes 10747904 | tf_op jit(solution)/shard_map/dot_general | solution.py:64
  207.4 23.7 %all_to_all.45 = bf16[8,512,256]{1,2,0:T(8,128)(2,1)S(1)} all-to-all(bf16[8,512,256]{1,2,0:T(8,128)(2,1)S(1)} %bitcast.146), channel_id=1, replica_groups=mesh['pair'=16,'col'=8] {'col'}, dimensions={0} | all-to-all | bytes 4194304 | tf_op jit(solution)/shard_map/all_to_all | solution.py:59
  231.1 0.3 convert_reduce_fusion
  231.4 1.3 fusion.21
  232.8 1.3 fusion.7
  234.1 1.5 copy.60
  235.6 3.6 %all-to-all-start.6 = ((bf16[8,512,256]{1,2,0:T(8,128)(2,1)}), bf16[8,512,256]{1,2,0:T(8,128)(2,1)S(1)}, u32[]{:S(2)}, u32[]{:S(2)}) async-start(bf16[8,512,256]{1,2,0:T(8,128)(2,1)} %bitcast.141), calls=%async_computation.6 | async-start | bytes 4194304 | tf_op jit(solution)/shard_map/all_to_all | solution.py:59
  239.4 0.6 fusion.130
  240.0 2.0 fusion.116
  241.9 2.0 fusion.117
  243.9 12.8 %all-to-all-done.6 = bf16[8,512,256]{1,2,0:T(8,128)(2,1)S(1)} async-done(((bf16[8,512,256]{1,2,0:T(8,128)(2,1)}), bf16[8,512,256]{1,2,0:T(8,128)(2,1)S(1)}, u32[]{:S(2)}, u32[]{:S(2)}) %all-to-all-start.6) | async-done | bytes 2097184 | tf_op jit(solution)/shard_map/all_to_all | solution.py:59
  256.6 0.4 reduce_sum.99
  257.1 3.1 %collective-permute-start.3 = (bf16[512,128]{0,1:T(8,128)(2,1)S(1)}, bf16[512,128]{0,1:T(8,128)(2,1)S(1)}, u32[]{:S(2)}, u32[]{:S(2)}) collective-permute-start(bf16[512,128]{0,1:T(8,128)(2,1)S(1)} %pad_maximum_fusion), channel_id=1, source_target_pairs={{0,32},{8,40},{16,48},{24,56},{32,0},{40,8},{48,16},{56,24},{64,96... | collective-permute-start | bytes 393224 | tf_op jit(solution)/shard_map/ppermute | solution.py:15
  260.2 2.1 fusion.118
  262.3 2.1 fusion.119
  264.4 2.3 fusion.44
  266.8 0.7 fusion.35
  267.5 0.4 multiply_add_fusion
  268.3 14.8 %all_to_all.46 = bf16[8,256,128]{1,2,0:T(8,128)(2,1)S(1)} all-to-all(bf16[8,256,128]{1,2,0:T(8,128)(2,1)S(1)} %fusion.49), channel_id=1, replica_groups=mesh['pair'=16,'col'=8] {'col'}, dimensions={0} | all-to-all | bytes 1048576 | tf_op jit(solution)/shard_map/all_to_all | solution.py:59
  283.2 0.8 copy.27
  (47 shorter events, 2.3 us)
Async XLA Ops:
  1.1 4.7 %copy-start = (bf16[1,2,4096,512]{3,2,1,0:T(8,128)(2,1)S(1)}, bf16[1,2,4096,512]{3,2,1,0:T(8,128)(2,1)}, u32[]{:S(2)}) copy-start(bf16[1,2,4096,512]{3,2,1,0:T(8,128)(2,1)} %param.5) | copy-start | bytes 25165828
  43.8 8.0 %collective-permute-start = (bf16[512,256]{1,0:T(8,128)(2,1)S(1)}, bf16[512,256]{1,0:T(8,128)(2,1)S(1)}, u32[]{:S(2)}, u32[]{:S(2)}) collective-permute-start(bf16[512,256]{1,0:T(8,128)(2,1)S(1)} %reduce_sum.90), channel_id=1, source_target_pairs={{0,32},{8,40},{16,48},{24,56},{32,0},{40,8},{48,16},{56,24},{64,96... | collective-permute-start | bytes 786440 | tf_op jit(solution)/shard_map/ppermute | solution.py:15
  55.3 34.1 %slice-start = ((s8[8388608]{0:T(1024)(128)(4,1)}), s8[4194304]{0:T(1024)(128)(4,1)S(1)}, s32[]{:S(2)}) async-start(s8[8388608]{0:T(1024)(128)(4,1)} %bitcast.134), calls=%async_computation.8 | async-start | bytes 8388608
  58.9 30.4 %slice-start.1 = ((s8[8388608]{0:T(1024)(128)(4,1)}), s8[4194304]{0:T(1024)(128)(4,1)S(1)}, s32[]{:S(2)}) async-start(s8[8388608]{0:T(1024)(128)(4,1)} %bitcast.134), calls=%async_computation.9 | async-start | bytes 8388608
  120.9 8.0 %collective-permute-start.1 = (bf16[512,256]{0,1:T(8,128)(2,1)S(1)}, bf16[512,256]{0,1:T(8,128)(2,1)S(1)}, u32[]{:S(2)}, u32[]{:S(2)}) collective-permute-start(bf16[512,256]{0,1:T(8,128)(2,1)S(1)} %reduce_sum.93), channel_id=1, source_target_pairs={{0,32},{8,40},{16,48},{24,56},{32,0},{40,8},{48,16},{56,24},{64,96... | collective-permute-start | bytes 786440 | tf_op jit(solution)/shard_map/ppermute | solution.py:15
  132.4 30.8 %slice-start.2 = ((s8[8388608]{0:T(1024)(128)(4,1)}), s8[4194304]{0:T(1024)(128)(4,1)S(1)}, s32[]{:S(2)}) async-start(s8[8388608]{0:T(1024)(128)(4,1)} %bitcast.136), calls=%async_computation.10 | async-start | bytes 8388608
  136.0 27.2 %slice-start.3 = ((s8[8388608]{0:T(1024)(128)(4,1)}), s8[4194304]{0:T(1024)(128)(4,1)S(1)}, s32[]{:S(2)}) async-start(s8[8388608]{0:T(1024)(128)(4,1)} %bitcast.136), calls=%async_computation.11 | async-start | bytes 8388608
  192.0 8.0 %collective-permute-start.2 = (bf16[512,256]{0,1:T(8,128)(2,1)S(1)}, bf16[512,256]{0,1:T(8,128)(2,1)S(1)}, u32[]{:S(2)}, u32[]{:S(2)}) collective-permute-start(bf16[512,256]{0,1:T(8,128)(2,1)S(1)} %reduce_sum.96), channel_id=1, source_target_pairs={{0,32},{8,40},{16,48},{24,56},{32,0},{40,8},{48,16},{56,24},{64,96... | collective-permute-start | bytes 786440 | tf_op jit(solution)/shard_map/ppermute | solution.py:15
  203.5 27.9 %slice-start.4 = ((s8[8388608]{0:T(1024)(128)(4,1)}), s8[4194304]{0:T(1024)(128)(4,1)S(1)}, s32[]{:S(2)}) async-start(s8[8388608]{0:T(1024)(128)(4,1)} %bitcast.138), calls=%async_computation.12 | async-start | bytes 8388608
  207.1 24.2 %slice-start.5 = ((s8[8388608]{0:T(1024)(128)(4,1)}), s8[4194304]{0:T(1024)(128)(4,1)S(1)}, s32[]{:S(2)}) async-start(s8[8388608]{0:T(1024)(128)(4,1)} %bitcast.138), calls=%async_computation.13 | async-start | bytes 8388608
  234.1 5.2 %copy-start.2 = (s32[16,3]{0,1:T(4,128)S(1)}, s32[16,3]{0,1:T(4,128)}, u32[]{:S(2)}) copy-start(s32[16,3]{0,1:T(4,128)} %param.9) | copy-start | bytes 580
  235.6 21.0 %all-to-all-start.6 = ((bf16[8,512,256]{1,2,0:T(8,128)(2,1)}), bf16[8,512,256]{1,2,0:T(8,128)(2,1)S(1)}, u32[]{:S(2)}, u32[]{:S(2)}) async-start(bf16[8,512,256]{1,2,0:T(8,128)(2,1)} %bitcast.141), calls=%async_computation.6 | async-start | bytes 4194304 | tf_op jit(solution)/shard_map/all_to_all | solution.py:59
  257.0 9.8 %copy-start.1 = (bf16[2,2048,512]{2,1,0:T(8,128)(2,1)S(1)}, bf16[2,2048,512]{2,1,0:T(8,128)(2,1)}, u32[]{:S(2)}) copy-start(bf16[2,2048,512]{2,1,0:T(8,128)(2,1)} %param.8) | copy-start | bytes 12582916
  257.1 7.3 %collective-permute-start.3 = (bf16[512,128]{0,1:T(8,128)(2,1)S(1)}, bf16[512,128]{0,1:T(8,128)(2,1)S(1)}, u32[]{:S(2)}, u32[]{:S(2)}) collective-permute-start(bf16[512,128]{0,1:T(8,128)(2,1)S(1)} %pad_maximum_fusion), channel_id=1, source_target_pairs={{0,32},{8,40},{16,48},{24,56},{32,0},{40,8},{48,16},{56,24},{64,96... | collective-permute-start | bytes 393224 | tf_op jit(solution)/shard_map/ppermute | solution.py:15

commit v2 on v1

--- a/solution.py
+++ b/solution.py
@@ -66,6 +66,21 @@
     )
 
 
+CHUNKS = 2
+
+
+def column_chunk(vector, index, count):
+    full_width = vector.shape[1] // 2
+    width = full_width // count
+    return jnp.concatenate(
+        [
+            vector[:, index * width : (index + 1) * width],
+            vector[:, full_width + index * width : full_width + (index + 1) * width],
+        ],
+        axis=1,
+    )
+
+
 def on_device(tmatrix, translation, incident, farfield, centres):
     pair_index = lax.axis_index("pair")
     column_half = jnp.bitwise_and(jnp.right_shift(pair_index, LEVEL), 1)
@@ -76,17 +91,32 @@
     own_matrix = tmatrix[0]
     own_coupling = translation[0]
     own_incident = incident[0]
-    full_width = own_incident.shape[1] // 2
-    half_width = full_width // 2
-    coeffs = col_sum(product(own_matrix, own_incident)).astype(jnp.bfloat16)
+    chunk_incident = [column_chunk(own_incident, j, CHUNKS) for j in range(CHUNKS)]
+    coeffs = [
+        col_sum(product(own_matrix, chunk_incident[j])).astype(jnp.bfloat16) for j in range(CHUNKS)
+    ]
     for iteration in range(ITERS):
-        partner_coeffs = partner(coeffs, "pair", LEVEL)
-        driven = (
-            own_incident.astype(jnp.float32) + col_sum(product(own_coupling, partner_coeffs))
-        ).astype(jnp.bfloat16)
-        coeffs = col_sum(product(own_matrix, driven)).astype(jnp.bfloat16)
-    incoming = partner(pick_half(coeffs, 1 - column_half, half_width), "pair", LEVEL)
-    own_half = pick_half(coeffs, column_half, half_width)
+        fresh = []
+        for j in range(CHUNKS):
+            partner_coeffs = partner(coeffs[j], "pair", LEVEL)
+            driven = (
+                chunk_incident[j].astype(jnp.float32)
+                + col_sum(product(own_coupling, partner_coeffs))
+            ).astype(jnp.bfloat16)
+            fresh.append(col_sum(product(own_matrix, driven)).astype(jnp.bfloat16))
+        coeffs = fresh
+    received = [partner(coeffs[j], "pair", LEVEL) for j in range(CHUNKS)]
+    per_half = CHUNKS // 2
+
+    def half_of(parts):
+        width = parts[0].shape[1] // 2
+        pieces = [jnp.where(column_half == 0, parts[i], parts[per_half + i]) for i in range(per_half)]
+        real_part = jnp.concatenate([piece[:, :width] for piece in pieces], axis=1)
+        imag_part = jnp.concatenate([piece[:, width:] for piece in pieces], axis=1)
+        return jnp.concatenate([real_part, imag_part], axis=1)
+
+    own_half = half_of(coeffs)
+    incoming = half_of(received)
     total_rows = farfield.shape[1]
     both = jnp.concatenate([own_half, incoming], axis=1)
     both_turned = jnp.concatenate([turned_block(own_half), turned_block(incoming)], axis=1)

time: 285 us -> 365 us (1.28)
  blocking collectives: 185 us -> 15.4 us
  waiting for transfers between devices: 27.3 us -> 134 us
  matrix products: 37 us -> 106 us
  starting transfers between devices: 16.1 us -> 77.9 us
  local copies, waits for them, and re-layouts: 6.27 us -> 17.9 us
    all_to_all x7 -> x1, blocking collectives: 185 us -> 15.4 us  [col_sum(): received = lax.all_to_all(blocks, 'col', 0, 0)]
    all_to_all x1 -> x14, waiting for transfers between devices: 12.8 us -> 128 us  [col_sum(): received = lax.all_to_all(blocks, 'col', 0, 0)]
    all_to_all x1 -> x14, starting transfers between devices: 3.6 us -> 62.9 us  [col_sum(): received = lax.all_to_all(blocks, 'col', 0, 0)]
    dot_general x7 -> x14, matrix products: 15.6 us -> 51.3 us  [product(): jnp.dot(matrix[1], turned_block(vector), preferred_element_type=jnp.float32)]
    dot_general x7 -> x14, matrix products: 18.4 us -> 51.3 us  [product(): jnp.dot(matrix[0], vector, preferred_element_type=jnp.float32)]
    reshape x6 -> x14, local copies, waits for them, and re-layouts: 2.5 us -> 15.2 us  [col_sum(): blocks = partial.astype(jnp.bfloat16).reshape(count, rows // count, width)]
    ppermute x4 -> x8, waiting for transfers between devices: 14.5 us -> 5.93 us  [partner(): return lax.ppermute(value, axis, pairs)]
    ppermute x4 -> x8, starting transfers between devices: 12.5 us -> 15 us  [partner(): return lax.ppermute(value, axis, pairs)]
  transfers between devices with their start and end apart: 5 -> 22, of which waited for: 4 -> 15; matrix products, arithmetic and copies ran while one was open for 3% -> 31% of each run, Pallas kernels for 0% -> 0%
where the time goes in v2:
time: 365 us; the launch traced here: 363 us
  waiting for transfers between devices  134 us (37%)
  matrix products  106 us (29%)
  starting transfers between devices  77.9 us (21%)
  local copies, waits for them, and re-layouts  17.9 us (5%)
  blocking collectives  15.4 us (4%)
  other arithmetic  11.4 us (3%)
    all_to_all x14, waiting for transfers between devices, col_sum(): received = lax.all_to_all(blocks, 'col', 0, 0)  128 us
    all_to_all x14, starting transfers between devices, col_sum(): received = lax.all_to_all(blocks, 'col', 0, 0)  62.9 us
    dot_general x14, matrix products, product(): jnp.dot(matrix[1], turned_block(vector), preferred_element_type=jnp.float32)  51.3 us
    dot_general x14, matrix products, product(): jnp.dot(matrix[0], vector, preferred_element_type=jnp.float32)  51.3 us
    all_to_all x1, blocking collectives, col_sum(): received = lax.all_to_all(blocks, 'col', 0, 0)  15.4 us
    reshape x14, local copies, waits for them, and re-layouts, col_sum(): blocks = partial.astype(jnp.bfloat16).reshape(count, rows // count, width)  15.2 us
    ppermute x8, starting transfers between devices, partner(): return lax.ppermute(value, axis, pairs)  15 us
  transfers between devices with their start and end apart: 22, of which 15 were waited for; matrix products, arithmetic and copies ran while one was open for 31% of the time, Pallas kernels for 0%

profile of v2, /device:TPU:0, one launch (start us, length us, event | category | flops | bytes accessed | tf_op | source)
XLA Modules:
  0.0 362.5 jit_solution(5210748358494895800)
XLA Ops:
  4.8 3.7 %fusion.7 = bf16[128,4096]{1,0:T(8,128)(2,1)S(1)} fusion(f32[128,4096]{1,0:T(8,128)S(1)} %fusion.46, bf16[1,2,4096,512]{3,2,1,0:T(8,128)(2,1)} %param.5, bf16[512,64]{0,1:T(8,128)(2,1)S(1)} %get-tuple-element.14, bf16[512,64]{0,1:T(8,128)(2,1)S(1)} %get-tuple-element.11), kind=kOutput, calls=%fused_computation.21 | convolution fusion | flops 538181632 | bytes 7471104 | tf_op jit(solution)/shard_map/dot_general | solution.py:64
  9.6 8.0 %all-to-all-start.7 = ((bf16[8,512,128]{1,2,0:T(8,128)(2,1)}), bf16[8,512,128]{1,2,0:T(8,128)(2,1)S(1)}, u32[]{:S(2)}, u32[]{:S(2)}) async-start(bf16[8,512,128]{1,2,0:T(8,128)(2,1)} %bitcast.162), calls=%async_computation.7 | async-start | bytes 2097152 | tf_op jit(solution)/shard_map/all_to_all | solution.py:59
  17.6 3.7 %fusion.54 = f32[128,4096]{1,0:T(8,128)S(1)} fusion(bf16[1,2,4096,512]{3,2,1,0:T(8,128)(2,1)} %param.5, bf16[512,64]{0,1:T(8,128)(2,1)S(1)} %get-tuple-element.15, bf16[512,64]{0,1:T(8,128)(2,1)S(1)} %get-tuple-element.16), kind=kOutput, calls=%fused_computation.68 | convolution fusion | flops 537133056 | bytes 6422528 | tf_op jit(solution)/shard_map/dot_general | solution.py:64
  21.3 3.7 %fusion = bf16[128,4096]{1,0:T(8,128)(2,1)S(1)} fusion(f32[128,4096]{1,0:T(8,128)S(1)} %fusion.54, bf16[1,2,4096,512]{3,2,1,0:T(8,128)(2,1)} %param.5, bf16[512,64]{0,1:T(8,128)(2,1)S(1)} %get-tuple-element.16, bf16[512,64]{0,1:T(8,128)(2,1)S(1)} %get-tuple-element.12), kind=kOutput, calls=%fused_computation.14 | convolution fusion | flops 538181632 | bytes 7471104 | tf_op jit(solution)/shard_map/dot_general | solution.py:64
  26.1 7.4 %all-to-all-done.7 = bf16[8,512,128]{1,2,0:T(8,128)(2,1)S(1)} async-done(((bf16[8,512,128]{1,2,0:T(8,128)(2,1)}), bf16[8,512,128]{1,2,0:T(8,128)(2,1)S(1)}, u32[]{:S(2)}, u32[]{:S(2)}) %all-to-all-start.7) | async-done | bytes 1048608 | tf_op jit(solution)/shard_map/all_to_all | solution.py:59
  33.5 4.1 %all-to-all-start = ((bf16[8,512,128]{1,2,0:T(8,128)(2,1)}), bf16[8,512,128]{1,2,0:T(8,128)(2,1)S(1)}, u32[]{:S(2)}, u32[]{:S(2)}) async-start(bf16[8,512,128]{1,2,0:T(8,128)(2,1)} %bitcast.169), calls=%async_computation | async-start | bytes 2097152 | tf_op jit(solution)/shard_map/all_to_all | solution.py:59
  40.8 12.6 %all-to-all-done = bf16[8,512,128]{1,2,0:T(8,128)(2,1)S(1)} async-done(((bf16[8,512,128]{1,2,0:T(8,128)(2,1)}), bf16[8,512,128]{1,2,0:T(8,128)(2,1)S(1)}, u32[]{:S(2)}, u32[]{:S(2)}) %all-to-all-start) | async-done | bytes 1048608 | tf_op jit(solution)/shard_map/all_to_all | solution.py:59
  60.4 3.7 %fusion.8 = bf16[128,4096]{1,0:T(8,128)(2,1)S(1)} fusion(f32[128,4096]{1,0:T(8,128)S(1)} %fusion.18, bf16[512,128]{0,1:T(8,128)(2,1)S(1)} %collective-permute-done.3, bf16[1,2,4096,512]{3,2,1,0:T(8,128)(2,1)} %param.6), kind=kOutput, calls=%fused_computation.22 | convolution fusion | flops 537919488 | bytes 7471104 | tf_op jit(solution)/shard_map/dot_general | solution.py:64
  65.2 4.3 %all-to-all-start.8 = ((bf16[8,512,128]{1,2,0:T(8,128)(2,1)}), bf16[8,512,128]{1,2,0:T(8,128)(2,1)S(1)}, u32[]{:S(2)}, u32[]{:S(2)}) async-start(bf16[8,512,128]{1,2,0:T(8,128)(2,1)} %bitcast.161), calls=%async_computation.8 | async-start | bytes 2097152 | tf_op jit(solution)/shard_map/all_to_all | solution.py:59
  69.5 3.7 %fusion.24 = f32[128,4096]{1,0:T(8,128)S(1)} fusion(bf16[1,2,4096,512]{3,2,1,0:T(8,128)(2,1)} %param.6, bf16[512,64]{0,1:T(8,128)(2,1)S(1)} %get-tuple-element.44, bf16[512,64]{0,1:T(8,128)(2,1)S(1)} %get-tuple-element.43), kind=kOutput, calls=%fused_computation.38 | convolution fusion | flops 537133056 | bytes 6422528 | tf_op jit(solution)/shard_map/dot_general | solution.py:64
  73.1 3.7 %fusion.1 = bf16[128,4096]{1,0:T(8,128)(2,1)S(1)} fusion(f32[128,4096]{1,0:T(8,128)S(1)} %fusion.24, bf16[512,128]{0,1:T(8,128)(2,1)S(1)} %collective-permute-done, bf16[1,2,4096,512]{3,2,1,0:T(8,128)(2,1)} %param.6), kind=kOutput, calls=%fused_computation.15 | convolution fusion | flops 537919488 | bytes 7471104 | tf_op jit(solution)/shard_map/dot_general | solution.py:64
  77.9 7.3 %all-to-all-done.8 = bf16[8,512,128]{1,2,0:T(8,128)(2,1)S(1)} async-done(((bf16[8,512,128]{1,2,0:T(8,128)(2,1)}), bf16[8,512,128]{1,2,0:T(8,128)(2,1)S(1)}, u32[]{:S(2)}, u32[]{:S(2)}) %all-to-all-start.8) | async-done | bytes 1048608 | tf_op jit(solution)/shard_map/all_to_all | solution.py:59
  85.2 4.1 %all-to-all-start.1 = ((bf16[8,512,128]{1,2,0:T(8,128)(2,1)}), bf16[8,512,128]{1,2,0:T(8,128)(2,1)S(1)}, u32[]{:S(2)}, u32[]{:S(2)}) async-start(bf16[8,512,128]{1,2,0:T(8,128)(2,1)} %bitcast.168), calls=%async_computation.1 | async-start | bytes 2097152 | tf_op jit(solution)/shard_map/all_to_all | solution.py:59
  89.4 15.7 %all-to-all-done.1 = bf16[8,512,128]{1,2,0:T(8,128)(2,1)S(1)} async-done(((bf16[8,512,128]{1,2,0:T(8,128)(2,1)}), bf16[8,512,128]{1,2,0:T(8,128)(2,1)S(1)}, u32[]{:S(2)}, u32[]{:S(2)}) %all-to-all-start.1) | async-done | bytes 1048608 | tf_op jit(solution)/shard_map/all_to_all | solution.py:59
  109.0 3.7 %fusion.9 = bf16[128,4096]{1,0:T(8,128)(2,1)S(1)} fusion(f32[128,4096]{1,0:T(8,128)S(1)} %fusion.44, bf16[1,2,4096,512]{3,2,1,0:T(8,128)(2,1)} %param.5, bf16[512,64]{0,1:T(8,128)(2,1)S(1)} %get-tuple-element.30, bf16[512,64]{0,1:T(8,128)(2,1)S(1)} %get-tuple-element.29), kind=kOutput, calls=%fused_computation.23 | convolution fusion | flops 538181632 | bytes 7471104 | tf_op jit(solution)/shard_map/dot_general | solution.py:64
  113.8 4.3 %all-to-all-start.9 = ((bf16[8,512,128]{1,2,0:T(8,128)(2,1)}), bf16[8,512,128]{1,2,0:T(8,128)(2,1)S(1)}, u32[]{:S(2)}, u32[]{:S(2)}) async-start(bf16[8,512,128]{1,2,0:T(8,128)(2,1)} %bitcast.160), calls=%async_computation.9 | async-start | bytes 2097152 | tf_op jit(solution)/shard_map/all_to_all | solution.py:59
  118.1 3.7 %fusion.52 = f32[128,4096]{1,0:T(8,128)S(1)} fusion(bf16[512,128]{0,1:T(8,128)(2,1)S(1)} %get-tuple-element.56, bf16[1,2,4096,512]{3,2,1,0:T(8,128)(2,1)} %param.5), kind=kOutput, calls=%fused_computation.66 | convolution fusion | flops 536870912 | bytes 6422528 | tf_op jit(solution)/shard_map/dot_general | solution.py:64
  121.8 3.7 %fusion.2 = bf16[128,4096]{1,0:T(8,128)(2,1)S(1)} fusion(f32[128,4096]{1,0:T(8,128)S(1)} %fusion.52, bf16[1,2,4096,512]{3,2,1,0:T(8,128)(2,1)} %param.5, bf16[512,64]{0,1:T(8,128)(2,1)S(1)} %get-tuple-element.42, bf16[512,64]{0,1:T(8,128)(2,1)S(1)} %get-tuple-element.41), kind=kOutput, calls=%fused_computation.16 | convolution fusion | flops 538181632 | bytes 7471104 | tf_op jit(solution)/shard_map/dot_general | solution.py:64
  126.5 7.4 %all-to-all-done.9 = bf16[8,512,128]{1,2,0:T(8,128)(2,1)S(1)} async-done(((bf16[8,512,128]{1,2,0:T(8,128)(2,1)}), bf16[8,512,128]{1,2,0:T(8,128)(2,1)S(1)}, u32[]{:S(2)}, u32[]{:S(2)}) %all-to-all-start.9) | async-done | bytes 1048608 | tf_op jit(solution)/shard_map/all_to_all | solution.py:59
  133.9 4.3 %all-to-all-start.2 = ((bf16[8,512,128]{1,2,0:T(8,128)(2,1)}), bf16[8,512,128]{1,2,0:T(8,128)(2,1)S(1)}, u32[]{:S(2)}, u32[]{:S(2)}) async-start(bf16[8,512,128]{1,2,0:T(8,128)(2,1)} %bitcast.167), calls=%async_computation.2 | async-start | bytes 2097152 | tf_op jit(solution)/shard_map/all_to_all | solution.py:59
  139.0 15.1 %all-to-all-done.2 = bf16[8,512,128]{1,2,0:T(8,128)(2,1)S(1)} async-done(((bf16[8,512,128]{1,2,0:T(8,128)(2,1)}), bf16[8,512,128]{1,2,0:T(8,128)(2,1)S(1)}, u32[]{:S(2)}, u32[]{:S(2)}) %all-to-all-start.2) | async-done | bytes 1048608 | tf_op jit(solution)/shard_map/all_to_all | solution.py:59
  158.5 3.7 %fusion.10 = bf16[128,4096]{1,0:T(8,128)(2,1)S(1)} fusion(f32[128,4096]{1,0:T(8,128)S(1)} %fusion.16, bf16[512,128]{0,1:T(8,128)(2,1)S(1)} %collective-permute-done.4, bf16[1,2,4096,512]{3,2,1,0:T(8,128)(2,1)} %param.6), kind=kOutput, calls=%fused_computation.24 | convolution fusion | flops 537919488 | bytes 7471104 | tf_op jit(solution)/shard_map/dot_general | solution.py:64
  163.3 4.3 %all-to-all-start.10 = ((bf16[8,512,128]{1,2,0:T(8,128)(2,1)}), bf16[8,512,128]{1,2,0:T(8,128)(2,1)S(1)}, u32[]{:S(2)}, u32[]{:S(2)}) async-start(bf16[8,512,128]{1,2,0:T(8,128)(2,1)} %bitcast.159), calls=%async_computation.10 | async-start | bytes 2097152 | tf_op jit(solution)/shard_map/all_to_all | solution.py:59
  167.6 3.7 %fusion.22 = f32[128,4096]{1,0:T(8,128)S(1)} fusion(bf16[1,2,4096,512]{3,2,1,0:T(8,128)(2,1)} %param.6, bf16[512,64]{0,1:T(8,128)(2,1)S(1)} %get-tuple-element.40, bf16[512,64]{0,1:T(8,128)(2,1)S(1)} %get-tuple-element.39), kind=kOutput, calls=%fused_computation.36 | convolution fusion | flops 537133056 | bytes 6422528 | tf_op jit(solution)/shard_map/dot_general | solution.py:64
  171.2 3.7 %fusion.3 = bf16[128,4096]{1,0:T(8,128)(2,1)S(1)} fusion(f32[128,4096]{1,0:T(8,128)S(1)} %fusion.22, bf16[512,128]{0,1:T(8,128)(2,1)S(1)} %collective-permute-done.1, bf16[1,2,4096,512]{3,2,1,0:T(8,128)(2,1)} %param.6), kind=kOutput, calls=%fused_computation.17 | convolution fusion | flops 537919488 | bytes 7471104 | tf_op jit(solution)/shard_map/dot_general | solution.py:64
  176.0 7.3 %all-to-all-done.10 = bf16[8,512,128]{1,2,0:T(8,128)(2,1)S(1)} async-done(((bf16[8,512,128]{1,2,0:T(8,128)(2,1)}), bf16[8,512,128]{1,2,0:T(8,128)(2,1)S(1)}, u32[]{:S(2)}, u32[]{:S(2)}) %all-to-all-start.10) | async-done | bytes 1048608 | tf_op jit(solution)/shard_map/all_to_all | solution.py:59
  183.3 4.1 %all-to-all-start.3 = ((bf16[8,512,128]{1,2,0:T(8,128)(2,1)}), bf16[8,512,128]{1,2,0:T(8,128)(2,1)S(1)}, u32[]{:S(2)}, u32[]{:S(2)}) async-start(bf16[8,512,128]{1,2,0:T(8,128)(2,1)} %bitcast.166), calls=%async_computation.3 | async-start | bytes 2097152 | tf_op jit(solution)/shard_map/all_to_all | solution.py:59
  191.2 3.7 %fusion.11 = bf16[128,4096]{1,0:T(8,128)(2,1)S(1)} fusion(f32[128,4096]{1,0:T(8,128)S(1)} %fusion.42, bf16[1,2,4096,512]{3,2,1,0:T(8,128)(2,1)} %param.5, bf16[512,64]{0,1:T(8,128)(2,1)S(1)} %get-tuple-element.26, bf16[512,64]{0,1:T(8,128)(2,1)S(1)} %get-tuple-element.25), kind=kOutput, calls=%fused_computation.25 | convolution fusion | flops 538181632 | bytes 7471104 | tf_op jit(solution)/shard_map/dot_general | solution.py:64
  196.0 7.2 %all-to-all-done.3 = bf16[8,512,128]{1,2,0:T(8,128)(2,1)S(1)} async-done(((bf16[8,512,128]{1,2,0:T(8,128)(2,1)}), bf16[8,512,128]{1,2,0:T(8,128)(2,1)S(1)}, u32[]{:S(2)}, u32[]{:S(2)}) %all-to-all-start.3) | async-done | bytes 1048608 | tf_op jit(solution)/shard_map/all_to_all | solution.py:59
  203.2 4.3 %all-to-all-start.11 = ((bf16[8,512,128]{1,2,0:T(8,128)(2,1)}), bf16[8,512,128]{1,2,0:T(8,128)(2,1)S(1)}, u32[]{:S(2)}, u32[]{:S(2)}) async-start(bf16[8,512,128]{1,2,0:T(8,128)(2,1)} %bitcast.158), calls=%async_computation.11 | async-start | bytes 2097152 | tf_op jit(solution)/shard_map/all_to_all | solution.py:59
  211.4 3.7 %fusion.4 = bf16[128,4096]{1,0:T(8,128)(2,1)S(1)} fusion(f32[128,4096]{1,0:T(8,128)S(1)} %fusion.50, bf16[1,2,4096,512]{3,2,1,0:T(8,128)(2,1)} %param.5, bf16[512,64]{0,1:T(8,128)(2,1)S(1)} %get-tuple-element.38, bf16[512,64]{0,1:T(8,128)(2,1)S(1)} %get-tuple-element.37), kind=kOutput, calls=%fused_computation.18 | convolution fusion | flops 538181632 | bytes 7471104 | tf_op jit(solution)/shard_map/dot_general | solution.py:64
  216.1 7.2 %all-to-all-done.11 = bf16[8,512,128]{1,2,0:T(8,128)(2,1)S(1)} async-done(((bf16[8,512,128]{1,2,0:T(8,128)(2,1)}), bf16[8,512,128]{1,2,0:T(8,128)(2,1)S(1)}, u32[]{:S(2)}, u32[]{:S(2)}) %all-to-all-start.11) | async-done | bytes 1048608 | tf_op jit(solution)/shard_map/all_to_all | solution.py:59
  223.4 4.3 %all-to-all-start.4 = ((bf16[8,512,128]{1,2,0:T(8,128)(2,1)}), bf16[8,512,128]{1,2,0:T(8,128)(2,1)S(1)}, u32[]{:S(2)}, u32[]{:S(2)}) async-start(bf16[8,512,128]{1,2,0:T(8,128)(2,1)} %bitcast.165), calls=%async_computation.4 | async-start | bytes 2097152 | tf_op jit(solution)/shard_map/all_to_all | solution.py:59
  230.9 12.6 %all-to-all-done.4 = bf16[8,512,128]{1,2,0:T(8,128)(2,1)S(1)} async-done(((bf16[8,512,128]{1,2,0:T(8,128)(2,1)}), bf16[8,512,128]{1,2,0:T(8,128)(2,1)S(1)}, u32[]{:S(2)}, u32[]{:S(2)}) %all-to-all-start.4) | async-done | bytes 1048608 | tf_op jit(solution)/shard_map/all_to_all | solution.py:59
  250.6 3.7 %fusion.12 = bf16[128,4096]{1,0:T(8,128)(2,1)S(1)} fusion(f32[128,4096]{1,0:T(8,128)S(1)} %fusion.14, bf16[512,128]{0,1:T(8,128)(2,1)S(1)} %collective-permute-done.5, bf16[1,2,4096,512]{3,2,1,0:T(8,128)(2,1)} %param.6), kind=kOutput, calls=%fused_computation.26 | convolution fusion | flops 537919488 | bytes 7471104 | tf_op jit(solution)/shard_map/dot_general | solution.py:64
  255.4 4.3 %all-to-all-start.12 = ((bf16[8,512,128]{1,2,0:T(8,128)(2,1)}), bf16[8,512,128]{1,2,0:T(8,128)(2,1)S(1)}, u32[]{:S(2)}, u32[]{:S(2)}) async-start(bf16[8,512,128]{1,2,0:T(8,128)(2,1)} %bitcast.157), calls=%async_computation.12 | async-start | bytes 2097152 | tf_op jit(solution)/shard_map/all_to_all | solution.py:59
  263.4 3.7 %fusion.5 = bf16[128,4096]{1,0:T(8,128)(2,1)S(1)} fusion(f32[128,4096]{1,0:T(8,128)S(1)} %fusion.20, bf16[512,128]{0,1:T(8,128)(2,1)S(1)} %collective-permute-done.2, bf16[1,2,4096,512]{3,2,1,0:T(8,128)(2,1)} %param.6), kind=kOutput, calls=%fused_computation.19 | convolution fusion | flops 537919488 | bytes 7471104 | tf_op jit(solution)/shard_map/dot_general | solution.py:64
  268.2 7.3 %all-to-all-done.12 = bf16[8,512,128]{1,2,0:T(8,128)(2,1)S(1)} async-done(((bf16[8,512,128]{1,2,0:T(8,128)(2,1)}), bf16[8,512,128]{1,2,0:T(8,128)(2,1)S(1)}, u32[]{:S(2)}, u32[]{:S(2)}) %all-to-all-start.12) | async-done | bytes 1048608 | tf_op jit(solution)/shard_map/all_to_all | solution.py:59
  275.4 4.1 %all-to-all-start.5 = ((bf16[8,512,128]{1,2,0:T(8,128)(2,1)}), bf16[8,512,128]{1,2,0:T(8,128)(2,1)S(1)}, u32[]{:S(2)}, u32[]{:S(2)}) async-start(bf16[8,512,128]{1,2,0:T(8,128)(2,1)} %bitcast.164), calls=%async_computation.5 | async-start | bytes 2097152 | tf_op jit(solution)/shard_map/all_to_all | solution.py:59
  283.4 3.7 %fusion.13 = bf16[128,4096]{1,0:T(8,128)(2,1)S(1)} fusion(f32[128,4096]{1,0:T(8,128)S(1)} %fusion.40, bf16[1,2,4096,512]{3,2,1,0:T(8,128)(2,1)} %param.5, bf16[512,64]{0,1:T(8,128)(2,1)S(1)} %get-tuple-element.22, bf16[512,64]{0,1:T(8,128)(2,1)S(1)} %get-tuple-element.21), kind=kOutput, calls=%fused_computation.27 | convolution fusion | flops 538181632 | bytes 7471104 | tf_op jit(solution)/shard_map/dot_general | solution.py:64
  288.2 7.2 %all-to-all-done.5 = bf16[8,512,128]{1,2,0:T(8,128)(2,1)S(1)} async-done(((bf16[8,512,128]{1,2,0:T(8,128)(2,1)}), bf16[8,512,128]{1,2,0:T(8,128)(2,1)S(1)}, u32[]{:S(2)}, u32[]{:S(2)}) %all-to-all-start.5) | async-done | bytes 1048608 | tf_op jit(solution)/shard_map/all_to_all | solution.py:59
  295.4 4.3 %all-to-all-start.13 = ((bf16[8,512,128]{1,2,0:T(8,128)(2,1)}), bf16[8,512,128]{1,2,0:T(8,128)(2,1)S(1)}, u32[]{:S(2)}, u32[]{:S(2)}) async-start(bf16[8,512,128]{1,2,0:T(8,128)(2,1)} %bitcast.156), calls=%async_computation.13 | async-start | bytes 2097152 | tf_op jit(solution)/shard_map/all_to_all | solution.py:59
  303.5 3.7 %fusion.6 = bf16[128,4096]{1,0:T(8,128)(2,1)S(1)} fusion(f32[128,4096]{1,0:T(8,128)S(1)} %fusion.48, bf16[1,2,4096,512]{3,2,1,0:T(8,128)(2,1)} %param.5, bf16[512,64]{0,1:T(8,128)(2,1)S(1)} %get-tuple-element.34, bf16[512,64]{0,1:T(8,128)(2,1)S(1)} %get-tuple-element.33), kind=kOutput, calls=%fused_computation.20 | convolution fusion | flops 538181632 | bytes 7471104 | tf_op jit(solution)/shard_map/dot_general | solution.py:64
  308.3 7.2 %all-to-all-done.13 = bf16[8,512,128]{1,2,0:T(8,128)(2,1)S(1)} async-done(((bf16[8,512,128]{1,2,0:T(8,128)(2,1)}), bf16[8,512,128]{1,2,0:T(8,128)(2,1)S(1)}, u32[]{:S(2)}, u32[]{:S(2)}) %all-to-all-start.13) | async-done | bytes 1048608 | tf_op jit(solution)/shard_map/all_to_all | solution.py:59
  315.5 4.3 %all-to-all-start.6 = ((bf16[8,512,128]{1,2,0:T(8,128)(2,1)}), bf16[8,512,128]{1,2,0:T(8,128)(2,1)S(1)}, u32[]{:S(2)}, u32[]{:S(2)}) async-start(bf16[8,512,128]{1,2,0:T(8,128)(2,1)} %bitcast.163), calls=%async_computation.6 | async-start | bytes 2097152 | tf_op jit(solution)/shard_map/all_to_all | solution.py:59
  329.4 6.2 %all-to-all-done.6 = bf16[8,512,128]{1,2,0:T(8,128)(2,1)S(1)} async-done(((bf16[8,512,128]{1,2,0:T(8,128)(2,1)}), bf16[8,512,128]{1,2,0:T(8,128)(2,1)S(1)}, u32[]{:S(2)}, u32[]{:S(2)}) %all-to-all-start.6) | async-done | bytes 1048608 | tf_op jit(solution)/shard_map/all_to_all | solution.py:59
  336.4 5.9 %collective-permute-done.6 = bf16[512,128]{0,1:T(8,128)(2,1)S(1)} collective-permute-done((bf16[512,128]{0,1:T(8,128)(2,1)S(1)}, bf16[512,128]{0,1:T(8,128)(2,1)S(1)}, u32[]{:S(2)}, u32[]{:S(2)}) %collective-permute-start.6) | collective-permute-done | bytes 131104 | tf_op jit(solution)/shard_map/ppermute | solution.py:15
  346.3 15.4 %all_to_all.75 = bf16[8,256,128]{1,2,0:T(8,128)(2,1)S(1)} all-to-all(bf16[8,256,128]{1,2,0:T(8,128)(2,1)S(1)} %fusion.74), channel_id=1, replica_groups=mesh['pair'=16,'col'=8] {'col'}, dimensions={0} | all-to-all | bytes 1048576 | tf_op jit(solution)/shard_map/all_to_all | solution.py:59
  (96 shorter events, 83.9 us)
Async XLA Ops:
  9.6 23.9 %all-to-all-start.7 = ((bf16[8,512,128]{1,2,0:T(8,128)(2,1)}), bf16[8,512,128]{1,2,0:T(8,128)(2,1)S(1)}, u32[]{:S(2)}, u32[]{:S(2)}) async-start(bf16[8,512,128]{1,2,0:T(8,128)(2,1)} %bitcast.162), calls=%async_computation.7 | async-start | bytes 2097152 | tf_op jit(solution)/shard_map/all_to_all | solution.py:59
  33.5 19.9 %all-to-all-start = ((bf16[8,512,128]{1,2,0:T(8,128)(2,1)}), bf16[8,512,128]{1,2,0:T(8,128)(2,1)S(1)}, u32[]{:S(2)}, u32[]{:S(2)}) async-start(bf16[8,512,128]{1,2,0:T(8,128)(2,1)} %bitcast.169), calls=%async_computation | async-start | bytes 2097152 | tf_op jit(solution)/shard_map/all_to_all | solution.py:59
  37.7 19.0 %collective-permute-start.3 = (bf16[512,128]{0,1:T(8,128)(2,1)S(1)}, bf16[512,128]{0,1:T(8,128)(2,1)S(1)}, u32[]{:S(2)}, u32[]{:S(2)}) collective-permute-start(bf16[512,128]{0,1:T(8,128)(2,1)S(1)} %reduce_sum.166), channel_id=1, source_target_pairs={{0,32},{8,40},{16,48},{24,56},{32,0},{40,8},{48,16},{56,24},{64,96... | collective-permute-start | bytes 393224 | tf_op jit(solution)/shard_map/ppermute | solution.py:15
  53.6 15.9 %collective-permute-start = (bf16[512,128]{0,1:T(8,128)(2,1)S(1)}, bf16[512,128]{0,1:T(8,128)(2,1)S(1)}, u32[]{:S(2)}, u32[]{:S(2)}) collective-permute-start(bf16[512,128]{0,1:T(8,128)(2,1)S(1)} %reduce_sum.159), channel_id=1, source_target_pairs={{0,32},{8,40},{16,48},{24,56},{32,0},{40,8},{48,16},{56,24},{64,96... | collective-permute-start | bytes 393224 | tf_op jit(solution)/shard_map/ppermute | solution.py:15
  65.2 20.0 %all-to-all-start.8 = ((bf16[8,512,128]{1,2,0:T(8,128)(2,1)}), bf16[8,512,128]{1,2,0:T(8,128)(2,1)S(1)}, u32[]{:S(2)}, u32[]{:S(2)}) async-start(bf16[8,512,128]{1,2,0:T(8,128)(2,1)} %bitcast.161), calls=%async_computation.8 | async-start | bytes 2097152 | tf_op jit(solution)/shard_map/all_to_all | solution.py:59
  85.2 19.9 %all-to-all-start.1 = ((bf16[8,512,128]{1,2,0:T(8,128)(2,1)}), bf16[8,512,128]{1,2,0:T(8,128)(2,1)S(1)}, u32[]{:S(2)}, u32[]{:S(2)}) async-start(bf16[8,512,128]{1,2,0:T(8,128)(2,1)} %bitcast.168), calls=%async_computation.1 | async-start | bytes 2097152 | tf_op jit(solution)/shard_map/all_to_all | solution.py:59
  113.8 20.1 %all-to-all-start.9 = ((bf16[8,512,128]{1,2,0:T(8,128)(2,1)}), bf16[8,512,128]{1,2,0:T(8,128)(2,1)S(1)}, u32[]{:S(2)}, u32[]{:S(2)}) async-start(bf16[8,512,128]{1,2,0:T(8,128)(2,1)} %bitcast.160), calls=%async_computation.9 | async-start | bytes 2097152 | tf_op jit(solution)/shard_map/all_to_all | solution.py:59
  133.9 20.1 %all-to-all-start.2 = ((bf16[8,512,128]{1,2,0:T(8,128)(2,1)}), bf16[8,512,128]{1,2,0:T(8,128)(2,1)S(1)}, u32[]{:S(2)}, u32[]{:S(2)}) async-start(bf16[8,512,128]{1,2,0:T(8,128)(2,1)} %bitcast.167), calls=%async_computation.2 | async-start | bytes 2097152 | tf_op jit(solution)/shard_map/all_to_all | solution.py:59
  138.4 16.4 %collective-permute-start.4 = (bf16[512,128]{0,1:T(8,128)(2,1)S(1)}, bf16[512,128]{0,1:T(8,128)(2,1)S(1)}, u32[]{:S(2)}, u32[]{:S(2)}) collective-permute-start(bf16[512,128]{0,1:T(8,128)(2,1)S(1)} %reduce_sum.168), channel_id=1, source_target_pairs={{0,32},{8,40},{16,48},{24,56},{32,0},{40,8},{48,16},{56,24},{64,96... | collective-permute-start | bytes 393224 | tf_op jit(solution)/shard_map/ppermute | solution.py:15
  154.2 13.3 %collective-permute-start.1 = (bf16[512,128]{0,1:T(8,128)(2,1)S(1)}, bf16[512,128]{0,1:T(8,128)(2,1)S(1)}, u32[]{:S(2)}, u32[]{:S(2)}) collective-permute-start(bf16[512,128]{0,1:T(8,128)(2,1)S(1)} %reduce_sum.161), channel_id=1, source_target_pairs={{0,32},{8,40},{16,48},{24,56},{32,0},{40,8},{48,16},{56,24},{64,96... | collective-permute-start | bytes 393224 | tf_op jit(solution)/shard_map/ppermute | solution.py:15
  163.3 20.0 %all-to-all-start.10 = ((bf16[8,512,128]{1,2,0:T(8,128)(2,1)}), bf16[8,512,128]{1,2,0:T(8,128)(2,1)S(1)}, u32[]{:S(2)}, u32[]{:S(2)}) async-start(bf16[8,512,128]{1,2,0:T(8,128)(2,1)} %bitcast.159), calls=%async_computation.10 | async-start | bytes 2097152 | tf_op jit(solution)/shard_map/all_to_all | solution.py:59
  183.3 19.9 %all-to-all-start.3 = ((bf16[8,512,128]{1,2,0:T(8,128)(2,1)}), bf16[8,512,128]{1,2,0:T(8,128)(2,1)S(1)}, u32[]{:S(2)}, u32[]{:S(2)}) async-start(bf16[8,512,128]{1,2,0:T(8,128)(2,1)} %bitcast.166), calls=%async_computation.3 | async-start | bytes 2097152 | tf_op jit(solution)/shard_map/all_to_all | solution.py:59
  203.2 20.1 %all-to-all-start.11 = ((bf16[8,512,128]{1,2,0:T(8,128)(2,1)}), bf16[8,512,128]{1,2,0:T(8,128)(2,1)S(1)}, u32[]{:S(2)}, u32[]{:S(2)}) async-start(bf16[8,512,128]{1,2,0:T(8,128)(2,1)} %bitcast.158), calls=%async_computation.11 | async-start | bytes 2097152 | tf_op jit(solution)/shard_map/all_to_all | solution.py:59
  223.4 20.1 %all-to-all-start.4 = ((bf16[8,512,128]{1,2,0:T(8,128)(2,1)}), bf16[8,512,128]{1,2,0:T(8,128)(2,1)S(1)}, u32[]{:S(2)}, u32[]{:S(2)}) async-start(bf16[8,512,128]{1,2,0:T(8,128)(2,1)} %bitcast.165), calls=%async_computation.4 | async-start | bytes 2097152 | tf_op jit(solution)/shard_map/all_to_all | solution.py:59
  227.8 19.2 %collective-permute-start.5 = (bf16[512,128]{0,1:T(8,128)(2,1)S(1)}, bf16[512,128]{0,1:T(8,128)(2,1)S(1)}, u32[]{:S(2)}, u32[]{:S(2)}) collective-permute-start(bf16[512,128]{0,1:T(8,128)(2,1)S(1)} %reduce_sum.170), channel_id=1, source_target_pairs={{0,32},{8,40},{16,48},{24,56},{32,0},{40,8},{48,16},{56,24},{64,96... | collective-permute-start | bytes 393224 | tf_op jit(solution)/shard_map/ppermute | solution.py:15
  243.6 16.1 %collective-permute-start.2 = (bf16[512,128]{0,1:T(8,128)(2,1)S(1)}, bf16[512,128]{0,1:T(8,128)(2,1)S(1)}, u32[]{:S(2)}, u32[]{:S(2)}) collective-permute-start(bf16[512,128]{0,1:T(8,128)(2,1)S(1)} %reduce_sum.163), channel_id=1, source_target_pairs={{0,32},{8,40},{16,48},{24,56},{32,0},{40,8},{48,16},{56,24},{64,96... | collective-permute-start | bytes 393224 | tf_op jit(solution)/shard_map/ppermute | solution.py:15
  255.4 20.0 %all-to-all-start.12 = ((bf16[8,512,128]{1,2,0:T(8,128)(2,1)}), bf16[8,512,128]{1,2,0:T(8,128)(2,1)S(1)}, u32[]{:S(2)}, u32[]{:S(2)}) async-start(bf16[8,512,128]{1,2,0:T(8,128)(2,1)} %bitcast.157), calls=%async_computation.12 | async-start | bytes 2097152 | tf_op jit(solution)/shard_map/all_to_all | solution.py:59
  275.4 19.9 %all-to-all-start.5 = ((bf16[8,512,128]{1,2,0:T(8,128)(2,1)}), bf16[8,512,128]{1,2,0:T(8,128)(2,1)S(1)}, u32[]{:S(2)}, u32[]{:S(2)}) async-start(bf16[8,512,128]{1,2,0:T(8,128)(2,1)} %bitcast.164), calls=%async_computation.5 | async-start | bytes 2097152 | tf_op jit(solution)/shard_map/all_to_all | solution.py:59
  295.4 20.1 %all-to-all-start.13 = ((bf16[8,512,128]{1,2,0:T(8,128)(2,1)}), bf16[8,512,128]{1,2,0:T(8,128)(2,1)S(1)}, u32[]{:S(2)}, u32[]{:S(2)}) async-start(bf16[8,512,128]{1,2,0:T(8,128)(2,1)} %bitcast.156), calls=%async_computation.13 | async-start | bytes 2097152 | tf_op jit(solution)/shard_map/all_to_all | solution.py:59
  303.5 16.3 %copy-start.1 = (s32[16,3]{0,1:T(4,128)S(1)}, s32[16,3]{0,1:T(4,128)}, u32[]{:S(2)}) copy-start(s32[16,3]{0,1:T(4,128)} %param.9) | copy-start | bytes 580
  315.5 20.1 %all-to-all-start.6 = ((bf16[8,512,128]{1,2,0:T(8,128)(2,1)}), bf16[8,512,128]{1,2,0:T(8,128)(2,1)S(1)}, u32[]{:S(2)}, u32[]{:S(2)}) async-start(bf16[8,512,128]{1,2,0:T(8,128)(2,1)} %bitcast.163), calls=%async_computation.6 | async-start | bytes 2097152 | tf_op jit(solution)/shard_map/all_to_all | solution.py:59
  328.8 7.6 %collective-permute-start.7 = (bf16[512,128]{0,1:T(8,128)(2,1)S(1)}, bf16[512,128]{0,1:T(8,128)(2,1)S(1)}, u32[]{:S(2)}, u32[]{:S(2)}) collective-permute-start(bf16[512,128]{0,1:T(8,128)(2,1)S(1)} %reduce_sum.172), channel_id=1, source_target_pairs={{0,32},{8,40},{16,48},{24,56},{32,0},{40,8},{48,16},{56,24},{64,96... | collective-permute-start | bytes 393224 | tf_op jit(solution)/shard_map/ppermute | solution.py:15
  335.8 9.0 %copy-start = (bf16[2,2048,512]{2,1,0:T(8,128)(2,1)S(1)}, bf16[2,2048,512]{2,1,0:T(8,128)(2,1)}, u32[]{:S(2)}) copy-start(bf16[2,2048,512]{2,1,0:T(8,128)(2,1)} %param.8) | copy-start | bytes 12582916
  335.8 6.6 %collective-permute-start.6 = (bf16[512,128]{0,1:T(8,128)(2,1)S(1)}, bf16[512,128]{0,1:T(8,128)(2,1)S(1)}, u32[]{:S(2)}, u32[]{:S(2)}) collective-permute-start(bf16[512,128]{0,1:T(8,128)(2,1)S(1)} %reduce_sum.165), channel_id=1, source_target_pairs={{0,32},{8,40},{16,48},{24,56},{32,0},{40,8},{48,16},{56,24},{64,96... | collective-permute-start | bytes 393224 | tf_op jit(solution)/shard_map/ppermute | solution.py:15

commit v3 on v1

--- a/solution.py
+++ b/solution.py
@@ -3,6 +3,7 @@
 import jax
 import jax.numpy as jnp
 from jax import lax
+from jax.experimental import pallas as pl
 from jax.sharding import PartitionSpec as P
 
 ITERS = 3
@@ -60,10 +61,31 @@
     return jnp.sum(received.astype(jnp.float32), axis=0)
 
 
-def product(matrix, vector):
-    return jnp.dot(matrix[0], vector, preferred_element_type=jnp.float32) + jnp.dot(
-        matrix[1], turned_block(vector), preferred_element_type=jnp.float32
-    )
+def product_body(matrix_ref, vector_ref, turned_ref, out_ref):
+    total = jnp.dot(matrix_ref[0, 0], vector_ref[...], preferred_element_type=jnp.float32)
+    total = total + jnp.dot(matrix_ref[0, 1], turned_ref[...], preferred_element_type=jnp.float32)
+    out_ref[...] = total.astype(out_ref.dtype)
+
+
+def product(matrices, vector, block_rows=1024):
+    _, _, rows, cols = matrices.shape
+    width = vector.shape[1]
+    return pl.pallas_call(
+        product_body,
+        grid=(rows // block_rows,),
+        in_specs=[
+            pl.BlockSpec((1, 2, block_rows, cols), lambda i: (0, 0, i, 0)),
+            pl.BlockSpec((cols, width), lambda i: (0, 0)),
+            pl.BlockSpec((cols, width), lambda i: (0, 0)),
+        ],
+        out_specs=pl.BlockSpec((block_rows, width), lambda i: (i, 0)),
+        out_shape=jax.ShapeDtypeStruct((rows, width), jnp.bfloat16),
+        cost_estimate=pl.CostEstimate(
+            flops=4 * rows * cols * width,
+            transcendentals=0,
+            bytes_accessed=2 * (2 * rows * cols + 2 * cols * width + rows * width),
+        ),
+    )(matrices, vector, turned_block(vector))
 
 
 def on_device(tmatrix, translation, incident, farfield, centres):
@@ -73,8 +95,8 @@
     other_centre = lax.dynamic_index_in_dim(
         centres, jnp.bitwise_xor(pair_index, 2**LEVEL), 0, keepdims=False
     )
-    own_matrix = tmatrix[0]
-    own_coupling = translation[0]
+    own_matrix = tmatrix
+    own_coupling = translation
     own_incident = incident[0]
     full_width = own_incident.shape[1] // 2
     half_width = full_width // 2

time: 285 us -> 296 us (1.039)
  Pallas kernels: 0 us -> 46.1 us
  matrix products: 37 us -> 3.58 us
  other arithmetic: 11.7 us -> 18.4 us
  local copies, waits for them, and re-layouts: 6.27 us -> 2.35 us
  blocking collectives: 185 us -> 182 us
    pallas_call x0 -> x7, Pallas kernels: none -> 46.1 us  [product(): pl.pallas_call(product_body, grid=(rows // block_rows,), in_specs=[pl.Blo...]
    dot_general x14 -> x0, matrix products: 34 us -> none  [the longest x7 18.4 us: product(): jnp.dot(matrix[0], vector, preferred_element_type=jnp.float32)]
    concatenate x0 -> x7, other arithmetic: none -> 5.27 us  [turned_block(): jnp.concatenate([-vector[:, half_width:], vector[:, :half_width]], axis=1)]
    all_to_all x7, blocking collectives: 185 us -> 182 us  [col_sum(): received = lax.all_to_all(blocks, 'col', 0, 0)]
where the time goes in v3:
time: 296 us; the launch traced here: 295 us
  blocking collectives  182 us (61%)
  Pallas kernels  46.1 us (16%)
  waiting for transfers between devices  26.1 us (9%)
  other arithmetic  18.4 us (6%)
  starting transfers between devices  16.3 us (6%)
  matrix products  3.58 us (1%)
    all_to_all x7, blocking collectives, col_sum(): received = lax.all_to_all(blocks, 'col', 0, 0)  182 us
    pallas_call x7, Pallas kernels, product(): pl.pallas_call(product_body, grid=(rows // block_rows,), in_specs=[pl.Blo...  46.1 us
    ppermute x4, waiting for transfers between devices, partner(): return lax.ppermute(value, axis, pairs)  14.6 us
    ppermute x4, starting transfers between devices, partner(): return lax.ppermute(value, axis, pairs)  12.5 us
    all_to_all x1, waiting for transfers between devices, col_sum(): received = lax.all_to_all(blocks, 'col', 0, 0)  11.5 us
  transfers between devices with their start and end apart: 5, of which 4 were waited for; matrix products, arithmetic and copies ran while one was open for 3% of the time, Pallas kernels for 0%

profile of v3, /device:TPU:0, one launch (start us, length us, event | category | flops | bytes accessed | tf_op | source)
XLA Modules:
  0.0 295.1 jit_solution(15555797423386145221)
XLA Ops:
  0.0 1.0 slice_negate_fusion.7
  1.0 0.8 pad_maximum_fusion.turned_ref
  1.7 6.6 %shard_map.55 = bf16[4096,256]{1,0:T(8,128)(2,1)} custom-call(bf16[1,2,4096,512]{3,2,1,0:T(8,128)(2,1)} %matrix_ref.13, bf16[512,256]{1,0:T(8,128)(2,1)} %bitcast.50, bf16[512,256]{1,0:T(8,128)(2,1)} %pad_maximum_fusion.turned_ref), custom_call_target="tpu_custom_call" | custom-call | flops 2147483648 | bytes 11010048 | tf_op jit(solution)/shard_map/pallas_call | solution.py:73
  8.3 36.4 %all_to_all.40 = bf16[8,512,256]{2,1,0:T(8,128)(2,1)S(1)} all-to-all(bf16[8,512,256]{2,1,0:T(8,128)(2,1)} %bitcast.48), channel_id=1, replica_groups=mesh['pair'=16,'col'=8] {'col'}, dimensions={0} | all-to-all | bytes 4194304 | tf_op jit(solution)/shard_map/all_to_all | solution.py:60
  44.8 0.4 reduce_sum.84
  45.2 3.1 %collective-permute-start = (bf16[512,256]{1,0:T(8,128)(2,1)S(1)}, bf16[512,256]{1,0:T(8,128)(2,1)S(1)}, u32[]{:S(2)}, u32[]{:S(2)}) collective-permute-start(bf16[512,256]{1,0:T(8,128)(2,1)S(1)} %reduce_sum.84), channel_id=1, source_target_pairs={{0,32},{8,40},{16,48},{24,56},{32,0},{40,8},{48,16},{56,24},{64,96... | collective-permute-start | bytes 786440 | tf_op jit(solution)/shard_map/ppermute | solution.py:16
  48.3 4.9 %collective-permute-done.vector_ref = bf16[512,256]{1,0:T(8,128)(2,1)S(1)} collective-permute-done((bf16[512,256]{1,0:T(8,128)(2,1)S(1)}, bf16[512,256]{1,0:T(8,128)(2,1)S(1)}, u32[]{:S(2)}, u32[]{:S(2)}) %collective-permute-start) | collective-permute-done | bytes 262176 | tf_op jit(solution)/shard_map/ppermute | solution.py:16
  53.2 0.8 pad_maximum_fusion.1.turned_ref
  53.9 6.6 %shard_map.56 = bf16[4096,256]{1,0:T(8,128)(2,1)} custom-call(bf16[1,2,4096,512]{3,2,1,0:T(8,128)(2,1)} %matrix_ref.12, bf16[512,256]{1,0:T(8,128)(2,1)} %copy-done.5, bf16[512,256]{1,0:T(8,128)(2,1)} %pad_maximum_fusion.1.turned_ref), custom_call_target="tpu_custom_call" | custom-call | flops 2147483648 | bytes 11010048 | tf_op jit(solution)/shard_map/pallas_call | solution.py:73
  60.5 29.7 %all_to_all.41 = bf16[8,512,256]{2,1,0:T(8,128)(2,1)S(1)} all-to-all(bf16[8,512,256]{2,1,0:T(8,128)(2,1)} %bitcast.43), channel_id=1, replica_groups=mesh['pair'=16,'col'=8] {'col'}, dimensions={0} | all-to-all | bytes 4194304 | tf_op jit(solution)/shard_map/all_to_all | solution.py:60
  90.2 0.3 convert_reduce_fusion.2
  90.5 0.6 copy-done
  91.3 0.7 pad_maximum_fusion.2.turned_ref
  92.0 6.6 %shard_map.57 = bf16[4096,256]{1,0:T(8,128)(2,1)} custom-call(bf16[1,2,4096,512]{3,2,1,0:T(8,128)(2,1)} %matrix_ref.13, bf16[512,256]{1,0:T(8,128)(2,1)} %copy-done.2, bf16[512,256]{1,0:T(8,128)(2,1)} %pad_maximum_fusion.2.turned_ref), custom_call_target="tpu_custom_call" | custom-call | flops 2147483648 | bytes 11010048 | tf_op jit(solution)/shard_map/pallas_call | solution.py:73
  98.6 28.5 %all_to_all.42 = bf16[8,512,256]{2,1,0:T(8,128)(2,1)S(1)} all-to-all(bf16[8,512,256]{2,1,0:T(8,128)(2,1)} %bitcast.44), channel_id=1, replica_groups=mesh['pair'=16,'col'=8] {'col'}, dimensions={0} | all-to-all | bytes 4194304 | tf_op jit(solution)/shard_map/all_to_all | solution.py:60
  127.2 0.4 reduce_sum.86
  127.6 3.1 %collective-permute-start.1 = (bf16[512,256]{1,0:T(8,128)(2,1)S(1)}, bf16[512,256]{1,0:T(8,128)(2,1)S(1)}, u32[]{:S(2)}, u32[]{:S(2)}) collective-permute-start(bf16[512,256]{1,0:T(8,128)(2,1)S(1)} %reduce_sum.86), channel_id=1, source_target_pairs={{0,32},{8,40},{16,48},{24,56},{32,0},{40,8},{48,16},{56,24},{64,96... | collective-permute-start | bytes 786440 | tf_op jit(solution)/shard_map/ppermute | solution.py:16
  130.7 4.9 %collective-permute-done.1.vector_ref = bf16[512,256]{1,0:T(8,128)(2,1)S(1)} collective-permute-done((bf16[512,256]{1,0:T(8,128)(2,1)S(1)}, bf16[512,256]{1,0:T(8,128)(2,1)S(1)}, u32[]{:S(2)}, u32[]{:S(2)}) %collective-permute-start.1) | collective-permute-done | bytes 262176 | tf_op jit(solution)/shard_map/ppermute | solution.py:16
  135.6 0.8 pad_maximum_fusion.3.turned_ref
  136.3 6.6 %shard_map.58 = bf16[4096,256]{1,0:T(8,128)(2,1)} custom-call(bf16[1,2,4096,512]{3,2,1,0:T(8,128)(2,1)} %matrix_ref.12, bf16[512,256]{1,0:T(8,128)(2,1)} %copy-done.6, bf16[512,256]{1,0:T(8,128)(2,1)} %pad_maximum_fusion.3.turned_ref), custom_call_target="tpu_custom_call" | custom-call | flops 2147483648 | bytes 11010048 | tf_op jit(solution)/shard_map/pallas_call | solution.py:73
  142.9 26.0 %all_to_all.43 = bf16[8,512,256]{2,1,0:T(8,128)(2,1)S(1)} all-to-all(bf16[8,512,256]{2,1,0:T(8,128)(2,1)} %bitcast.45), channel_id=1, replica_groups=mesh['pair'=16,'col'=8] {'col'}, dimensions={0} | all-to-all | bytes 4194304 | tf_op jit(solution)/shard_map/all_to_all | solution.py:60
  168.9 0.3 convert_reduce_fusion.1
  169.3 0.7 pad_maximum_fusion.4.turned_ref
  170.1 6.6 %shard_map.59 = bf16[4096,256]{1,0:T(8,128)(2,1)} custom-call(bf16[1,2,4096,512]{3,2,1,0:T(8,128)(2,1)} %matrix_ref.13, bf16[512,256]{1,0:T(8,128)(2,1)} %copy-done.3, bf16[512,256]{1,0:T(8,128)(2,1)} %pad_maximum_fusion.4.turned_ref), custom_call_target="tpu_custom_call" | custom-call | flops 2147483648 | bytes 11010048 | tf_op jit(solution)/shard_map/pallas_call | solution.py:73
  176.6 24.5 %all_to_all.44 = bf16[8,512,256]{2,1,0:T(8,128)(2,1)S(1)} all-to-all(bf16[8,512,256]{2,1,0:T(8,128)(2,1)} %bitcast.46), channel_id=1, replica_groups=mesh['pair'=16,'col'=8] {'col'}, dimensions={0} | all-to-all | bytes 4194304 | tf_op jit(solution)/shard_map/all_to_all | solution.py:60
  201.1 0.4 reduce_sum.88
  201.5 3.1 %collective-permute-start.2 = (bf16[512,256]{1,0:T(8,128)(2,1)S(1)}, bf16[512,256]{1,0:T(8,128)(2,1)S(1)}, u32[]{:S(2)}, u32[]{:S(2)}) collective-permute-start(bf16[512,256]{1,0:T(8,128)(2,1)S(1)} %reduce_sum.88), channel_id=1, source_target_pairs={{0,32},{8,40},{16,48},{24,56},{32,0},{40,8},{48,16},{56,24},{64,96... | collective-permute-start | bytes 786440 | tf_op jit(solution)/shard_map/ppermute | solution.py:16
  204.6 4.9 %collective-permute-done.2.vector_ref = bf16[512,256]{1,0:T(8,128)(2,1)S(1)} collective-permute-done((bf16[512,256]{1,0:T(8,128)(2,1)S(1)}, bf16[512,256]{1,0:T(8,128)(2,1)S(1)}, u32[]{:S(2)}, u32[]{:S(2)}) %collective-permute-start.2) | collective-permute-done | bytes 262176 | tf_op jit(solution)/shard_map/ppermute | solution.py:16
  209.5 0.8 pad_maximum_fusion.5.turned_ref
  210.3 6.6 %shard_map.60 = bf16[4096,256]{1,0:T(8,128)(2,1)} custom-call(bf16[1,2,4096,512]{3,2,1,0:T(8,128)(2,1)} %matrix_ref.12, bf16[512,256]{1,0:T(8,128)(2,1)} %copy-done.7, bf16[512,256]{1,0:T(8,128)(2,1)} %pad_maximum_fusion.5.turned_ref), custom_call_target="tpu_custom_call" | custom-call | flops 2147483648 | bytes 11010048 | tf_op jit(solution)/shard_map/pallas_call | solution.py:73
  216.9 22.1 %all_to_all.45 = bf16[8,512,256]{2,1,0:T(8,128)(2,1)S(1)} all-to-all(bf16[8,512,256]{2,1,0:T(8,128)(2,1)} %bitcast.47), channel_id=1, replica_groups=mesh['pair'=16,'col'=8] {'col'}, dimensions={0} | all-to-all | bytes 4194304 | tf_op jit(solution)/shard_map/all_to_all | solution.py:60
  239.0 0.3 convert_reduce_fusion
  239.4 0.7 pad_maximum_fusion.6.turned_ref
  240.2 6.6 %shard_map.61 = bf16[4096,256]{1,0:T(8,128)(2,1)} custom-call(bf16[1,2,4096,512]{3,2,1,0:T(8,128)(2,1)} %matrix_ref.13, bf16[512,256]{1,0:T(8,128)(2,1)} %copy-done.4, bf16[512,256]{1,0:T(8,128)(2,1)} %pad_maximum_fusion.6.turned_ref), custom_call_target="tpu_custom_call" | custom-call | flops 2147483648 | bytes 11010048 | tf_op jit(solution)/shard_map/pallas_call | solution.py:73
  246.8 3.7 %all-to-all-start.6 = ((bf16[8,512,256]{2,1,0:T(8,128)(2,1)}), bf16[8,512,256]{2,1,0:T(8,128)(2,1)S(1)}, u32[]{:S(2)}, u32[]{:S(2)}) async-start(bf16[8,512,256]{2,1,0:T(8,128)(2,1)} %bitcast.42), calls=%async_computation.6 | async-start | bytes 4194304 | tf_op jit(solution)/shard_map/all_to_all | solution.py:60
  250.6 0.6 fusion.49
  251.2 2.1 fusion.42
  253.3 2.1 fusion.43
  255.5 11.5 %all-to-all-done.6 = bf16[8,512,256]{2,1,0:T(8,128)(2,1)S(1)} async-done(((bf16[8,512,256]{2,1,0:T(8,128)(2,1)}), bf16[8,512,256]{2,1,0:T(8,128)(2,1)S(1)}, u32[]{:S(2)}, u32[]{:S(2)}) %all-to-all-start.6) | async-done | bytes 2097184 | tf_op jit(solution)/shard_map/all_to_all | solution.py:60
  267.0 0.4 reduce_sum.90
  267.7 3.3 %collective-permute-start.3 = (bf16[512,128]{1,0:T(8,128)(2,1)S(1)}, bf16[512,128]{1,0:T(8,128)(2,1)S(1)}, u32[]{:S(2)}, u32[]{:S(2)}) collective-permute-start(bf16[512,128]{1,0:T(8,128)(2,1)S(1)} %pad_maximum_fusion.7), channel_id=1, source_target_pairs={{0,32},{8,40},{16,48},{24,56},{32,0},{40,8},{48,16},{56,24},{64,96... | collective-permute-start | bytes 393224 | tf_op jit(solution)/shard_map/ppermute | solution.py:16
  271.0 1.9 fusion.44
  272.9 1.9 fusion.45
  275.0 2.6 fusion.1
  277.8 0.9 fusion
  278.7 0.4 multiply_add_fusion
  279.5 14.7 %all_to_all.46 = bf16[8,256,128]{1,2,0:T(8,128)(2,1)S(1)} all-to-all(bf16[8,256,128]{1,2,0:T(8,128)(2,1)S(1)} %fusion.6), channel_id=1, replica_groups=mesh['pair'=16,'col'=8] {'col'}, dimensions={0} | all-to-all | bytes 1048576 | tf_op jit(solution)/shard_map/all_to_all | solution.py:60
  294.3 0.8 copy.11
  (37 shorter events, 1.5 us)
Async XLA Ops:
  45.2 8.0 %collective-permute-start = (bf16[512,256]{1,0:T(8,128)(2,1)S(1)}, bf16[512,256]{1,0:T(8,128)(2,1)S(1)}, u32[]{:S(2)}, u32[]{:S(2)}) collective-permute-start(bf16[512,256]{1,0:T(8,128)(2,1)S(1)} %reduce_sum.84), channel_id=1, source_target_pairs={{0,32},{8,40},{16,48},{24,56},{32,0},{40,8},{48,16},{56,24},{64,96... | collective-permute-start | bytes 786440 | tf_op jit(solution)/shard_map/ppermute | solution.py:16
  53.1 0.8 copy-start.5
  90.2 1.0 copy-start
  91.2 0.8 copy-start.2
  127.6 8.0 %collective-permute-start.1 = (bf16[512,256]{1,0:T(8,128)(2,1)S(1)}, bf16[512,256]{1,0:T(8,128)(2,1)S(1)}, u32[]{:S(2)}, u32[]{:S(2)}) collective-permute-start(bf16[512,256]{1,0:T(8,128)(2,1)S(1)} %reduce_sum.86), channel_id=1, source_target_pairs={{0,32},{8,40},{16,48},{24,56},{32,0},{40,8},{48,16},{56,24},{64,96... | collective-permute-start | bytes 786440 | tf_op jit(solution)/shard_map/ppermute | solution.py:16
  135.5 0.8 copy-start.6
  169.3 0.8 copy-start.3
  201.5 8.0 %collective-permute-start.2 = (bf16[512,256]{1,0:T(8,128)(2,1)S(1)}, bf16[512,256]{1,0:T(8,128)(2,1)S(1)}, u32[]{:S(2)}, u32[]{:S(2)}) collective-permute-start(bf16[512,256]{1,0:T(8,128)(2,1)S(1)} %reduce_sum.88), channel_id=1, source_target_pairs={{0,32},{8,40},{16,48},{24,56},{32,0},{40,8},{48,16},{56,24},{64,96... | collective-permute-start | bytes 786440 | tf_op jit(solution)/shard_map/ppermute | solution.py:16
  209.5 0.8 copy-start.7
  239.4 0.8 copy-start.4
  246.8 3.8 %copy-start.8 = (s32[16,3]{0,1:T(4,128)S(1)}, s32[16,3]{0,1:T(4,128)}, u32[]{:S(2)}) copy-start(s32[16,3]{0,1:T(4,128)} %param.9) | copy-start | bytes 580
  246.8 20.2 %all-to-all-start.6 = ((bf16[8,512,256]{2,1,0:T(8,128)(2,1)}), bf16[8,512,256]{2,1,0:T(8,128)(2,1)S(1)}, u32[]{:S(2)}, u32[]{:S(2)}) async-start(bf16[8,512,256]{2,1,0:T(8,128)(2,1)} %bitcast.42), calls=%async_computation.6 | async-start | bytes 4194304 | tf_op jit(solution)/shard_map/all_to_all | solution.py:60
  267.7 7.1 %collective-permute-start.3 = (bf16[512,128]{1,0:T(8,128)(2,1)S(1)}, bf16[512,128]{1,0:T(8,128)(2,1)S(1)}, u32[]{:S(2)}, u32[]{:S(2)}) collective-permute-start(bf16[512,128]{1,0:T(8,128)(2,1)S(1)} %pad_maximum_fusion.7), channel_id=1, source_target_pairs={{0,32},{8,40},{16,48},{24,56},{32,0},{40,8},{48,16},{56,24},{64,96... | collective-permute-start | bytes 393224 | tf_op jit(solution)/shard_map/ppermute | solution.py:16
  275.0 2.8 copy-start.1

commit v4 on v1

--- a/solution.py
+++ b/solution.py
@@ -61,9 +61,8 @@
 
 
 def product(matrix, vector):
-    return jnp.dot(matrix[0], vector, preferred_element_type=jnp.float32) + jnp.dot(
-        matrix[1], turned_block(vector), preferred_element_type=jnp.float32
-    )
+    stacked = jnp.stack([vector, turned_block(vector)])
+    return jnp.einsum("prc,pck->rk", matrix, stacked, preferred_element_type=jnp.float32)
 
 
 def on_device(tmatrix, translation, incident, farfield, centres):

time: 285 us -> 281 us (0.986)
  matrix products: 37 us -> 33.8 us
    dot_general x14 -> x7, matrix products: 34 us -> 30.6 us  [product(): jnp.einsum('prc,pck->rk', matrix, stacked, preferred_element_type=jnp.flo...]
where the time goes in v4:
time: 281 us; the launch traced here: 280 us
  blocking collectives  185 us (66%)
  matrix products  33.8 us (12%)
  waiting for transfers between devices  27.2 us (10%)
  starting transfers between devices  16.2 us (6%)
  other arithmetic  12 us (4%)
  local copies, waits for them, and re-layouts  5.53 us (2%)
    all_to_all x7, blocking collectives, col_sum(): received = lax.all_to_all(blocks, 'col', 0, 0)  185 us
    dot_general x7, matrix products, product(): jnp.einsum('prc,pck->rk', matrix, stacked, preferred_element_type=jnp.flo...  30.6 us
    ppermute x4, waiting for transfers between devices, partner(): return lax.ppermute(value, axis, pairs)  14.5 us
    all_to_all x1, waiting for transfers between devices, col_sum(): received = lax.all_to_all(blocks, 'col', 0, 0)  12.7 us
    ppermute x4, starting transfers between devices, partner(): return lax.ppermute(value, axis, pairs)  12.5 us
  transfers between devices with their start and end apart: 5, of which 4 were waited for; matrix products, arithmetic and copies ran while one was open for 3% of the time, Pallas kernels for 0%

profile of v4, /device:TPU:0, one launch (start us, length us, event | category | flops | bytes accessed | tf_op | source)
XLA Modules:
  0.0 280.1 jit_solution(4731092735786897245)
XLA Ops:
  0.0 1.1 copy.9
  1.2 5.8 %fusion.53 = bf16[256,4096]{1,0:T(8,128)(2,1)S(1)} fusion(bf16[1,2,4096,512]{3,2,1,0:T(8,128)(2,1)} %param.5, bf16[1,512,256]{1,2,0:T(8,128)(2,1)S(1)} %maximum_bitcast_fusion, bf16[1,512,256]{1,2,0:T(8,128)(2,1)S(1)} %copy.9), kind=kOutput, calls=%fused_computation.27 | convolution fusion | flops 2148794368 | bytes 11010048 | tf_op jit(solution)/shard_map/prc,pck->rk/dot_general | solution.py:65
  6.9 0.2 copy.60
  7.1 36.2 %all_to_all.40 = bf16[8,512,256]{1,2,0:T(8,128)(2,1)S(1)} all-to-all(bf16[8,512,256]{1,2,0:T(8,128)(2,1)S(1)} %bitcast.167), channel_id=1, replica_groups=mesh['pair'=16,'col'=8] {'col'}, dimensions={0} | all-to-all | bytes 4194304 | tf_op jit(solution)/shard_map/all_to_all | solution.py:59
  43.3 0.4 reduce_sum.90
  43.7 3.1 %collective-permute-start = (bf16[512,256]{0,1:T(8,128)(2,1)S(1)}, bf16[512,256]{0,1:T(8,128)(2,1)S(1)}, u32[]{:S(2)}, u32[]{:S(2)}) collective-permute-start(bf16[512,256]{0,1:T(8,128)(2,1)S(1)} %reduce_sum.90), channel_id=1, source_target_pairs={{0,32},{8,40},{16,48},{24,56},{32,0},{40,8},{48,16},{56,24},{64,96... | collective-permute-start | bytes 786440 | tf_op jit(solution)/shard_map/ppermute | solution.py:15
  46.8 4.9 %collective-permute-done = bf16[512,256]{0,1:T(8,128)(2,1)S(1)} collective-permute-done((bf16[512,256]{0,1:T(8,128)(2,1)S(1)}, bf16[512,256]{0,1:T(8,128)(2,1)S(1)}, u32[]{:S(2)}, u32[]{:S(2)}) %collective-permute-start) | collective-permute-done | bytes 262176 | tf_op jit(solution)/shard_map/ppermute | solution.py:15
  51.7 5.9 %fusion.41 = bf16[256,4096]{1,0:T(8,128)(2,1)S(1)} fusion(bf16[1,2,4096,512]{3,2,1,0:T(8,128)(2,1)} %param.6, bf16[1,512,256]{1,2,0:T(8,128)(2,1)S(1)} %maximum_bitcast_fusion.1, bf16[1,512,256]{1,2,0:T(8,128)(2,1)S(1)} %bitcast.189), kind=kOutput, calls=%fused_computation.23 | convolution fusion | flops 2148794368 | bytes 11010048 | tf_op jit(solution)/shard_map/prc,pck->rk/dot_general | solution.py:65
  57.6 0.2 copy.59
  57.8 29.8 %all_to_all.41 = bf16[8,512,256]{1,2,0:T(8,128)(2,1)S(1)} all-to-all(bf16[8,512,256]{1,2,0:T(8,128)(2,1)S(1)} %bitcast.168), channel_id=1, replica_groups=mesh['pair'=16,'col'=8] {'col'}, dimensions={0} | all-to-all | bytes 4194304 | tf_op jit(solution)/shard_map/all_to_all | solution.py:59
  87.6 0.3 convert_reduce_fusion.2
  88.2 2.4 fusion.50
  90.6 0.2 copy.58
  90.7 28.3 %all_to_all.42 = bf16[8,512,256]{1,2,0:T(8,128)(2,1)S(1)} all-to-all(bf16[8,512,256]{1,2,0:T(8,128)(2,1)S(1)} %bitcast.169), channel_id=1, replica_groups=mesh['pair'=16,'col'=8] {'col'}, dimensions={0} | all-to-all | bytes 4194304 | tf_op jit(solution)/shard_map/all_to_all | solution.py:59
  119.1 0.4 reduce_sum.93
  119.5 3.1 %collective-permute-start.1 = (bf16[512,256]{0,1:T(8,128)(2,1)S(1)}, bf16[512,256]{0,1:T(8,128)(2,1)S(1)}, u32[]{:S(2)}, u32[]{:S(2)}) collective-permute-start(bf16[512,256]{0,1:T(8,128)(2,1)S(1)} %reduce_sum.93), channel_id=1, source_target_pairs={{0,32},{8,40},{16,48},{24,56},{32,0},{40,8},{48,16},{56,24},{64,96... | collective-permute-start | bytes 786440 | tf_op jit(solution)/shard_map/ppermute | solution.py:15
  122.6 4.9 %collective-permute-done.1 = bf16[512,256]{0,1:T(8,128)(2,1)S(1)} collective-permute-done((bf16[512,256]{0,1:T(8,128)(2,1)S(1)}, bf16[512,256]{0,1:T(8,128)(2,1)S(1)}, u32[]{:S(2)}, u32[]{:S(2)}) %collective-permute-start.1) | collective-permute-done | bytes 262176 | tf_op jit(solution)/shard_map/ppermute | solution.py:15
  127.5 5.9 %fusion.38 = bf16[256,4096]{1,0:T(8,128)(2,1)S(1)} fusion(bf16[1,2,4096,512]{3,2,1,0:T(8,128)(2,1)} %param.6, bf16[1,512,256]{1,2,0:T(8,128)(2,1)S(1)} %maximum_bitcast_fusion.3, bf16[1,512,256]{1,2,0:T(8,128)(2,1)S(1)} %bitcast.190), kind=kOutput, calls=%fused_computation.22 | convolution fusion | flops 2148794368 | bytes 11010048 | tf_op jit(solution)/shard_map/prc,pck->rk/dot_general | solution.py:65
  133.4 0.2 copy.57
  133.6 26.5 %all_to_all.43 = bf16[8,512,256]{1,2,0:T(8,128)(2,1)S(1)} all-to-all(bf16[8,512,256]{1,2,0:T(8,128)(2,1)S(1)} %bitcast.170), channel_id=1, replica_groups=mesh['pair'=16,'col'=8] {'col'}, dimensions={0} | all-to-all | bytes 4194304 | tf_op jit(solution)/shard_map/all_to_all | solution.py:59
  160.1 0.3 convert_reduce_fusion.1
  160.6 2.4 fusion.47
  163.0 0.2 copy.56
  163.2 25.5 %all_to_all.44 = bf16[8,512,256]{1,2,0:T(8,128)(2,1)S(1)} all-to-all(bf16[8,512,256]{1,2,0:T(8,128)(2,1)S(1)} %bitcast.171), channel_id=1, replica_groups=mesh['pair'=16,'col'=8] {'col'}, dimensions={0} | all-to-all | bytes 4194304 | tf_op jit(solution)/shard_map/all_to_all | solution.py:59
  188.7 0.4 reduce_sum.96
  189.1 3.1 %collective-permute-start.2 = (bf16[512,256]{0,1:T(8,128)(2,1)S(1)}, bf16[512,256]{0,1:T(8,128)(2,1)S(1)}, u32[]{:S(2)}, u32[]{:S(2)}) collective-permute-start(bf16[512,256]{0,1:T(8,128)(2,1)S(1)} %reduce_sum.96), channel_id=1, source_target_pairs={{0,32},{8,40},{16,48},{24,56},{32,0},{40,8},{48,16},{56,24},{64,96... | collective-permute-start | bytes 786440 | tf_op jit(solution)/shard_map/ppermute | solution.py:15
  192.2 4.8 %collective-permute-done.2 = bf16[512,256]{0,1:T(8,128)(2,1)S(1)} collective-permute-done((bf16[512,256]{0,1:T(8,128)(2,1)S(1)}, bf16[512,256]{0,1:T(8,128)(2,1)S(1)}, u32[]{:S(2)}, u32[]{:S(2)}) %collective-permute-start.2) | collective-permute-done | bytes 262176 | tf_op jit(solution)/shard_map/ppermute | solution.py:15
  197.1 5.9 %fusion.35 = bf16[256,4096]{1,0:T(8,128)(2,1)S(1)} fusion(bf16[1,2,4096,512]{3,2,1,0:T(8,128)(2,1)} %param.6, bf16[1,512,256]{1,2,0:T(8,128)(2,1)S(1)} %maximum_bitcast_fusion.5, bf16[1,512,256]{1,2,0:T(8,128)(2,1)S(1)} %bitcast.191), kind=kOutput, calls=%fused_computation.21 | convolution fusion | flops 2148794368 | bytes 11010048 | tf_op jit(solution)/shard_map/prc,pck->rk/dot_general | solution.py:65
  203.2 23.7 %all_to_all.45 = bf16[8,512,256]{1,2,0:T(8,128)(2,1)S(1)} all-to-all(bf16[8,512,256]{1,2,0:T(8,128)(2,1)S(1)} %bitcast.172), channel_id=1, replica_groups=mesh['pair'=16,'col'=8] {'col'}, dimensions={0} | all-to-all | bytes 4194304 | tf_op jit(solution)/shard_map/all_to_all | solution.py:59
  226.9 0.3 convert_reduce_fusion
  227.5 2.4 fusion.44
  229.9 1.5 copy.54
  231.4 3.7 %all-to-all-start.6 = ((bf16[8,512,256]{1,2,0:T(8,128)(2,1)}), bf16[8,512,256]{1,2,0:T(8,128)(2,1)S(1)}, u32[]{:S(2)}, u32[]{:S(2)}) async-start(bf16[8,512,256]{1,2,0:T(8,128)(2,1)} %bitcast.166), calls=%async_computation.6 | async-start | bytes 4194304 | tf_op jit(solution)/shard_map/all_to_all | solution.py:59
  235.2 0.6 fusion.136
  235.8 2.0 fusion.122
  237.8 2.0 fusion.123
  239.8 12.7 %all-to-all-done.6 = bf16[8,512,256]{1,2,0:T(8,128)(2,1)S(1)} async-done(((bf16[8,512,256]{1,2,0:T(8,128)(2,1)}), bf16[8,512,256]{1,2,0:T(8,128)(2,1)S(1)}, u32[]{:S(2)}, u32[]{:S(2)}) %all-to-all-start.6) | async-done | bytes 2097184 | tf_op jit(solution)/shard_map/all_to_all | solution.py:59
  252.5 0.4 reduce_sum.99
  253.0 3.1 %collective-permute-start.3 = (bf16[512,128]{0,1:T(8,128)(2,1)S(1)}, bf16[512,128]{0,1:T(8,128)(2,1)S(1)}, u32[]{:S(2)}, u32[]{:S(2)}) collective-permute-start(bf16[512,128]{0,1:T(8,128)(2,1)S(1)} %pad_maximum_fusion), channel_id=1, source_target_pairs={{0,32},{8,40},{16,48},{24,56},{32,0},{40,8},{48,16},{56,24},{64,96... | collective-permute-start | bytes 393224 | tf_op jit(solution)/shard_map/ppermute | solution.py:15
  256.1 2.0 fusion.124
  258.2 2.1 fusion.125
  260.3 2.5 fusion.57
  262.8 0.3 copy-done
  263.1 0.7 fusion.56
  263.8 0.3 multiply_add_fusion
  264.3 0.2 fusion.62
  264.5 14.8 %all_to_all.46 = bf16[8,256,128]{1,2,0:T(8,128)(2,1)S(1)} all-to-all(bf16[8,256,128]{1,2,0:T(8,128)(2,1)S(1)} %fusion.62), channel_id=1, replica_groups=mesh['pair'=16,'col'=8] {'col'}, dimensions={0} | all-to-all | bytes 1048576 | tf_op jit(solution)/shard_map/all_to_all | solution.py:59
  279.4 0.8 copy.25
  (49 shorter events, 1.4 us)
Async XLA Ops:
  43.7 8.0 %collective-permute-start = (bf16[512,256]{0,1:T(8,128)(2,1)S(1)}, bf16[512,256]{0,1:T(8,128)(2,1)S(1)}, u32[]{:S(2)}, u32[]{:S(2)}) collective-permute-start(bf16[512,256]{0,1:T(8,128)(2,1)S(1)} %reduce_sum.90), channel_id=1, source_target_pairs={{0,32},{8,40},{16,48},{24,56},{32,0},{40,8},{48,16},{56,24},{64,96... | collective-permute-start | bytes 786440 | tf_op jit(solution)/shard_map/ppermute | solution.py:15
  51.7 36.5 %slice-start = ((s8[8388608]{0:T(1024)(128)(4,1)}), s8[4194304]{0:T(1024)(128)(4,1)S(1)}, s32[]{:S(2)}) async-start(s8[8388608]{0:T(1024)(128)(4,1)} %bitcast.192), calls=%async_computation.8 | async-start | bytes 8388608
  57.6 30.5 %slice-start.1 = ((s8[8388608]{0:T(1024)(128)(4,1)}), s8[4194304]{0:T(1024)(128)(4,1)S(1)}, s32[]{:S(2)}) async-start(s8[8388608]{0:T(1024)(128)(4,1)} %bitcast.192), calls=%async_computation.9 | async-start | bytes 8388608
  119.5 8.0 %collective-permute-start.1 = (bf16[512,256]{0,1:T(8,128)(2,1)S(1)}, bf16[512,256]{0,1:T(8,128)(2,1)S(1)}, u32[]{:S(2)}, u32[]{:S(2)}) collective-permute-start(bf16[512,256]{0,1:T(8,128)(2,1)S(1)} %reduce_sum.93), channel_id=1, source_target_pairs={{0,32},{8,40},{16,48},{24,56},{32,0},{40,8},{48,16},{56,24},{64,96... | collective-permute-start | bytes 786440 | tf_op jit(solution)/shard_map/ppermute | solution.py:15
  127.5 33.1 %slice-start.2 = ((s8[8388608]{0:T(1024)(128)(4,1)}), s8[4194304]{0:T(1024)(128)(4,1)S(1)}, s32[]{:S(2)}) async-start(s8[8388608]{0:T(1024)(128)(4,1)} %bitcast.194), calls=%async_computation.10 | async-start | bytes 8388608
  133.4 27.2 %slice-start.3 = ((s8[8388608]{0:T(1024)(128)(4,1)}), s8[4194304]{0:T(1024)(128)(4,1)S(1)}, s32[]{:S(2)}) async-start(s8[8388608]{0:T(1024)(128)(4,1)} %bitcast.194), calls=%async_computation.11 | async-start | bytes 8388608
  189.1 8.0 %collective-permute-start.2 = (bf16[512,256]{0,1:T(8,128)(2,1)S(1)}, bf16[512,256]{0,1:T(8,128)(2,1)S(1)}, u32[]{:S(2)}, u32[]{:S(2)}) collective-permute-start(bf16[512,256]{0,1:T(8,128)(2,1)S(1)} %reduce_sum.96), channel_id=1, source_target_pairs={{0,32},{8,40},{16,48},{24,56},{32,0},{40,8},{48,16},{56,24},{64,96... | collective-permute-start | bytes 786440 | tf_op jit(solution)/shard_map/ppermute | solution.py:15
  197.1 30.3 %slice-start.4 = ((s8[8388608]{0:T(1024)(128)(4,1)}), s8[4194304]{0:T(1024)(128)(4,1)S(1)}, s32[]{:S(2)}) async-start(s8[8388608]{0:T(1024)(128)(4,1)} %bitcast.196), calls=%async_computation.12 | async-start | bytes 8388608
  203.0 24.4 %slice-start.5 = ((s8[8388608]{0:T(1024)(128)(4,1)}), s8[4194304]{0:T(1024)(128)(4,1)S(1)}, s32[]{:S(2)}) async-start(s8[8388608]{0:T(1024)(128)(4,1)} %bitcast.196), calls=%async_computation.13 | async-start | bytes 8388608
  231.4 3.8 %copy-start.1 = (s32[16,3]{0,1:T(4,128)S(1)}, s32[16,3]{0,1:T(4,128)}, u32[]{:S(2)}) copy-start(s32[16,3]{0,1:T(4,128)} %param.9) | copy-start | bytes 580
  231.4 21.1 %all-to-all-start.6 = ((bf16[8,512,256]{1,2,0:T(8,128)(2,1)}), bf16[8,512,256]{1,2,0:T(8,128)(2,1)S(1)}, u32[]{:S(2)}, u32[]{:S(2)}) async-start(bf16[8,512,256]{1,2,0:T(8,128)(2,1)} %bitcast.166), calls=%async_computation.6 | async-start | bytes 4194304 | tf_op jit(solution)/shard_map/all_to_all | solution.py:59
  253.0 7.2 %collective-permute-start.3 = (bf16[512,128]{0,1:T(8,128)(2,1)S(1)}, bf16[512,128]{0,1:T(8,128)(2,1)S(1)}, u32[]{:S(2)}, u32[]{:S(2)}) collective-permute-start(bf16[512,128]{0,1:T(8,128)(2,1)S(1)} %pad_maximum_fusion), channel_id=1, source_target_pairs={{0,32},{8,40},{16,48},{24,56},{32,0},{40,8},{48,16},{56,24},{64,96... | collective-permute-start | bytes 393224 | tf_op jit(solution)/shard_map/ppermute | solution.py:15
  260.2 2.8 %copy-start = (bf16[2,2048,512]{2,1,0:T(8,128)(2,1)S(1)}, bf16[2,2048,512]{2,1,0:T(8,128)(2,1)}, u32[]{:S(2)}) copy-start(bf16[2,2048,512]{2,1,0:T(8,128)(2,1)} %param.8) | copy-start | bytes 12582916

commit v5 on v4

--- a/solution.py
+++ b/solution.py
@@ -4,6 +4,7 @@
 import jax.numpy as jnp
 from jax import lax
 from jax.sharding import PartitionSpec as P
+
 
 ITERS = 3
 LEVEL = 2
@@ -65,6 +66,19 @@
     return jnp.einsum("prc,pck->rk", matrix, stacked, preferred_element_type=jnp.float32)
 
 
+def split_product(matrix, parts):
+    total = None
+    start = 0
+    for index, piece in enumerate(parts):
+        rows = piece.shape[0]
+        term = product(matrix[:, :, start : start + rows], piece)
+        if index + 1 < len(parts):
+            term = lax.optimization_barrier(term)
+        total = term if total is None else total + term
+        start += rows
+    return total
+
+
 def on_device(tmatrix, translation, incident, farfield, centres):
     pair_index = lax.axis_index("pair")
     column_half = jnp.bitwise_and(jnp.right_shift(pair_index, LEVEL), 1)
@@ -78,11 +92,12 @@
     full_width = own_incident.shape[1] // 2
     half_width = full_width // 2
     coeffs = col_sum(product(own_matrix, own_incident)).astype(jnp.bfloat16)
-    for iteration in range(ITERS):
-        partner_coeffs = partner(coeffs, "pair", LEVEL)
-        driven = (
-            own_incident.astype(jnp.float32) + col_sum(product(own_coupling, partner_coeffs))
-        ).astype(jnp.bfloat16)
+    for _ in range(ITERS):
+        half_rows = coeffs.shape[0] // 2
+        first_part = partner(coeffs[:half_rows], "pair", LEVEL)
+        second_part = partner(coeffs[half_rows:], "pair", LEVEL)
+        summed = col_sum(split_product(own_coupling, [first_part, second_part]))
+        driven = (own_incident.astype(jnp.float32) + summed).astype(jnp.bfloat16)
         coeffs = col_sum(product(own_matrix, driven)).astype(jnp.bfloat16)
     incoming = partner(pick_half(coeffs, 1 - column_half, half_width), "pair", LEVEL)
     own_half = pick_half(coeffs, column_half, half_width)

time: 281 us -> 275 us (0.979)
  blocking collectives: 185 us -> 178 us
  waiting for transfers between devices: 27.2 us -> 22 us
  matrix products: 33.8 us -> 36.8 us
    all_to_all x7, blocking collectives: 185 us -> 178 us  [col_sum(): received = lax.all_to_all(blocks, 'col', 0, 0)]
    ppermute x4 -> x7, waiting for transfers between devices: 14.5 us -> 10.1 us  [partner(): return lax.ppermute(value, axis, pairs)]
    dot_general x7 -> x10, matrix products: 30.6 us -> 33.7 us  [product(): jnp.einsum('prc,pck->rk', matrix, stacked, preferred_element_type=jnp.flo...]
    ppermute x4 -> x7, starting transfers between devices: 12.5 us -> 14.1 us  [partner(): return lax.ppermute(value, axis, pairs)]
  transfers between devices with their start and end apart: 5 -> 8, of which waited for: 4 -> 4; matrix products, arithmetic and copies ran while one was open for 3% -> 7% of each run, Pallas kernels for 0% -> 0%
where the time goes in v5:
time: 275 us; the launch traced here: 274 us
  blocking collectives  178 us (65%)
  matrix products  36.8 us (13%)
  waiting for transfers between devices  22 us (8%)
  starting transfers between devices  17.7 us (6%)
  other arithmetic  13.9 us (5%)
  local copies, waits for them, and re-layouts  5.35 us (2%)
    all_to_all x7, blocking collectives, col_sum(): received = lax.all_to_all(blocks, 'col', 0, 0)  178 us
    dot_general x10, matrix products, product(): jnp.einsum('prc,pck->rk', matrix, stacked, preferred_element_type=jnp.flo...  33.7 us
    ppermute x7, starting transfers between devices, partner(): return lax.ppermute(value, axis, pairs)  14.1 us
    all_to_all x1, waiting for transfers between devices, col_sum(): received = lax.all_to_all(blocks, 'col', 0, 0)  12 us
    ppermute x7, waiting for transfers between devices, partner(): return lax.ppermute(value, axis, pairs)  10.1 us
  transfers between devices with their start and end apart: 8, of which 4 were waited for; matrix products, arithmetic and copies ran while one was open for 7% of the time, Pallas kernels for 0%

profile of v5, /device:TPU:0, one launch (start us, length us, event | category | flops | bytes accessed | tf_op | source)
XLA Modules:
  0.0 274.5 jit_solution(1707121652146279083)
XLA Ops:
  0.0 1.1 copy.9
  1.2 5.8 %fusion.29 = bf16[256,4096]{1,0:T(8,128)(2,1)S(1)} fusion(bf16[1,2,4096,512]{3,2,1,0:T(8,128)(2,1)} %param.5, bf16[1,512,256]{1,2,0:T(8,128)(2,1)S(1)} %maximum_bitcast_fusion, bf16[1,512,256]{1,2,0:T(8,128)(2,1)S(1)} %copy.9), kind=kOutput, calls=%fused_computation.21 | convolution fusion | flops 2148794368 | bytes 11010048 | tf_op jit(solution)/shard_map/prc,pck->rk/dot_general | solution.py:66
  7.1 36.2 %all_to_all.40 = bf16[8,512,256]{1,2,0:T(8,128)(2,1)S(1)} all-to-all(bf16[8,512,256]{1,2,0:T(8,128)(2,1)S(1)} %bitcast.176), channel_id=1, replica_groups=mesh['pair'=16,'col'=8] {'col'}, dimensions={0} | all-to-all | bytes 4194304 | tf_op jit(solution)/shard_map/all_to_all | solution.py:60
  43.3 0.4 reduce_sum.90
  43.7 3.1 %collective-permute-start = (bf16[256,256]{0,1:T(8,128)(2,1)S(1)}, bf16[256,256]{0,1:T(8,128)(2,1)S(1)}, u32[]{:S(2)}, u32[]{:S(2)}) collective-permute-start(bf16[256,256]{0,1:T(8,128)(2,1)S(1)} %get-tuple-element.27), channel_id=1, source_target_pairs={{0,32},{8,40},{16,48},{24,56},{32,0},{40,8},{48,16},{56,24},{64,96... | collective-permute-start | bytes 393224 | tf_op jit(solution)/shard_map/ppermute | solution.py:16
  46.8 0.5 collective-permute-start.1
  47.3 4.2 %collective-permute-done = bf16[256,256]{0,1:T(8,128)(2,1)S(1)} collective-permute-done((bf16[256,256]{0,1:T(8,128)(2,1)S(1)}, bf16[256,256]{0,1:T(8,128)(2,1)S(1)}, u32[]{:S(2)}, u32[]{:S(2)}) %collective-permute-start) | collective-permute-done | bytes 131104 | tf_op jit(solution)/shard_map/ppermute | solution.py:16
  51.5 3.5 %convolution_bitcast_fusion.5 = f32[4096,256]{0,1:T(8,128)S(1)} fusion(bf16[2,4096,512]{2,1,0:T(8,128)(2,1)} %bitcast.165, bf16[1,256,256]{1,2,0:T(8,128)(2,1)S(1)} %maximum_bitcast_fusion.4, bf16[1,256,256]{1,2,0:T(8,128)(2,1)S(1)} %bitcast.197), kind=kOutput, calls=%fused_computation.17 | convolution fusion | flops 1073872896 | bytes 8650752 | tf_op jit(solution)/shard_map/prc,pck->rk/dot_general | solution.py:66
  55.1 3.5 %convolution_bitcast_fusion.4 = f32[4096,256]{0,1:T(8,128)S(1)} fusion(bf16[2,4096,512]{2,1,0:T(8,128)(2,1)} %bitcast.166, bf16[1,256,256]{1,2,0:T(8,128)(2,1)S(1)} %maximum_bitcast_fusion.5, bf16[1,256,256]{1,2,0:T(8,128)(2,1)S(1)} %bitcast.194), kind=kOutput, calls=%fused_computation.16 | convolution fusion | flops 1073872896 | bytes 8650752 | tf_op jit(solution)/shard_map/prc,pck->rk/dot_general | solution.py:66
  58.6 0.6 add_convert_fusion.2
  59.4 28.1 %all_to_all.41 = bf16[8,512,256]{1,2,0:T(8,128)(2,1)S(1)} all-to-all(bf16[8,512,256]{1,2,0:T(8,128)(2,1)S(1)} %bitcast.177), channel_id=1, replica_groups=mesh['pair'=16,'col'=8] {'col'}, dimensions={0} | all-to-all | bytes 4194304 | tf_op jit(solution)/shard_map/all_to_all | solution.py:60
  87.5 0.3 convert_reduce_fusion.2
  88.1 2.4 fusion.26
  90.6 26.9 %all_to_all.42 = bf16[8,512,256]{1,2,0:T(8,128)(2,1)S(1)} all-to-all(bf16[8,512,256]{1,2,0:T(8,128)(2,1)S(1)} %bitcast.178), channel_id=1, replica_groups=mesh['pair'=16,'col'=8] {'col'}, dimensions={0} | all-to-all | bytes 4194304 | tf_op jit(solution)/shard_map/all_to_all | solution.py:60
  117.6 0.4 reduce_sum.93
  118.0 2.9 %collective-permute-start.2 = (bf16[256,256]{0,1:T(8,128)(2,1)S(1)}, bf16[256,256]{0,1:T(8,128)(2,1)S(1)}, u32[]{:S(2)}, u32[]{:S(2)}) collective-permute-start(bf16[256,256]{0,1:T(8,128)(2,1)S(1)} %get-tuple-element.23), channel_id=1, source_target_pairs={{0,32},{8,40},{16,48},{24,56},{32,0},{40,8},{48,16},{56,24},{64,96... | collective-permute-start | bytes 393224 | tf_op jit(solution)/shard_map/ppermute | solution.py:16
  120.8 0.8 collective-permute-start.3
  121.6 2.9 %collective-permute-done.2 = bf16[256,256]{0,1:T(8,128)(2,1)S(1)} collective-permute-done((bf16[256,256]{0,1:T(8,128)(2,1)S(1)}, bf16[256,256]{0,1:T(8,128)(2,1)S(1)}, u32[]{:S(2)}, u32[]{:S(2)}) %collective-permute-start.2) | collective-permute-done | bytes 131104 | tf_op jit(solution)/shard_map/ppermute | solution.py:16
  124.5 3.5 %convolution_bitcast_fusion.3 = f32[4096,256]{0,1:T(8,128)S(1)} fusion(bf16[2,4096,512]{2,1,0:T(8,128)(2,1)} %bitcast.167, bf16[1,256,256]{1,2,0:T(8,128)(2,1)S(1)} %maximum_bitcast_fusion.6, bf16[1,256,256]{1,2,0:T(8,128)(2,1)S(1)} %bitcast.198), kind=kOutput, calls=%fused_computation.15 | convolution fusion | flops 1073872896 | bytes 8650752 | tf_op jit(solution)/shard_map/prc,pck->rk/dot_general | solution.py:66
  128.1 3.5 %convolution_bitcast_fusion.2 = f32[4096,256]{0,1:T(8,128)S(1)} fusion(bf16[2,4096,512]{2,1,0:T(8,128)(2,1)} %bitcast.168, bf16[1,256,256]{1,2,0:T(8,128)(2,1)S(1)} %maximum_bitcast_fusion.7, bf16[1,256,256]{1,2,0:T(8,128)(2,1)S(1)} %bitcast.195), kind=kOutput, calls=%fused_computation.14 | convolution fusion | flops 1073872896 | bytes 8650752 | tf_op jit(solution)/shard_map/prc,pck->rk/dot_general | solution.py:66
  131.6 0.6 add_convert_fusion.1
  132.4 25.1 %all_to_all.43 = bf16[8,512,256]{1,2,0:T(8,128)(2,1)S(1)} all-to-all(bf16[8,512,256]{1,2,0:T(8,128)(2,1)S(1)} %bitcast.179), channel_id=1, replica_groups=mesh['pair'=16,'col'=8] {'col'}, dimensions={0} | all-to-all | bytes 4194304 | tf_op jit(solution)/shard_map/all_to_all | solution.py:60
  157.5 0.3 convert_reduce_fusion.1
  158.1 2.4 fusion.23
  160.7 24.1 %all_to_all.44 = bf16[8,512,256]{1,2,0:T(8,128)(2,1)S(1)} all-to-all(bf16[8,512,256]{1,2,0:T(8,128)(2,1)S(1)} %bitcast.180), channel_id=1, replica_groups=mesh['pair'=16,'col'=8] {'col'}, dimensions={0} | all-to-all | bytes 4194304 | tf_op jit(solution)/shard_map/all_to_all | solution.py:60
  184.8 0.4 reduce_sum.96
  185.2 3.3 %collective-permute-start.4 = (bf16[256,256]{0,1:T(8,128)(2,1)S(1)}, bf16[256,256]{0,1:T(8,128)(2,1)S(1)}, u32[]{:S(2)}, u32[]{:S(2)}) collective-permute-start(bf16[256,256]{0,1:T(8,128)(2,1)S(1)} %get-tuple-element.19), channel_id=1, source_target_pairs={{0,32},{8,40},{16,48},{24,56},{32,0},{40,8},{48,16},{56,24},{64,96... | collective-permute-start | bytes 393224 | tf_op jit(solution)/shard_map/ppermute | solution.py:16
  188.5 0.3 collective-permute-start.5
  188.8 2.9 %collective-permute-done.4 = bf16[256,256]{0,1:T(8,128)(2,1)S(1)} collective-permute-done((bf16[256,256]{0,1:T(8,128)(2,1)S(1)}, bf16[256,256]{0,1:T(8,128)(2,1)S(1)}, u32[]{:S(2)}, u32[]{:S(2)}) %collective-permute-start.4) | collective-permute-done | bytes 131104 | tf_op jit(solution)/shard_map/ppermute | solution.py:16
  191.8 3.5 %convolution_bitcast_fusion.1 = f32[4096,256]{0,1:T(8,128)S(1)} fusion(bf16[2,4096,512]{2,1,0:T(8,128)(2,1)} %bitcast.169, bf16[1,256,256]{1,2,0:T(8,128)(2,1)S(1)} %maximum_bitcast_fusion.8, bf16[1,256,256]{1,2,0:T(8,128)(2,1)S(1)} %bitcast.199), kind=kOutput, calls=%fused_computation.13 | convolution fusion | flops 1073872896 | bytes 8650752 | tf_op jit(solution)/shard_map/prc,pck->rk/dot_general | solution.py:66
  195.3 3.5 %convolution_bitcast_fusion = f32[4096,256]{0,1:T(8,128)S(1)} fusion(bf16[2,4096,512]{2,1,0:T(8,128)(2,1)} %bitcast.170, bf16[1,256,256]{1,2,0:T(8,128)(2,1)S(1)} %maximum_bitcast_fusion.9, bf16[1,256,256]{1,2,0:T(8,128)(2,1)S(1)} %bitcast.196), kind=kOutput, calls=%fused_computation.12 | convolution fusion | flops 1073872896 | bytes 8650752 | tf_op jit(solution)/shard_map/prc,pck->rk/dot_general | solution.py:66
  198.8 0.6 add_convert_fusion
  199.7 22.9 %all_to_all.45 = bf16[8,512,256]{1,2,0:T(8,128)(2,1)S(1)} all-to-all(bf16[8,512,256]{1,2,0:T(8,128)(2,1)S(1)} %bitcast.181), channel_id=1, replica_groups=mesh['pair'=16,'col'=8] {'col'}, dimensions={0} | all-to-all | bytes 4194304 | tf_op jit(solution)/shard_map/all_to_all | solution.py:60
  223.2 2.4 fusion.20
  225.5 1.5 copy.54
  227.1 3.6 %all-to-all-start.6 = ((bf16[8,512,256]{1,2,0:T(8,128)(2,1)}), bf16[8,512,256]{1,2,0:T(8,128)(2,1)S(1)}, u32[]{:S(2)}, u32[]{:S(2)}) async-start(bf16[8,512,256]{1,2,0:T(8,128)(2,1)} %bitcast.175), calls=%async_computation.6 | async-start | bytes 4194304 | tf_op jit(solution)/shard_map/all_to_all | solution.py:60
  230.8 0.6 fusion.133
  231.4 2.0 fusion.113
  233.3 2.0 fusion.114
  235.3 12.0 %all-to-all-done.6 = bf16[8,512,256]{1,2,0:T(8,128)(2,1)S(1)} async-done(((bf16[8,512,256]{1,2,0:T(8,128)(2,1)}), bf16[8,512,256]{1,2,0:T(8,128)(2,1)S(1)}, u32[]{:S(2)}, u32[]{:S(2)}) %all-to-all-start.6) | async-done | bytes 2097184 | tf_op jit(solution)/shard_map/all_to_all | solution.py:60
  247.3 0.4 reduce_sum.99
  247.7 3.3 %collective-permute-start.6 = (bf16[512,128]{0,1:T(8,128)(2,1)S(1)}, bf16[512,128]{0,1:T(8,128)(2,1)S(1)}, u32[]{:S(2)}, u32[]{:S(2)}) collective-permute-start(bf16[512,128]{0,1:T(8,128)(2,1)S(1)} %pad_maximum_fusion), channel_id=1, source_target_pairs={{0,32},{8,40},{16,48},{24,56},{32,0},{40,8},{48,16},{56,24},{64,96... | collective-permute-start | bytes 393224 | tf_op jit(solution)/shard_map/ppermute | solution.py:16
  251.0 2.0 fusion.115
  253.1 2.1 fusion.116
  255.1 2.3 fusion.39
  257.5 0.7 fusion.38
  259.0 14.7 %all_to_all.46 = bf16[8,256,128]{1,2,0:T(8,128)(2,1)S(1)} all-to-all(bf16[8,256,128]{1,2,0:T(8,128)(2,1)S(1)} %fusion.44), channel_id=1, replica_groups=mesh['pair'=16,'col'=8] {'col'}, dimensions={0} | all-to-all | bytes 1048576 | tf_op jit(solution)/shard_map/all_to_all | solution.py:60
  273.7 0.8 copy.25
  (70 shorter events, 3.2 us)
Async XLA Ops:
  43.7 7.8 %collective-permute-start = (bf16[256,256]{0,1:T(8,128)(2,1)S(1)}, bf16[256,256]{0,1:T(8,128)(2,1)S(1)}, u32[]{:S(2)}, u32[]{:S(2)}) collective-permute-start(bf16[256,256]{0,1:T(8,128)(2,1)S(1)} %get-tuple-element.27), channel_id=1, source_target_pairs={{0,32},{8,40},{16,48},{24,56},{32,0},{40,8},{48,16},{56,24},{64,96... | collective-permute-start | bytes 393224 | tf_op jit(solution)/shard_map/ppermute | solution.py:16
  46.8 8.2 %collective-permute-start.1 = (bf16[256,256]{0,1:T(8,128)(2,1)S(1)}, bf16[256,256]{0,1:T(8,128)(2,1)S(1)}, u32[]{:S(2)}, u32[]{:S(2)}) collective-permute-start(bf16[256,256]{0,1:T(8,128)(2,1)S(1)} %get-tuple-element.26), channel_id=1, source_target_pairs={{0,32},{8,40},{16,48},{24,56},{32,0},{40,8},{48,16},{56,24},{64,96... | collective-permute-start | bytes 393224 | tf_op jit(solution)/shard_map/ppermute | solution.py:16
  58.5 29.5 %slice-start = ((s8[8388608]{0:T(1024)(128)(4,1)}), s8[4194304]{0:T(1024)(128)(4,1)S(1)}, s32[]{:S(2)}) async-start(s8[8388608]{0:T(1024)(128)(4,1)} %bitcast.201), calls=%async_computation.8 | async-start | bytes 8388608
  59.2 28.8 %slice-start.1 = ((s8[8388608]{0:T(1024)(128)(4,1)}), s8[4194304]{0:T(1024)(128)(4,1)S(1)}, s32[]{:S(2)}) async-start(s8[8388608]{0:T(1024)(128)(4,1)} %bitcast.201), calls=%async_computation.9 | async-start | bytes 8388608
  118.0 6.6 %collective-permute-start.2 = (bf16[256,256]{0,1:T(8,128)(2,1)S(1)}, bf16[256,256]{0,1:T(8,128)(2,1)S(1)}, u32[]{:S(2)}, u32[]{:S(2)}) collective-permute-start(bf16[256,256]{0,1:T(8,128)(2,1)S(1)} %get-tuple-element.23), channel_id=1, source_target_pairs={{0,32},{8,40},{16,48},{24,56},{32,0},{40,8},{48,16},{56,24},{64,96... | collective-permute-start | bytes 393224 | tf_op jit(solution)/shard_map/ppermute | solution.py:16
  120.8 7.2 %collective-permute-start.3 = (bf16[256,256]{0,1:T(8,128)(2,1)S(1)}, bf16[256,256]{0,1:T(8,128)(2,1)S(1)}, u32[]{:S(2)}, u32[]{:S(2)}) collective-permute-start(bf16[256,256]{0,1:T(8,128)(2,1)S(1)} %get-tuple-element.22), channel_id=1, source_target_pairs={{0,32},{8,40},{16,48},{24,56},{32,0},{40,8},{48,16},{56,24},{64,96... | collective-permute-start | bytes 393224 | tf_op jit(solution)/shard_map/ppermute | solution.py:16
  131.6 26.5 %slice-start.2 = ((s8[8388608]{0:T(1024)(128)(4,1)}), s8[4194304]{0:T(1024)(128)(4,1)S(1)}, s32[]{:S(2)}) async-start(s8[8388608]{0:T(1024)(128)(4,1)} %bitcast.203), calls=%async_computation.10 | async-start | bytes 8388608
  132.2 25.9 %slice-start.3 = ((s8[8388608]{0:T(1024)(128)(4,1)}), s8[4194304]{0:T(1024)(128)(4,1)S(1)}, s32[]{:S(2)}) async-start(s8[8388608]{0:T(1024)(128)(4,1)} %bitcast.203), calls=%async_computation.11 | async-start | bytes 8388608
  185.2 6.6 %collective-permute-start.4 = (bf16[256,256]{0,1:T(8,128)(2,1)S(1)}, bf16[256,256]{0,1:T(8,128)(2,1)S(1)}, u32[]{:S(2)}, u32[]{:S(2)}) collective-permute-start(bf16[256,256]{0,1:T(8,128)(2,1)S(1)} %get-tuple-element.19), channel_id=1, source_target_pairs={{0,32},{8,40},{16,48},{24,56},{32,0},{40,8},{48,16},{56,24},{64,96... | collective-permute-start | bytes 393224 | tf_op jit(solution)/shard_map/ppermute | solution.py:16
  188.5 6.8 %collective-permute-start.5 = (bf16[256,256]{0,1:T(8,128)(2,1)S(1)}, bf16[256,256]{0,1:T(8,128)(2,1)S(1)}, u32[]{:S(2)}, u32[]{:S(2)}) collective-permute-start(bf16[256,256]{0,1:T(8,128)(2,1)S(1)} %get-tuple-element.18), channel_id=1, source_target_pairs={{0,32},{8,40},{16,48},{24,56},{32,0},{40,8},{48,16},{56,24},{64,96... | collective-permute-start | bytes 393224 | tf_op jit(solution)/shard_map/ppermute | solution.py:16
  198.8 24.3 %slice-start.4 = ((s8[8388608]{0:T(1024)(128)(4,1)}), s8[4194304]{0:T(1024)(128)(4,1)S(1)}, s32[]{:S(2)}) async-start(s8[8388608]{0:T(1024)(128)(4,1)} %bitcast.205), calls=%async_computation.12 | async-start | bytes 8388608
  199.4 23.7 %slice-start.5 = ((s8[8388608]{0:T(1024)(128)(4,1)}), s8[4194304]{0:T(1024)(128)(4,1)S(1)}, s32[]{:S(2)}) async-start(s8[8388608]{0:T(1024)(128)(4,1)} %bitcast.205), calls=%async_computation.13 | async-start | bytes 8388608
  225.5 5.2 %copy-start.1 = (s32[16,3]{0,1:T(4,128)S(1)}, s32[16,3]{0,1:T(4,128)}, u32[]{:S(2)}) copy-start(s32[16,3]{0,1:T(4,128)} %param.9) | copy-start | bytes 580
  227.1 20.2 %all-to-all-start.6 = ((bf16[8,512,256]{1,2,0:T(8,128)(2,1)}), bf16[8,512,256]{1,2,0:T(8,128)(2,1)S(1)}, u32[]{:S(2)}, u32[]{:S(2)}) async-start(bf16[8,512,256]{1,2,0:T(8,128)(2,1)} %bitcast.175), calls=%async_computation.6 | async-start | bytes 4194304 | tf_op jit(solution)/shard_map/all_to_all | solution.py:60
  247.7 9.8 %copy-start = (bf16[2,2048,512]{2,1,0:T(8,128)(2,1)S(1)}, bf16[2,2048,512]{2,1,0:T(8,128)(2,1)}, u32[]{:S(2)}) copy-start(bf16[2,2048,512]{2,1,0:T(8,128)(2,1)} %param.8) | copy-start | bytes 12582916
  247.7 7.4 %collective-permute-start.6 = (bf16[512,128]{0,1:T(8,128)(2,1)S(1)}, bf16[512,128]{0,1:T(8,128)(2,1)S(1)}, u32[]{:S(2)}, u32[]{:S(2)}) collective-permute-start(bf16[512,128]{0,1:T(8,128)(2,1)S(1)} %pad_maximum_fusion), channel_id=1, source_target_pairs={{0,32},{8,40},{16,48},{24,56},{32,0},{40,8},{48,16},{56,24},{64,96... | collective-permute-start | bytes 393224 | tf_op jit(solution)/shard_map/ppermute | solution.py:16

commit v6 on v5

--- a/solution.py
+++ b/solution.py
@@ -93,7 +93,7 @@
     half_width = full_width // 2
     coeffs = col_sum(product(own_matrix, own_incident)).astype(jnp.bfloat16)
     for _ in range(ITERS):
-        half_rows = coeffs.shape[0] // 2
+        half_rows = coeffs.shape[0] // 4
         first_part = partner(coeffs[:half_rows], "pair", LEVEL)
         second_part = partner(coeffs[half_rows:], "pair", LEVEL)
         summed = col_sum(split_product(own_coupling, [first_part, second_part]))
@@ -102,14 +102,10 @@
     incoming = partner(pick_half(coeffs, 1 - column_half, half_width), "pair", LEVEL)
     own_half = pick_half(coeffs, column_half, half_width)
     total_rows = farfield.shape[1]
-    both = jnp.concatenate([own_half, incoming], axis=1)
-    both_turned = jnp.concatenate([turned_block(own_half), turned_block(incoming)], axis=1)
-    field = jnp.dot(farfield[0], both, preferred_element_type=jnp.float32) + jnp.dot(
-        farfield[1], both_turned, preferred_element_type=jnp.float32
-    )
-    width = own_half.shape[1]
-    merged = rotate(field[:, :width], direction_phase(own_centre, total_rows, total_rows)) + rotate(
-        field[:, width:], direction_phase(other_centre, total_rows, total_rows)
+    own_field = product(farfield, own_half)
+    other_field = product(farfield, incoming)
+    merged = rotate(own_field, direction_phase(own_centre, total_rows, total_rows)) + rotate(
+        other_field, direction_phase(other_centre, total_rows, total_rows)
     )
     amplitude = col_sum(merged)
     return amplitude[None]

time: 275 us -> 281 us (1.022); the launches traced: 274 us -> 277 us
  blocking collectives: 178 us -> 182 us
    dot_general x10 -> x12, matrix products: 33.7 us -> 39 us  [product(): jnp.einsum('prc,pck->rk', matrix, stacked, preferred_element_type=jnp.flo...]
    all_to_all x7, blocking collectives: 178 us -> 182 us  [col_sum(): received = lax.all_to_all(blocks, 'col', 0, 0)]
    all_to_all x1, waiting for transfers between devices: 12 us -> 8.05 us  [col_sum(): received = lax.all_to_all(blocks, 'col', 0, 0)]
    dot_general x2 -> x0, matrix products: 3.09 us -> none  [the longest x1 2.34 us: on_device(): jnp.dot(farfield[1], both_turned, preferred_element_type=jnp.float32)]
  transfers between devices with their start and end apart: 8 -> 8, of which waited for: 4 -> 8; matrix products, arithmetic and copies ran while one was open for 7% -> 7% of each run, Pallas kernels for 0% -> 0%
where the time goes in v6:
time: 281 us; the launch traced here: 277 us
  blocking collectives  182 us (65%)
  matrix products  39 us (14%)
  waiting for transfers between devices  19.4 us (7%)
  starting transfers between devices  16.4 us (6%)
  other arithmetic  14 us (5%)
  local copies, waits for them, and re-layouts  5.37 us (2%)
    all_to_all x7, blocking collectives, col_sum(): received = lax.all_to_all(blocks, 'col', 0, 0)  182 us
    dot_general x12, matrix products, product(): jnp.einsum('prc,pck->rk', matrix, stacked, preferred_element_type=jnp.flo...  39 us
    ppermute x7, starting transfers between devices, partner(): return lax.ppermute(value, axis, pairs)  12.8 us
    ppermute x7, waiting for transfers between devices, partner(): return lax.ppermute(value, axis, pairs)  11.3 us
    all_to_all x1, waiting for transfers between devices, col_sum(): received = lax.all_to_all(blocks, 'col', 0, 0)  8.05 us
  transfers between devices with their start and end apart: 8, of which 8 were waited for; matrix products, arithmetic and copies ran while one was open for 7% of the time, Pallas kernels for 0%

profile of v6, /device:TPU:0, one launch (start us, length us, event | category | flops | bytes accessed | tf_op | source)
XLA Modules:
  0.0 277.0 jit_solution(8640461671565461111)
XLA Ops:
  0.0 1.1 copy.9
  1.2 5.8 %fusion.29 = bf16[256,4096]{1,0:T(8,128)(2,1)S(1)} fusion(bf16[1,2,4096,512]{3,2,1,0:T(8,128)(2,1)} %param.5, bf16[1,512,256]{1,2,0:T(8,128)(2,1)S(1)} %maximum_bitcast_fusion, bf16[1,512,256]{1,2,0:T(8,128)(2,1)S(1)} %copy.9), kind=kOutput, calls=%fused_computation.21 | convolution fusion | flops 2148794368 | bytes 11010048 | tf_op jit(solution)/shard_map/prc,pck->rk/dot_general | solution.py:66
  7.1 36.2 %all_to_all.40 = bf16[8,512,256]{1,2,0:T(8,128)(2,1)S(1)} all-to-all(bf16[8,512,256]{1,2,0:T(8,128)(2,1)S(1)} %bitcast.179), channel_id=1, replica_groups=mesh['pair'=16,'col'=8] {'col'}, dimensions={0} | all-to-all | bytes 4194304 | tf_op jit(solution)/shard_map/all_to_all | solution.py:60
  43.3 0.4 reduce_sum.90
  43.7 3.1 %collective-permute-start = (bf16[128,256]{0,1:T(8,128)(2,1)S(1)}, bf16[128,256]{0,1:T(8,128)(2,1)S(1)}, u32[]{:S(2)}, u32[]{:S(2)}) collective-permute-start(bf16[128,256]{0,1:T(8,128)(2,1)S(1)} %slice.172), channel_id=1, source_target_pairs={{0,32},{8,40},{16,48},{24,56},{32,0},{40,8},{48,16},{56,24},{64,96... | collective-permute-start | bytes 196616 | tf_op jit(solution)/shard_map/ppermute | solution.py:16
  46.9 0.6 collective-permute-start.1
  47.4 2.8 %collective-permute-done = bf16[128,256]{0,1:T(8,128)(2,1)S(1)} collective-permute-done((bf16[128,256]{0,1:T(8,128)(2,1)S(1)}, bf16[128,256]{0,1:T(8,128)(2,1)S(1)}, u32[]{:S(2)}, u32[]{:S(2)}) %collective-permute-start) | collective-permute-done | bytes 65568 | tf_op jit(solution)/shard_map/ppermute | solution.py:16
  50.3 2.3 convolution_bitcast_fusion.5
  52.6 1.5 collective-permute-done.1
  54.2 4.6 %convolution_bitcast_fusion.4 = f32[4096,256]{0,1:T(8,128)S(1)} fusion(bf16[2,4096,512]{2,1,0:T(8,128)(2,1)} %bitcast.186, bf16[1,384,256]{1,2,0:T(8,128)(2,1)S(1)} %maximum_bitcast_fusion.4, bf16[1,384,256]{1,2,0:T(8,128)(2,1)S(1)} %bitcast.208), kind=kOutput, calls=%fused_computation.16 | convolution fusion | flops 1610809344 | bytes 10878976 | tf_op jit(solution)/shard_map/prc,pck->rk/dot_general | solution.py:66
  58.8 0.6 add_convert_fusion.2
  59.6 29.0 %all_to_all.41 = bf16[8,512,256]{1,2,0:T(8,128)(2,1)S(1)} all-to-all(bf16[8,512,256]{1,2,0:T(8,128)(2,1)S(1)} %bitcast.180), channel_id=1, replica_groups=mesh['pair'=16,'col'=8] {'col'}, dimensions={0} | all-to-all | bytes 4194304 | tf_op jit(solution)/shard_map/all_to_all | solution.py:60
  89.2 2.4 fusion.26
  91.8 28.3 %all_to_all.42 = bf16[8,512,256]{1,2,0:T(8,128)(2,1)S(1)} all-to-all(bf16[8,512,256]{1,2,0:T(8,128)(2,1)S(1)} %bitcast.181), channel_id=1, replica_groups=mesh['pair'=16,'col'=8] {'col'}, dimensions={0} | all-to-all | bytes 4194304 | tf_op jit(solution)/shard_map/all_to_all | solution.py:60
  120.4 1.5 collective-permute-start.2
  122.0 2.4 collective-permute-start.3
  124.3 2.0 collective-permute-done.2
  126.3 2.3 convolution_bitcast_fusion.3
  128.6 0.7 collective-permute-done.3
  129.4 4.6 %convolution_bitcast_fusion.2 = f32[4096,256]{0,1:T(8,128)S(1)} fusion(bf16[2,4096,512]{2,1,0:T(8,128)(2,1)} %bitcast.188, bf16[1,384,256]{1,2,0:T(8,128)(2,1)S(1)} %maximum_bitcast_fusion.5, bf16[1,384,256]{1,2,0:T(8,128)(2,1)S(1)} %bitcast.209), kind=kOutput, calls=%fused_computation.14 | convolution fusion | flops 1610809344 | bytes 10878976 | tf_op jit(solution)/shard_map/prc,pck->rk/dot_general | solution.py:66
  134.1 0.6 add_convert_fusion.1
  134.9 26.0 %all_to_all.43 = bf16[8,512,256]{1,2,0:T(8,128)(2,1)S(1)} all-to-all(bf16[8,512,256]{1,2,0:T(8,128)(2,1)S(1)} %bitcast.182), channel_id=1, replica_groups=mesh['pair'=16,'col'=8] {'col'}, dimensions={0} | all-to-all | bytes 4194304 | tf_op jit(solution)/shard_map/all_to_all | solution.py:60
  161.5 2.4 fusion.23
  164.0 25.1 %all_to_all.44 = bf16[8,512,256]{1,2,0:T(8,128)(2,1)S(1)} all-to-all(bf16[8,512,256]{1,2,0:T(8,128)(2,1)S(1)} %bitcast.183), channel_id=1, replica_groups=mesh['pair'=16,'col'=8] {'col'}, dimensions={0} | all-to-all | bytes 4194304 | tf_op jit(solution)/shard_map/all_to_all | solution.py:60
  189.5 2.2 collective-permute-start.4
  191.7 1.5 collective-permute-start.5
  193.2 2.1 collective-permute-done.4
  195.4 2.3 convolution_bitcast_fusion.1
  197.7 1.3 collective-permute-done.5
  199.0 4.6 %convolution_bitcast_fusion = f32[4096,256]{0,1:T(8,128)S(1)} fusion(bf16[2,4096,512]{2,1,0:T(8,128)(2,1)} %bitcast.190, bf16[1,384,256]{1,2,0:T(8,128)(2,1)S(1)} %maximum_bitcast_fusion.6, bf16[1,384,256]{1,2,0:T(8,128)(2,1)S(1)} %bitcast.210), kind=kOutput, calls=%fused_computation.12 | convolution fusion | flops 1610809344 | bytes 10878976 | tf_op jit(solution)/shard_map/prc,pck->rk/dot_general | solution.py:66
  203.7 0.6 add_convert_fusion
  204.5 23.0 %all_to_all.45 = bf16[8,512,256]{1,2,0:T(8,128)(2,1)S(1)} all-to-all(bf16[8,512,256]{1,2,0:T(8,128)(2,1)S(1)} %bitcast.184), channel_id=1, replica_groups=mesh['pair'=16,'col'=8] {'col'}, dimensions={0} | all-to-all | bytes 4194304 | tf_op jit(solution)/shard_map/all_to_all | solution.py:60
  228.1 2.4 fusion.20
  230.4 1.5 copy.48
  232.0 3.6 %all-to-all-start.6 = ((bf16[8,512,256]{1,2,0:T(8,128)(2,1)}), bf16[8,512,256]{1,2,0:T(8,128)(2,1)S(1)}, u32[]{:S(2)}, u32[]{:S(2)}) async-start(bf16[8,512,256]{1,2,0:T(8,128)(2,1)} %bitcast.178), calls=%async_computation.6 | async-start | bytes 4194304 | tf_op jit(solution)/shard_map/all_to_all | solution.py:60
  235.7 0.6 fusion.118
  236.3 2.1 fusion.101
  238.4 2.1 fusion.102
  240.4 1.9 fusion.103
  242.4 1.9 fusion.104
  244.3 8.1 %all-to-all-done.6 = bf16[8,512,256]{1,2,0:T(8,128)(2,1)S(1)} async-done(((bf16[8,512,256]{1,2,0:T(8,128)(2,1)}), bf16[8,512,256]{1,2,0:T(8,128)(2,1)S(1)}, u32[]{:S(2)}, u32[]{:S(2)}) %all-to-all-start.6) | async-done | bytes 2097184 | tf_op jit(solution)/shard_map/all_to_all | solution.py:60
  252.4 0.4 reduce_sum.99
  252.8 1.5 collective-permute-start.6
  254.4 3.8 %convolution_bitcast_fusion.7 = f32[2048,128]{0,1:T(8,128)S(1)} fusion(bf16[2,2048,512]{2,1,0:T(8,128)(2,1)} %param.8, bf16[1,512,128]{1,2,0:T(8,128)(2,1)S(1)} %get-tuple-element.33, bf16[1,512,128]{1,2,0:T(8,128)(2,1)S(1)} %get-tuple-element.32), kind=kOutput, calls=%fused_computation.32 | convolution fusion | flops 537001984 | bytes 5505024 | tf_op jit(solution)/shard_map/prc,pck->rk/dot_general | solution.py:66
  258.4 0.9 collective-permute-done.6
  259.4 1.5 convolution_bitcast_fusion.6
  261.4 14.8 %all_to_all.46 = bf16[8,256,128]{1,2,0:T(8,128)(2,1)S(1)} all-to-all(bf16[8,256,128]{1,2,0:T(8,128)(2,1)S(1)} %fusion.38), channel_id=1, replica_groups=mesh['pair'=16,'col'=8] {'col'}, dimensions={0} | all-to-all | bytes 1048576 | tf_op jit(solution)/shard_map/all_to_all | solution.py:60
  276.2 0.8 copy.24
  (76 shorter events, 4.7 us)
Async XLA Ops:
  43.7 6.5 %collective-permute-start = (bf16[128,256]{0,1:T(8,128)(2,1)S(1)}, bf16[128,256]{0,1:T(8,128)(2,1)S(1)}, u32[]{:S(2)}, u32[]{:S(2)}) collective-permute-start(bf16[128,256]{0,1:T(8,128)(2,1)S(1)} %slice.172), channel_id=1, source_target_pairs={{0,32},{8,40},{16,48},{24,56},{32,0},{40,8},{48,16},{56,24},{64,96... | collective-permute-start | bytes 196616 | tf_op jit(solution)/shard_map/ppermute | solution.py:16
  46.9 7.3 %collective-permute-start.1 = (bf16[384,256]{0,1:T(8,128)(2,1)S(1)}, bf16[384,256]{0,1:T(8,128)(2,1)S(1)}, u32[]{:S(2)}, u32[]{:S(2)}) collective-permute-start(bf16[384,256]{0,1:T(8,128)(2,1)S(1)} %slice.176), channel_id=1, source_target_pairs={{0,32},{8,40},{16,48},{24,56},{32,0},{40,8},{48,16},{56,24},{64,96... | collective-permute-start | bytes 589832 | tf_op jit(solution)/shard_map/ppermute | solution.py:16
  58.8 30.4 %slice-start = ((s8[8388608]{0:T(1024)(128)(4,1)}), s8[4194304]{0:T(1024)(128)(4,1)S(1)}, s32[]{:S(2)}) async-start(s8[8388608]{0:T(1024)(128)(4,1)} %bitcast.211), calls=%async_computation.8 | async-start | bytes 8388608
  59.4 29.8 %slice-start.1 = ((s8[8388608]{0:T(1024)(128)(4,1)}), s8[4194304]{0:T(1024)(128)(4,1)S(1)}, s32[]{:S(2)}) async-start(s8[8388608]{0:T(1024)(128)(4,1)} %bitcast.211), calls=%async_computation.9 | async-start | bytes 8388608
  120.4 5.8 %collective-permute-start.2 = (bf16[128,256]{0,1:T(8,128)(2,1)S(1)}, bf16[128,256]{0,1:T(8,128)(2,1)S(1)}, u32[]{:S(2)}, u32[]{:S(2)}) collective-permute-start(bf16[128,256]{0,1:T(8,128)(2,1)S(1)} %slice.182), channel_id=1, source_target_pairs={{0,32},{8,40},{16,48},{24,56},{32,0},{40,8},{48,16},{56,24},{64,96... | collective-permute-start | bytes 196616 | tf_op jit(solution)/shard_map/ppermute | solution.py:16
  122.0 7.4 %collective-permute-start.3 = (bf16[384,256]{0,1:T(8,128)(2,1)S(1)}, bf16[384,256]{0,1:T(8,128)(2,1)S(1)}, u32[]{:S(2)}, u32[]{:S(2)}) collective-permute-start(bf16[384,256]{0,1:T(8,128)(2,1)S(1)} %slice.185), channel_id=1, source_target_pairs={{0,32},{8,40},{16,48},{24,56},{32,0},{40,8},{48,16},{56,24},{64,96... | collective-permute-start | bytes 589832 | tf_op jit(solution)/shard_map/ppermute | solution.py:16
  134.1 27.4 %slice-start.2 = ((s8[8388608]{0:T(1024)(128)(4,1)}), s8[4194304]{0:T(1024)(128)(4,1)S(1)}, s32[]{:S(2)}) async-start(s8[8388608]{0:T(1024)(128)(4,1)} %bitcast.213), calls=%async_computation.10 | async-start | bytes 8388608
  134.7 26.7 %slice-start.3 = ((s8[8388608]{0:T(1024)(128)(4,1)}), s8[4194304]{0:T(1024)(128)(4,1)S(1)}, s32[]{:S(2)}) async-start(s8[8388608]{0:T(1024)(128)(4,1)} %bitcast.213), calls=%async_computation.11 | async-start | bytes 8388608
  189.5 5.8 %collective-permute-start.4 = (bf16[128,256]{0,1:T(8,128)(2,1)S(1)}, bf16[128,256]{0,1:T(8,128)(2,1)S(1)}, u32[]{:S(2)}, u32[]{:S(2)}) collective-permute-start(bf16[128,256]{0,1:T(8,128)(2,1)S(1)} %slice.190), channel_id=1, source_target_pairs={{0,32},{8,40},{16,48},{24,56},{32,0},{40,8},{48,16},{56,24},{64,96... | collective-permute-start | bytes 196616 | tf_op jit(solution)/shard_map/ppermute | solution.py:16
  191.7 7.3 %collective-permute-start.5 = (bf16[384,256]{0,1:T(8,128)(2,1)S(1)}, bf16[384,256]{0,1:T(8,128)(2,1)S(1)}, u32[]{:S(2)}, u32[]{:S(2)}) collective-permute-start(bf16[384,256]{0,1:T(8,128)(2,1)S(1)} %slice.193), channel_id=1, source_target_pairs={{0,32},{8,40},{16,48},{24,56},{32,0},{40,8},{48,16},{56,24},{64,96... | collective-permute-start | bytes 589832 | tf_op jit(solution)/shard_map/ppermute | solution.py:16
  203.7 24.4 %slice-start.4 = ((s8[8388608]{0:T(1024)(128)(4,1)}), s8[4194304]{0:T(1024)(128)(4,1)S(1)}, s32[]{:S(2)}) async-start(s8[8388608]{0:T(1024)(128)(4,1)} %bitcast.215), calls=%async_computation.12 | async-start | bytes 8388608
  204.3 23.7 %slice-start.5 = ((s8[8388608]{0:T(1024)(128)(4,1)}), s8[4194304]{0:T(1024)(128)(4,1)S(1)}, s32[]{:S(2)}) async-start(s8[8388608]{0:T(1024)(128)(4,1)} %bitcast.215), calls=%async_computation.13 | async-start | bytes 8388608
  230.4 5.1 %copy-start.1 = (s32[16,3]{0,1:T(4,128)S(1)}, s32[16,3]{0,1:T(4,128)}, u32[]{:S(2)}) copy-start(s32[16,3]{0,1:T(4,128)} %param.9) | copy-start | bytes 580
  232.0 20.4 %all-to-all-start.6 = ((bf16[8,512,256]{1,2,0:T(8,128)(2,1)}), bf16[8,512,256]{1,2,0:T(8,128)(2,1)S(1)}, u32[]{:S(2)}, u32[]{:S(2)}) async-start(bf16[8,512,256]{1,2,0:T(8,128)(2,1)} %bitcast.178), calls=%async_computation.6 | async-start | bytes 4194304 | tf_op jit(solution)/shard_map/all_to_all | solution.py:60
  252.8 6.6 %collective-permute-start.6 = (bf16[512,128]{0,1:T(8,128)(2,1)S(1)}, bf16[512,128]{0,1:T(8,128)(2,1)S(1)}, u32[]{:S(2)}, u32[]{:S(2)}) collective-permute-start(bf16[512,128]{0,1:T(8,128)(2,1)S(1)} %pad_maximum_fusion), channel_id=1, source_target_pairs={{0,32},{8,40},{16,48},{24,56},{32,0},{40,8},{48,16},{56,24},{64,96... | collective-permute-start | bytes 393224 | tf_op jit(solution)/shard_map/ppermute | solution.py:16
  254.4 5.0 %copy-start = (bf16[2,2048,512]{2,1,0:T(8,128)(2,1)S(1)}, bf16[2,2048,512]{2,1,0:T(8,128)(2,1)}, u32[]{:S(2)}) copy-start(bf16[2,2048,512]{2,1,0:T(8,128)(2,1)} %param.8) | copy-start | bytes 12582916

commit v7 on v6

--- a/solution.py
+++ b/solution.py
@@ -68,14 +68,13 @@
 
 def split_product(matrix, parts):
     total = None
-    start = 0
-    for index, piece in enumerate(parts):
+    for start, piece in parts:
         rows = piece.shape[0]
         term = product(matrix[:, :, start : start + rows], piece)
-        if index + 1 < len(parts):
-            term = lax.optimization_barrier(term)
-        total = term if total is None else total + term
-        start += rows
+        if total is None:
+            total = lax.optimization_barrier(term)
+        else:
+            total = term + total
     return total
 
 
@@ -93,17 +92,22 @@
     half_width = full_width // 2
     coeffs = col_sum(product(own_matrix, own_incident)).astype(jnp.bfloat16)
     for _ in range(ITERS):
-        half_rows = coeffs.shape[0] // 4
+        half_rows = coeffs.shape[0] // 2
         first_part = partner(coeffs[:half_rows], "pair", LEVEL)
         second_part = partner(coeffs[half_rows:], "pair", LEVEL)
-        summed = col_sum(split_product(own_coupling, [first_part, second_part]))
+        summed = col_sum(split_product(own_coupling, [(0, first_part), (half_rows, second_part)]))
         driven = (own_incident.astype(jnp.float32) + summed).astype(jnp.bfloat16)
         coeffs = col_sum(product(own_matrix, driven)).astype(jnp.bfloat16)
-    incoming = partner(pick_half(coeffs, 1 - column_half, half_width), "pair", LEVEL)
+    outgoing = pick_half(coeffs, 1 - column_half, half_width)
+    tail_rows = outgoing.shape[0] // 2
+    incoming_parts = [
+        partner(outgoing[:tail_rows], "pair", LEVEL),
+        partner(outgoing[tail_rows:], "pair", LEVEL),
+    ]
     own_half = pick_half(coeffs, column_half, half_width)
     total_rows = farfield.shape[1]
     own_field = product(farfield, own_half)
-    other_field = product(farfield, incoming)
+    other_field = split_product(farfield, [(0, incoming_parts[0]), (tail_rows, incoming_parts[1])])
     merged = rotate(own_field, direction_phase(own_centre, total_rows, total_rows)) + rotate(
         other_field, direction_phase(other_centre, total_rows, total_rows)
     )

time: 281 us -> 274 us (0.975); the launches traced: 277 us -> 273 us
  blocking collectives: 182 us -> 178 us
    all_to_all x7, blocking collectives: 182 us -> 178 us  [col_sum(): received = lax.all_to_all(blocks, 'col', 0, 0)]
    ppermute x7 -> x8, starting transfers between devices: 12.8 us -> 14.5 us  [partner(): return lax.ppermute(value, axis, pairs)]
    dot_general x12 -> x13, matrix products: 39 us -> 39.8 us  [product(): jnp.einsum('prc,pck->rk', matrix, stacked, preferred_element_type=jnp.flo...]
    ppermute x7 -> x8, waiting for transfers between devices: 11.3 us -> 11.4 us  [partner(): return lax.ppermute(value, axis, pairs)]
  transfers between devices with their start and end apart: 8 -> 9, of which waited for: 8 -> 5; matrix products, arithmetic and copies ran while one was open for 7% -> 9% of each run, Pallas kernels for 0% -> 0%
where the time goes in v7:
time: 274 us; the launch traced here: 273 us
  blocking collectives  178 us (65%)
  matrix products  39.8 us (15%)
  waiting for transfers between devices  19.1 us (7%)
  starting transfers between devices  18.1 us (7%)
  other arithmetic  12.2 us (4%)
  local copies, waits for them, and re-layouts  5.32 us (2%)
    all_to_all x7, blocking collectives, col_sum(): received = lax.all_to_all(blocks, 'col', 0, 0)  178 us
    dot_general x13, matrix products, product(): jnp.einsum('prc,pck->rk', matrix, stacked, preferred_element_type=jnp.flo...  39.8 us
    ppermute x8, starting transfers between devices, partner(): return lax.ppermute(value, axis, pairs)  14.5 us
    ppermute x8, waiting for transfers between devices, partner(): return lax.ppermute(value, axis, pairs)  11.4 us
    all_to_all x1, waiting for transfers between devices, col_sum(): received = lax.all_to_all(blocks, 'col', 0, 0)  7.67 us
  transfers between devices with their start and end apart: 9, of which 5 were waited for; matrix products, arithmetic and copies ran while one was open for 9% of the time, Pallas kernels for 0%

profile of v7, /device:TPU:0, one launch (start us, length us, event | category | flops | bytes accessed | tf_op | source)
XLA Modules:
  0.0 273.2 jit_solution(13728780981897355435)
XLA Ops:
  0.0 1.1 copy.9
  1.2 5.8 %fusion.35 = bf16[256,4096]{1,0:T(8,128)(2,1)S(1)} fusion(bf16[1,2,4096,512]{3,2,1,0:T(8,128)(2,1)} %param.5, bf16[1,512,256]{1,2,0:T(8,128)(2,1)S(1)} %maximum_bitcast_fusion, bf16[1,512,256]{1,2,0:T(8,128)(2,1)S(1)} %copy.9), kind=kOutput, calls=%fused_computation.27 | convolution fusion | flops 2148794368 | bytes 11010048 | tf_op jit(solution)/shard_map/prc,pck->rk/dot_general | solution.py:66
  7.1 36.2 %all_to_all.40 = bf16[8,512,256]{1,2,0:T(8,128)(2,1)S(1)} all-to-all(bf16[8,512,256]{1,2,0:T(8,128)(2,1)S(1)} %bitcast.202), channel_id=1, replica_groups=mesh['pair'=16,'col'=8] {'col'}, dimensions={0} | all-to-all | bytes 4194304 | tf_op jit(solution)/shard_map/all_to_all | solution.py:60
  43.3 0.4 reduce_sum.90
  43.7 3.1 %collective-permute-start.1 = (bf16[256,256]{0,1:T(8,128)(2,1)S(1)}, bf16[256,256]{0,1:T(8,128)(2,1)S(1)}, u32[]{:S(2)}, u32[]{:S(2)}) collective-permute-start(bf16[256,256]{0,1:T(8,128)(2,1)S(1)} %get-tuple-element.27), channel_id=1, source_target_pairs={{0,32},{8,40},{16,48},{24,56},{32,0},{40,8},{48,16},{56,24},{64,96... | collective-permute-start | bytes 393224 | tf_op jit(solution)/shard_map/ppermute | solution.py:16
  46.8 0.5 collective-permute-start
  47.3 4.2 %collective-permute-done.1 = bf16[256,256]{0,1:T(8,128)(2,1)S(1)} collective-permute-done((bf16[256,256]{0,1:T(8,128)(2,1)S(1)}, bf16[256,256]{0,1:T(8,128)(2,1)S(1)}, u32[]{:S(2)}, u32[]{:S(2)}) %collective-permute-start.1) | collective-permute-done | bytes 131104 | tf_op jit(solution)/shard_map/ppermute | solution.py:16
  51.5 3.5 %convolution_bitcast_fusion.4 = f32[4096,256]{0,1:T(8,128)S(1)} fusion(bf16[2,4096,512]{2,1,0:T(8,128)(2,1)} %bitcast.194, bf16[1,256,256]{1,2,0:T(8,128)(2,1)S(1)} %maximum_bitcast_fusion.5, bf16[1,256,256]{1,2,0:T(8,128)(2,1)S(1)} %bitcast.226), kind=kOutput, calls=%fused_computation.16 | convolution fusion | flops 1073872896 | bytes 8650752 | tf_op jit(solution)/shard_map/prc,pck->rk/dot_general | solution.py:66
  55.1 3.7 %fusion.25 = bf16[4096,256]{0,1:T(8,128)(2,1)S(1)} fusion(f32[4096,256]{0,1:T(8,128)S(1)} %convolution_bitcast_fusion.4, bf16[2,4096,512]{2,1,0:T(8,128)(2,1)} %bitcast.195, bf16[1,256,256]{1,2,0:T(8,128)(2,1)S(1)} %maximum_bitcast_fusion.4, bf16[1,256,256]{1,2,0:T(8,128)(2,1)S(1)} %bitcast.223), kind=kOutput, calls=%fused_computation.23 | convolution fusion | flops 1075970048 | bytes 10747904 | tf_op jit(solution)/shard_map/prc,pck->rk/dot_general | solution.py:66
  59.0 27.9 %all_to_all.41 = bf16[8,512,256]{1,2,0:T(8,128)(2,1)S(1)} all-to-all(bf16[8,512,256]{1,2,0:T(8,128)(2,1)S(1)} %bitcast.203), channel_id=1, replica_groups=mesh['pair'=16,'col'=8] {'col'}, dimensions={0} | all-to-all | bytes 4194304 | tf_op jit(solution)/shard_map/all_to_all | solution.py:60
  87.0 0.3 convert_reduce_fusion.2
  87.5 2.4 fusion.32
  90.1 26.9 %all_to_all.42 = bf16[8,512,256]{1,2,0:T(8,128)(2,1)S(1)} all-to-all(bf16[8,512,256]{1,2,0:T(8,128)(2,1)S(1)} %bitcast.204), channel_id=1, replica_groups=mesh['pair'=16,'col'=8] {'col'}, dimensions={0} | all-to-all | bytes 4194304 | tf_op jit(solution)/shard_map/all_to_all | solution.py:60
  117.0 0.4 reduce_sum.93
  117.4 3.0 %collective-permute-start.3 = (bf16[256,256]{0,1:T(8,128)(2,1)S(1)}, bf16[256,256]{0,1:T(8,128)(2,1)S(1)}, u32[]{:S(2)}, u32[]{:S(2)}) collective-permute-start(bf16[256,256]{0,1:T(8,128)(2,1)S(1)} %get-tuple-element.23), channel_id=1, source_target_pairs={{0,32},{8,40},{16,48},{24,56},{32,0},{40,8},{48,16},{56,24},{64,96... | collective-permute-start | bytes 393224 | tf_op jit(solution)/shard_map/ppermute | solution.py:16
  120.4 0.6 collective-permute-start.2
  121.0 2.9 %collective-permute-done.3 = bf16[256,256]{0,1:T(8,128)(2,1)S(1)} collective-permute-done((bf16[256,256]{0,1:T(8,128)(2,1)S(1)}, bf16[256,256]{0,1:T(8,128)(2,1)S(1)}, u32[]{:S(2)}, u32[]{:S(2)}) %collective-permute-start.3) | collective-permute-done | bytes 131104 | tf_op jit(solution)/shard_map/ppermute | solution.py:16
  124.0 3.5 %convolution_bitcast_fusion.2 = f32[4096,256]{0,1:T(8,128)S(1)} fusion(bf16[2,4096,512]{2,1,0:T(8,128)(2,1)} %bitcast.196, bf16[1,256,256]{1,2,0:T(8,128)(2,1)S(1)} %maximum_bitcast_fusion.7, bf16[1,256,256]{1,2,0:T(8,128)(2,1)S(1)} %bitcast.227), kind=kOutput, calls=%fused_computation.14 | convolution fusion | flops 1073872896 | bytes 8650752 | tf_op jit(solution)/shard_map/prc,pck->rk/dot_general | solution.py:66
  127.5 3.7 %fusion.24 = bf16[4096,256]{0,1:T(8,128)(2,1)S(1)} fusion(f32[4096,256]{0,1:T(8,128)S(1)} %convolution_bitcast_fusion.2, bf16[2,4096,512]{2,1,0:T(8,128)(2,1)} %bitcast.197, bf16[1,256,256]{1,2,0:T(8,128)(2,1)S(1)} %maximum_bitcast_fusion.6, bf16[1,256,256]{1,2,0:T(8,128)(2,1)S(1)} %bitcast.224), kind=kOutput, calls=%fused_computation.22 | convolution fusion | flops 1075970048 | bytes 10747904 | tf_op jit(solution)/shard_map/prc,pck->rk/dot_general | solution.py:66
  131.5 25.2 %all_to_all.43 = bf16[8,512,256]{1,2,0:T(8,128)(2,1)S(1)} all-to-all(bf16[8,512,256]{1,2,0:T(8,128)(2,1)S(1)} %bitcast.205), channel_id=1, replica_groups=mesh['pair'=16,'col'=8] {'col'}, dimensions={0} | all-to-all | bytes 4194304 | tf_op jit(solution)/shard_map/all_to_all | solution.py:60
  156.7 0.3 convert_reduce_fusion.1
  157.2 2.4 fusion.29
  159.8 24.1 %all_to_all.44 = bf16[8,512,256]{1,2,0:T(8,128)(2,1)S(1)} all-to-all(bf16[8,512,256]{1,2,0:T(8,128)(2,1)S(1)} %bitcast.206), channel_id=1, replica_groups=mesh['pair'=16,'col'=8] {'col'}, dimensions={0} | all-to-all | bytes 4194304 | tf_op jit(solution)/shard_map/all_to_all | solution.py:60
  183.9 0.4 reduce_sum.96
  184.3 3.3 %collective-permute-start.5 = (bf16[256,256]{0,1:T(8,128)(2,1)S(1)}, bf16[256,256]{0,1:T(8,128)(2,1)S(1)}, u32[]{:S(2)}, u32[]{:S(2)}) collective-permute-start(bf16[256,256]{0,1:T(8,128)(2,1)S(1)} %get-tuple-element.19), channel_id=1, source_target_pairs={{0,32},{8,40},{16,48},{24,56},{32,0},{40,8},{48,16},{56,24},{64,96... | collective-permute-start | bytes 393224 | tf_op jit(solution)/shard_map/ppermute | solution.py:16
  187.9 2.9 %collective-permute-done.5 = bf16[256,256]{0,1:T(8,128)(2,1)S(1)} collective-permute-done((bf16[256,256]{0,1:T(8,128)(2,1)S(1)}, bf16[256,256]{0,1:T(8,128)(2,1)S(1)}, u32[]{:S(2)}, u32[]{:S(2)}) %collective-permute-start.5) | collective-permute-done | bytes 131104 | tf_op jit(solution)/shard_map/ppermute | solution.py:16
  190.9 3.5 %convolution_bitcast_fusion = f32[4096,256]{0,1:T(8,128)S(1)} fusion(bf16[2,4096,512]{2,1,0:T(8,128)(2,1)} %bitcast.198, bf16[1,256,256]{1,2,0:T(8,128)(2,1)S(1)} %maximum_bitcast_fusion.9, bf16[1,256,256]{1,2,0:T(8,128)(2,1)S(1)} %bitcast.228), kind=kOutput, calls=%fused_computation.12 | convolution fusion | flops 1073872896 | bytes 8650752 | tf_op jit(solution)/shard_map/prc,pck->rk/dot_general | solution.py:66
  194.4 3.7 %fusion.23 = bf16[4096,256]{0,1:T(8,128)(2,1)S(1)} fusion(f32[4096,256]{0,1:T(8,128)S(1)} %convolution_bitcast_fusion, bf16[2,4096,512]{2,1,0:T(8,128)(2,1)} %bitcast.199, bf16[1,256,256]{1,2,0:T(8,128)(2,1)S(1)} %maximum_bitcast_fusion.8, bf16[1,256,256]{1,2,0:T(8,128)(2,1)S(1)} %bitcast.225), kind=kOutput, calls=%fused_computation.21 | convolution fusion | flops 1075970048 | bytes 10747904 | tf_op jit(solution)/shard_map/prc,pck->rk/dot_general | solution.py:66
  198.4 22.9 %all_to_all.45 = bf16[8,512,256]{1,2,0:T(8,128)(2,1)S(1)} all-to-all(bf16[8,512,256]{1,2,0:T(8,128)(2,1)S(1)} %bitcast.207), channel_id=1, replica_groups=mesh['pair'=16,'col'=8] {'col'}, dimensions={0} | all-to-all | bytes 4194304 | tf_op jit(solution)/shard_map/all_to_all | solution.py:60
  221.3 0.3 convert_reduce_fusion
  221.9 2.4 fusion.26
  224.3 1.5 copy.48
  225.8 3.6 %all-to-all-start.6 = ((bf16[8,512,256]{1,2,0:T(8,128)(2,1)}), bf16[8,512,256]{1,2,0:T(8,128)(2,1)S(1)}, u32[]{:S(2)}, u32[]{:S(2)}) async-start(bf16[8,512,256]{1,2,0:T(8,128)(2,1)} %bitcast.201), calls=%async_computation.6 | async-start | bytes 4194304 | tf_op jit(solution)/shard_map/all_to_all | solution.py:60
  229.5 0.6 fusion.135
  230.1 2.0 fusion.114
  232.1 2.0 fusion.115
  234.1 2.1 fusion.116
  236.2 2.1 fusion.117
  238.3 7.7 %all-to-all-done.6 = bf16[8,512,256]{1,2,0:T(8,128)(2,1)S(1)} async-done(((bf16[8,512,256]{1,2,0:T(8,128)(2,1)}), bf16[8,512,256]{1,2,0:T(8,128)(2,1)S(1)}, u32[]{:S(2)}, u32[]{:S(2)}) %all-to-all-start.6) | async-done | bytes 2097184 | tf_op jit(solution)/shard_map/all_to_all | solution.py:60
  246.0 0.4 reduce_sum.99
  246.4 3.3 %collective-permute-start.6 = (bf16[256,128]{0,1:T(8,128)(2,1)S(1)}, bf16[256,128]{0,1:T(8,128)(2,1)S(1)}, u32[]{:S(2)}, u32[]{:S(2)}) collective-permute-start(bf16[256,128]{0,1:T(8,128)(2,1)S(1)} %get-tuple-element.30), channel_id=1, source_target_pairs={{0,32},{8,40},{16,48},{24,56},{32,0},{40,8},{48,16},{56,24},{64,96... | collective-permute-start | bytes 196616 | tf_op jit(solution)/shard_map/ppermute | solution.py:16
  249.7 0.3 collective-permute-start.7
  250.1 3.8 %convolution_bitcast_fusion.6 = f32[2048,128]{0,1:T(8,128)S(1)} fusion(bf16[2,2048,512]{2,1,0:T(8,128)(2,1)} %param.8, bf16[1,512,128]{1,2,0:T(8,128)(2,1)S(1)} %get-tuple-element.49, bf16[1,512,128]{1,2,0:T(8,128)(2,1)S(1)} %get-tuple-element.48), kind=kOutput, calls=%fused_computation.37 | convolution fusion | flops 537001984 | bytes 5505024 | tf_op jit(solution)/shard_map/prc,pck->rk/dot_general | solution.py:66
  254.1 1.4 collective-permute-done.7
  255.5 0.8 convolution_bitcast_fusion.7
  256.4 0.8 fusion.44
  257.7 14.7 %all_to_all.46 = bf16[8,256,128]{1,2,0:T(8,128)(2,1)S(1)} all-to-all(bf16[8,256,128]{1,2,0:T(8,128)(2,1)S(1)} %fusion.47), channel_id=1, replica_groups=mesh['pair'=16,'col'=8] {'col'}, dimensions={0} | all-to-all | bytes 1048576 | tf_op jit(solution)/shard_map/all_to_all | solution.py:60
  272.4 0.8 copy.24
  (75 shorter events, 3.2 us)
Async XLA Ops:
  43.7 7.8 %collective-permute-start.1 = (bf16[256,256]{0,1:T(8,128)(2,1)S(1)}, bf16[256,256]{0,1:T(8,128)(2,1)S(1)}, u32[]{:S(2)}, u32[]{:S(2)}) collective-permute-start(bf16[256,256]{0,1:T(8,128)(2,1)S(1)} %get-tuple-element.27), channel_id=1, source_target_pairs={{0,32},{8,40},{16,48},{24,56},{32,0},{40,8},{48,16},{56,24},{64,96... | collective-permute-start | bytes 393224 | tf_op jit(solution)/shard_map/ppermute | solution.py:16
  46.8 8.2 %collective-permute-start = (bf16[256,256]{0,1:T(8,128)(2,1)S(1)}, bf16[256,256]{0,1:T(8,128)(2,1)S(1)}, u32[]{:S(2)}, u32[]{:S(2)}) collective-permute-start(bf16[256,256]{0,1:T(8,128)(2,1)S(1)} %get-tuple-element.26), channel_id=1, source_target_pairs={{0,32},{8,40},{16,48},{24,56},{32,0},{40,8},{48,16},{56,24},{64,96... | collective-permute-start | bytes 393224 | tf_op jit(solution)/shard_map/ppermute | solution.py:16
  55.1 32.4 %slice-start = ((s8[8388608]{0:T(1024)(128)(4,1)}), s8[4194304]{0:T(1024)(128)(4,1)S(1)}, s32[]{:S(2)}) async-start(s8[8388608]{0:T(1024)(128)(4,1)} %bitcast.232), calls=%async_computation.8 | async-start | bytes 8388608
  58.8 28.7 %slice-start.1 = ((s8[8388608]{0:T(1024)(128)(4,1)}), s8[4194304]{0:T(1024)(128)(4,1)S(1)}, s32[]{:S(2)}) async-start(s8[8388608]{0:T(1024)(128)(4,1)} %bitcast.232), calls=%async_computation.9 | async-start | bytes 8388608
  117.4 6.6 %collective-permute-start.3 = (bf16[256,256]{0,1:T(8,128)(2,1)S(1)}, bf16[256,256]{0,1:T(8,128)(2,1)S(1)}, u32[]{:S(2)}, u32[]{:S(2)}) collective-permute-start(bf16[256,256]{0,1:T(8,128)(2,1)S(1)} %get-tuple-element.23), channel_id=1, source_target_pairs={{0,32},{8,40},{16,48},{24,56},{32,0},{40,8},{48,16},{56,24},{64,96... | collective-permute-start | bytes 393224 | tf_op jit(solution)/shard_map/ppermute | solution.py:16
  120.4 7.1 %collective-permute-start.2 = (bf16[256,256]{0,1:T(8,128)(2,1)S(1)}, bf16[256,256]{0,1:T(8,128)(2,1)S(1)}, u32[]{:S(2)}, u32[]{:S(2)}) collective-permute-start(bf16[256,256]{0,1:T(8,128)(2,1)S(1)} %get-tuple-element.22), channel_id=1, source_target_pairs={{0,32},{8,40},{16,48},{24,56},{32,0},{40,8},{48,16},{56,24},{64,96... | collective-permute-start | bytes 393224 | tf_op jit(solution)/shard_map/ppermute | solution.py:16
  127.5 29.7 %slice-start.2 = ((s8[8388608]{0:T(1024)(128)(4,1)}), s8[4194304]{0:T(1024)(128)(4,1)S(1)}, s32[]{:S(2)}) async-start(s8[8388608]{0:T(1024)(128)(4,1)} %bitcast.234), calls=%async_computation.10 | async-start | bytes 8388608
  131.2 26.0 %slice-start.3 = ((s8[8388608]{0:T(1024)(128)(4,1)}), s8[4194304]{0:T(1024)(128)(4,1)S(1)}, s32[]{:S(2)}) async-start(s8[8388608]{0:T(1024)(128)(4,1)} %bitcast.234), calls=%async_computation.11 | async-start | bytes 8388608
  184.3 6.6 %collective-permute-start.5 = (bf16[256,256]{0,1:T(8,128)(2,1)S(1)}, bf16[256,256]{0,1:T(8,128)(2,1)S(1)}, u32[]{:S(2)}, u32[]{:S(2)}) collective-permute-start(bf16[256,256]{0,1:T(8,128)(2,1)S(1)} %get-tuple-element.19), channel_id=1, source_target_pairs={{0,32},{8,40},{16,48},{24,56},{32,0},{40,8},{48,16},{56,24},{64,96... | collective-permute-start | bytes 393224 | tf_op jit(solution)/shard_map/ppermute | solution.py:16
  187.6 6.7 %collective-permute-start.4 = (bf16[256,256]{0,1:T(8,128)(2,1)S(1)}, bf16[256,256]{0,1:T(8,128)(2,1)S(1)}, u32[]{:S(2)}, u32[]{:S(2)}) collective-permute-start(bf16[256,256]{0,1:T(8,128)(2,1)S(1)} %get-tuple-element.18), channel_id=1, source_target_pairs={{0,32},{8,40},{16,48},{24,56},{32,0},{40,8},{48,16},{56,24},{64,96... | collective-permute-start | bytes 393224 | tf_op jit(solution)/shard_map/ppermute | solution.py:16
  194.4 27.4 %slice-start.4 = ((s8[8388608]{0:T(1024)(128)(4,1)}), s8[4194304]{0:T(1024)(128)(4,1)S(1)}, s32[]{:S(2)}) async-start(s8[8388608]{0:T(1024)(128)(4,1)} %bitcast.236), calls=%async_computation.12 | async-start | bytes 8388608
  198.2 23.7 %slice-start.5 = ((s8[8388608]{0:T(1024)(128)(4,1)}), s8[4194304]{0:T(1024)(128)(4,1)S(1)}, s32[]{:S(2)}) async-start(s8[8388608]{0:T(1024)(128)(4,1)} %bitcast.236), calls=%async_computation.13 | async-start | bytes 8388608
  224.3 5.1 %copy-start.1 = (s32[16,3]{0,1:T(4,128)S(1)}, s32[16,3]{0,1:T(4,128)}, u32[]{:S(2)}) copy-start(s32[16,3]{0,1:T(4,128)} %param.9) | copy-start | bytes 580
  225.8 20.2 %all-to-all-start.6 = ((bf16[8,512,256]{1,2,0:T(8,128)(2,1)}), bf16[8,512,256]{1,2,0:T(8,128)(2,1)S(1)}, u32[]{:S(2)}, u32[]{:S(2)}) async-start(bf16[8,512,256]{1,2,0:T(8,128)(2,1)} %bitcast.201), calls=%async_computation.6 | async-start | bytes 4194304 | tf_op jit(solution)/shard_map/all_to_all | solution.py:60
  246.4 9.9 %collective-permute-start.6 = (bf16[256,128]{0,1:T(8,128)(2,1)S(1)}, bf16[256,128]{0,1:T(8,128)(2,1)S(1)}, u32[]{:S(2)}, u32[]{:S(2)}) collective-permute-start(bf16[256,128]{0,1:T(8,128)(2,1)S(1)} %get-tuple-element.30), channel_id=1, source_target_pairs={{0,32},{8,40},{16,48},{24,56},{32,0},{40,8},{48,16},{56,24},{64,96... | collective-permute-start | bytes 196616 | tf_op jit(solution)/shard_map/ppermute | solution.py:16
  249.7 5.8 %collective-permute-start.7 = (bf16[256,128]{0,1:T(8,128)(2,1)S(1)}, bf16[256,128]{0,1:T(8,128)(2,1)S(1)}, u32[]{:S(2)}, u32[]{:S(2)}) collective-permute-start(bf16[256,128]{0,1:T(8,128)(2,1)S(1)} %get-tuple-element.31), channel_id=1, source_target_pairs={{0,32},{8,40},{16,48},{24,56},{32,0},{40,8},{48,16},{56,24},{64,96... | collective-permute-start | bytes 196616 | tf_op jit(solution)/shard_map/ppermute | solution.py:16
  250.1 5.5 %copy-start = (bf16[2,2048,512]{2,1,0:T(8,128)(2,1)S(1)}, bf16[2,2048,512]{2,1,0:T(8,128)(2,1)}, u32[]{:S(2)}) copy-start(bf16[2,2048,512]{2,1,0:T(8,128)(2,1)} %param.8) | copy-start | bytes 12582916

commit v8 on v7

--- a/solution.py
+++ b/solution.py
@@ -92,22 +92,17 @@
     half_width = full_width // 2
     coeffs = col_sum(product(own_matrix, own_incident)).astype(jnp.bfloat16)
     for _ in range(ITERS):
-        half_rows = coeffs.shape[0] // 2
+        half_rows = coeffs.shape[0] // 4
         first_part = partner(coeffs[:half_rows], "pair", LEVEL)
         second_part = partner(coeffs[half_rows:], "pair", LEVEL)
         summed = col_sum(split_product(own_coupling, [(0, first_part), (half_rows, second_part)]))
         driven = (own_incident.astype(jnp.float32) + summed).astype(jnp.bfloat16)
         coeffs = col_sum(product(own_matrix, driven)).astype(jnp.bfloat16)
-    outgoing = pick_half(coeffs, 1 - column_half, half_width)
-    tail_rows = outgoing.shape[0] // 2
-    incoming_parts = [
-        partner(outgoing[:tail_rows], "pair", LEVEL),
-        partner(outgoing[tail_rows:], "pair", LEVEL),
-    ]
+    incoming = partner(pick_half(coeffs, 1 - column_half, half_width), "pair", LEVEL)
     own_half = pick_half(coeffs, column_half, half_width)
     total_rows = farfield.shape[1]
     own_field = product(farfield, own_half)
-    other_field = split_product(farfield, [(0, incoming_parts[0]), (tail_rows, incoming_parts[1])])
+    other_field = product(farfield, incoming)
     merged = rotate(own_field, direction_phase(own_centre, total_rows, total_rows)) + rotate(
         other_field, direction_phase(other_centre, total_rows, total_rows)
     )

time: 274 us -> 278 us (1.015)
  blocking collectives: 178 us -> 182 us
    all_to_all x7, blocking collectives: 178 us -> 182 us  [col_sum(): received = lax.all_to_all(blocks, 'col', 0, 0)]
    ppermute x8 -> x7, starting transfers between devices: 14.5 us -> 13.1 us  [partner(): return lax.ppermute(value, axis, pairs)]
    ppermute x8 -> x7, waiting for transfers between devices: 11.4 us -> 10.7 us  [partner(): return lax.ppermute(value, axis, pairs)]
    dot_general x13 -> x12, matrix products: 39.8 us -> 39.5 us  [product(): jnp.einsum('prc,pck->rk', matrix, stacked, preferred_element_type=jnp.flo...]
  transfers between devices with their start and end apart: 9 -> 8, of which waited for: 5 -> 8; matrix products, arithmetic and copies ran while one was open for 9% -> 7% of each run, Pallas kernels for 0% -> 0%
where the time goes in v8:
time: 278 us; the launch traced here: 275 us
  blocking collectives  182 us (65%)
  matrix products  39.5 us (14%)
  waiting for transfers between devices  18.5 us (7%)
  starting transfers between devices  16.7 us (6%)
  other arithmetic  12.1 us (4%)
  local copies, waits for them, and re-layouts  5.37 us (2%)
    all_to_all x7, blocking collectives, col_sum(): received = lax.all_to_all(blocks, 'col', 0, 0)  182 us
    dot_general x12, matrix products, product(): jnp.einsum('prc,pck->rk', matrix, stacked, preferred_element_type=jnp.flo...  39.5 us
    ppermute x7, starting transfers between devices, partner(): return lax.ppermute(value, axis, pairs)  13.1 us
    ppermute x7, waiting for transfers between devices, partner(): return lax.ppermute(value, axis, pairs)  10.7 us
    all_to_all x1, waiting for transfers between devices, col_sum(): received = lax.all_to_all(blocks, 'col', 0, 0)  7.86 us
  transfers between devices with their start and end apart: 8, of which 8 were waited for; matrix products, arithmetic and copies ran while one was open for 7% of the time, Pallas kernels for 0%

profile of v8, /device:TPU:0, one launch (start us, length us, event | category | flops | bytes accessed | tf_op | source)
XLA Modules:
  0.0 274.6 jit_solution(18215199298695500879)
XLA Ops:
  0.0 1.1 copy.9
  1.2 5.8 %fusion.32 = bf16[256,4096]{1,0:T(8,128)(2,1)S(1)} fusion(bf16[1,2,4096,512]{3,2,1,0:T(8,128)(2,1)} %param.5, bf16[1,512,256]{1,2,0:T(8,128)(2,1)S(1)} %maximum_bitcast_fusion, bf16[1,512,256]{1,2,0:T(8,128)(2,1)S(1)} %copy.9), kind=kOutput, calls=%fused_computation.24 | convolution fusion | flops 2148794368 | bytes 11010048 | tf_op jit(solution)/shard_map/prc,pck->rk/dot_general | solution.py:66
  7.1 36.2 %all_to_all.40 = bf16[8,512,256]{1,2,0:T(8,128)(2,1)S(1)} all-to-all(bf16[8,512,256]{1,2,0:T(8,128)(2,1)S(1)} %bitcast.188), channel_id=1, replica_groups=mesh['pair'=16,'col'=8] {'col'}, dimensions={0} | all-to-all | bytes 4194304 | tf_op jit(solution)/shard_map/all_to_all | solution.py:60
  43.3 0.4 reduce_sum.90
  43.7 3.1 %collective-permute-start.1 = (bf16[128,256]{0,1:T(8,128)(2,1)S(1)}, bf16[128,256]{0,1:T(8,128)(2,1)S(1)}, u32[]{:S(2)}, u32[]{:S(2)}) collective-permute-start(bf16[128,256]{0,1:T(8,128)(2,1)S(1)} %slice.176), channel_id=1, source_target_pairs={{0,32},{8,40},{16,48},{24,56},{32,0},{40,8},{48,16},{56,24},{64,96... | collective-permute-start | bytes 196616 | tf_op jit(solution)/shard_map/ppermute | solution.py:16
  46.9 0.6 collective-permute-start
  47.4 2.8 %collective-permute-done.1 = bf16[128,256]{0,1:T(8,128)(2,1)S(1)} collective-permute-done((bf16[128,256]{0,1:T(8,128)(2,1)S(1)}, bf16[128,256]{0,1:T(8,128)(2,1)S(1)}, u32[]{:S(2)}, u32[]{:S(2)}) %collective-permute-start.1) | collective-permute-done | bytes 65568 | tf_op jit(solution)/shard_map/ppermute | solution.py:16
  50.3 2.3 convolution_bitcast_fusion.4
  52.6 1.5 collective-permute-done
  54.2 4.8 %fusion.37 = bf16[4096,256]{0,1:T(8,128)(2,1)S(1)} fusion(f32[4096,256]{0,1:T(8,128)S(1)} %convolution_bitcast_fusion.4, bf16[2,4096,512]{2,1,0:T(8,128)(2,1)} %bitcast.195, bf16[1,384,256]{1,2,0:T(8,128)(2,1)S(1)} %maximum_bitcast_fusion.4, bf16[1,384,256]{1,2,0:T(8,128)(2,1)S(1)} %bitcast.220), kind=kOutput, calls=%fused_computation.27 | convolution fusion | flops 1612906496 | bytes 12976128 | tf_op jit(solution)/shard_map/prc,pck->rk/dot_general | solution.py:66
  59.2 28.9 %all_to_all.41 = bf16[8,512,256]{1,2,0:T(8,128)(2,1)S(1)} all-to-all(bf16[8,512,256]{1,2,0:T(8,128)(2,1)S(1)} %bitcast.189), channel_id=1, replica_groups=mesh['pair'=16,'col'=8] {'col'}, dimensions={0} | all-to-all | bytes 4194304 | tf_op jit(solution)/shard_map/all_to_all | solution.py:60
  88.0 0.3 convert_reduce_fusion.2
  88.6 2.4 fusion.29
  91.2 28.1 %all_to_all.42 = bf16[8,512,256]{1,2,0:T(8,128)(2,1)S(1)} all-to-all(bf16[8,512,256]{1,2,0:T(8,128)(2,1)S(1)} %bitcast.190), channel_id=1, replica_groups=mesh['pair'=16,'col'=8] {'col'}, dimensions={0} | all-to-all | bytes 4194304 | tf_op jit(solution)/shard_map/all_to_all | solution.py:60
  119.3 0.4 reduce_sum.93
  119.7 1.8 collective-permute-start.3
  121.5 1.9 collective-permute-start.2
  123.4 2.1 collective-permute-done.3
  125.6 2.3 convolution_bitcast_fusion.2
  127.9 0.8 collective-permute-done.2
  128.8 4.8 %fusion.36 = bf16[4096,256]{0,1:T(8,128)(2,1)S(1)} fusion(f32[4096,256]{0,1:T(8,128)S(1)} %convolution_bitcast_fusion.2, bf16[2,4096,512]{2,1,0:T(8,128)(2,1)} %bitcast.197, bf16[1,384,256]{1,2,0:T(8,128)(2,1)S(1)} %maximum_bitcast_fusion.5, bf16[1,384,256]{1,2,0:T(8,128)(2,1)S(1)} %bitcast.221), kind=kOutput, calls=%fused_computation.26 | convolution fusion | flops 1612906496 | bytes 12976128 | tf_op jit(solution)/shard_map/prc,pck->rk/dot_general | solution.py:66
  133.8 26.0 %all_to_all.43 = bf16[8,512,256]{1,2,0:T(8,128)(2,1)S(1)} all-to-all(bf16[8,512,256]{1,2,0:T(8,128)(2,1)S(1)} %bitcast.191), channel_id=1, replica_groups=mesh['pair'=16,'col'=8] {'col'}, dimensions={0} | all-to-all | bytes 4194304 | tf_op jit(solution)/shard_map/all_to_all | solution.py:60
  160.3 2.4 fusion.26
  162.9 25.1 %all_to_all.44 = bf16[8,512,256]{1,2,0:T(8,128)(2,1)S(1)} all-to-all(bf16[8,512,256]{1,2,0:T(8,128)(2,1)S(1)} %bitcast.192), channel_id=1, replica_groups=mesh['pair'=16,'col'=8] {'col'}, dimensions={0} | all-to-all | bytes 4194304 | tf_op jit(solution)/shard_map/all_to_all | solution.py:60
  188.0 0.4 reduce_sum.96
  188.4 1.7 collective-permute-start.5
  190.1 2.0 collective-permute-start.4
  192.1 2.1 collective-permute-done.5
  194.2 2.3 convolution_bitcast_fusion
  196.6 0.8 collective-permute-done.4
  197.4 4.8 %fusion.35 = bf16[4096,256]{0,1:T(8,128)(2,1)S(1)} fusion(f32[4096,256]{0,1:T(8,128)S(1)} %convolution_bitcast_fusion, bf16[2,4096,512]{2,1,0:T(8,128)(2,1)} %bitcast.199, bf16[1,384,256]{1,2,0:T(8,128)(2,1)S(1)} %maximum_bitcast_fusion.6, bf16[1,384,256]{1,2,0:T(8,128)(2,1)S(1)} %bitcast.222), kind=kOutput, calls=%fused_computation.25 | convolution fusion | flops 1612906496 | bytes 12976128 | tf_op jit(solution)/shard_map/prc,pck->rk/dot_general | solution.py:66
  202.4 23.0 %all_to_all.45 = bf16[8,512,256]{1,2,0:T(8,128)(2,1)S(1)} all-to-all(bf16[8,512,256]{1,2,0:T(8,128)(2,1)S(1)} %bitcast.193), channel_id=1, replica_groups=mesh['pair'=16,'col'=8] {'col'}, dimensions={0} | all-to-all | bytes 4194304 | tf_op jit(solution)/shard_map/all_to_all | solution.py:60
  225.9 2.4 fusion.23
  228.3 1.5 copy.48
  229.9 3.6 %all-to-all-start.6 = ((bf16[8,512,256]{1,2,0:T(8,128)(2,1)}), bf16[8,512,256]{1,2,0:T(8,128)(2,1)S(1)}, u32[]{:S(2)}, u32[]{:S(2)}) async-start(bf16[8,512,256]{1,2,0:T(8,128)(2,1)} %bitcast.187), calls=%async_computation.6 | async-start | bytes 4194304 | tf_op jit(solution)/shard_map/all_to_all | solution.py:60
  233.6 0.6 fusion.124
  234.2 2.1 fusion.107
  236.3 2.1 fusion.108
  238.4 1.9 fusion.109
  240.3 1.9 fusion.110
  242.2 7.9 %all-to-all-done.6 = bf16[8,512,256]{1,2,0:T(8,128)(2,1)S(1)} async-done(((bf16[8,512,256]{1,2,0:T(8,128)(2,1)}), bf16[8,512,256]{1,2,0:T(8,128)(2,1)S(1)}, u32[]{:S(2)}, u32[]{:S(2)}) %all-to-all-start.6) | async-done | bytes 2097184 | tf_op jit(solution)/shard_map/all_to_all | solution.py:60
  250.1 0.4 reduce_sum.99
  250.5 2.0 collective-permute-start.6
  252.5 3.8 %convolution_bitcast_fusion.7 = f32[2048,128]{0,1:T(8,128)S(1)} fusion(bf16[2,2048,512]{2,1,0:T(8,128)(2,1)} %param.8, bf16[1,512,128]{1,2,0:T(8,128)(2,1)S(1)} %get-tuple-element.33, bf16[1,512,128]{1,2,0:T(8,128)(2,1)S(1)} %get-tuple-element.32), kind=kOutput, calls=%fused_computation.35 | convolution fusion | flops 537001984 | bytes 5505024 | tf_op jit(solution)/shard_map/prc,pck->rk/dot_general | solution.py:66
  256.6 0.5 collective-permute-done.6
  257.1 1.5 convolution_bitcast_fusion.6
  259.1 14.7 %all_to_all.46 = bf16[8,256,128]{1,2,0:T(8,128)(2,1)S(1)} all-to-all(bf16[8,256,128]{1,2,0:T(8,128)(2,1)S(1)} %fusion.44), channel_id=1, replica_groups=mesh['pair'=16,'col'=8] {'col'}, dimensions={0} | all-to-all | bytes 1048576 | tf_op jit(solution)/shard_map/all_to_all | solution.py:60
  273.9 0.8 copy.24
  (73 shorter events, 3.6 us)
Async XLA Ops:
  43.7 6.5 %collective-permute-start.1 = (bf16[128,256]{0,1:T(8,128)(2,1)S(1)}, bf16[128,256]{0,1:T(8,128)(2,1)S(1)}, u32[]{:S(2)}, u32[]{:S(2)}) collective-permute-start(bf16[128,256]{0,1:T(8,128)(2,1)S(1)} %slice.176), channel_id=1, source_target_pairs={{0,32},{8,40},{16,48},{24,56},{32,0},{40,8},{48,16},{56,24},{64,96... | collective-permute-start | bytes 196616 | tf_op jit(solution)/shard_map/ppermute | solution.py:16
  46.9 7.3 %collective-permute-start = (bf16[384,256]{0,1:T(8,128)(2,1)S(1)}, bf16[384,256]{0,1:T(8,128)(2,1)S(1)}, u32[]{:S(2)}, u32[]{:S(2)}) collective-permute-start(bf16[384,256]{0,1:T(8,128)(2,1)S(1)} %slice.172), channel_id=1, source_target_pairs={{0,32},{8,40},{16,48},{24,56},{32,0},{40,8},{48,16},{56,24},{64,96... | collective-permute-start | bytes 589832 | tf_op jit(solution)/shard_map/ppermute | solution.py:16
  54.2 34.4 %slice-start = ((s8[8388608]{0:T(1024)(128)(4,1)}), s8[4194304]{0:T(1024)(128)(4,1)S(1)}, s32[]{:S(2)}) async-start(s8[8388608]{0:T(1024)(128)(4,1)} %bitcast.223), calls=%async_computation.8 | async-start | bytes 8388608
  58.9 29.6 %slice-start.1 = ((s8[8388608]{0:T(1024)(128)(4,1)}), s8[4194304]{0:T(1024)(128)(4,1)S(1)}, s32[]{:S(2)}) async-start(s8[8388608]{0:T(1024)(128)(4,1)} %bitcast.223), calls=%async_computation.9 | async-start | bytes 8388608
  119.7 5.8 %collective-permute-start.3 = (bf16[128,256]{0,1:T(8,128)(2,1)S(1)}, bf16[128,256]{0,1:T(8,128)(2,1)S(1)}, u32[]{:S(2)}, u32[]{:S(2)}) collective-permute-start(bf16[128,256]{0,1:T(8,128)(2,1)S(1)} %slice.185), channel_id=1, source_target_pairs={{0,32},{8,40},{16,48},{24,56},{32,0},{40,8},{48,16},{56,24},{64,96... | collective-permute-start | bytes 196616 | tf_op jit(solution)/shard_map/ppermute | solution.py:16
  121.5 7.3 %collective-permute-start.2 = (bf16[384,256]{0,1:T(8,128)(2,1)S(1)}, bf16[384,256]{0,1:T(8,128)(2,1)S(1)}, u32[]{:S(2)}, u32[]{:S(2)}) collective-permute-start(bf16[384,256]{0,1:T(8,128)(2,1)S(1)} %slice.182), channel_id=1, source_target_pairs={{0,32},{8,40},{16,48},{24,56},{32,0},{40,8},{48,16},{56,24},{64,96... | collective-permute-start | bytes 589832 | tf_op jit(solution)/shard_map/ppermute | solution.py:16
  128.8 31.5 %slice-start.2 = ((s8[8388608]{0:T(1024)(128)(4,1)}), s8[4194304]{0:T(1024)(128)(4,1)S(1)}, s32[]{:S(2)}) async-start(s8[8388608]{0:T(1024)(128)(4,1)} %bitcast.225), calls=%async_computation.10 | async-start | bytes 8388608
  133.6 26.7 %slice-start.3 = ((s8[8388608]{0:T(1024)(128)(4,1)}), s8[4194304]{0:T(1024)(128)(4,1)S(1)}, s32[]{:S(2)}) async-start(s8[8388608]{0:T(1024)(128)(4,1)} %bitcast.225), calls=%async_computation.11 | async-start | bytes 8388608
  188.4 5.8 %collective-permute-start.5 = (bf16[128,256]{0,1:T(8,128)(2,1)S(1)}, bf16[128,256]{0,1:T(8,128)(2,1)S(1)}, u32[]{:S(2)}, u32[]{:S(2)}) collective-permute-start(bf16[128,256]{0,1:T(8,128)(2,1)S(1)} %slice.193), channel_id=1, source_target_pairs={{0,32},{8,40},{16,48},{24,56},{32,0},{40,8},{48,16},{56,24},{64,96... | collective-permute-start | bytes 196616 | tf_op jit(solution)/shard_map/ppermute | solution.py:16
  190.1 7.3 %collective-permute-start.4 = (bf16[384,256]{0,1:T(8,128)(2,1)S(1)}, bf16[384,256]{0,1:T(8,128)(2,1)S(1)}, u32[]{:S(2)}, u32[]{:S(2)}) collective-permute-start(bf16[384,256]{0,1:T(8,128)(2,1)S(1)} %slice.190), channel_id=1, source_target_pairs={{0,32},{8,40},{16,48},{24,56},{32,0},{40,8},{48,16},{56,24},{64,96... | collective-permute-start | bytes 589832 | tf_op jit(solution)/shard_map/ppermute | solution.py:16
  197.4 28.5 %slice-start.4 = ((s8[8388608]{0:T(1024)(128)(4,1)}), s8[4194304]{0:T(1024)(128)(4,1)S(1)}, s32[]{:S(2)}) async-start(s8[8388608]{0:T(1024)(128)(4,1)} %bitcast.227), calls=%async_computation.12 | async-start | bytes 8388608
  202.2 23.7 %slice-start.5 = ((s8[8388608]{0:T(1024)(128)(4,1)}), s8[4194304]{0:T(1024)(128)(4,1)S(1)}, s32[]{:S(2)}) async-start(s8[8388608]{0:T(1024)(128)(4,1)} %bitcast.227), calls=%async_computation.13 | async-start | bytes 8388608
  228.3 5.1 %copy-start.1 = (s32[16,3]{0,1:T(4,128)S(1)}, s32[16,3]{0,1:T(4,128)}, u32[]{:S(2)}) copy-start(s32[16,3]{0,1:T(4,128)} %param.9) | copy-start | bytes 580
  229.9 20.2 %all-to-all-start.6 = ((bf16[8,512,256]{1,2,0:T(8,128)(2,1)}), bf16[8,512,256]{1,2,0:T(8,128)(2,1)S(1)}, u32[]{:S(2)}, u32[]{:S(2)}) async-start(bf16[8,512,256]{1,2,0:T(8,128)(2,1)} %bitcast.187), calls=%async_computation.6 | async-start | bytes 4194304 | tf_op jit(solution)/shard_map/all_to_all | solution.py:60
  250.5 6.6 %collective-permute-start.6 = (bf16[512,128]{0,1:T(8,128)(2,1)S(1)}, bf16[512,128]{0,1:T(8,128)(2,1)S(1)}, u32[]{:S(2)}, u32[]{:S(2)}) collective-permute-start(bf16[512,128]{0,1:T(8,128)(2,1)S(1)} %pad_maximum_fusion), channel_id=1, source_target_pairs={{0,32},{8,40},{16,48},{24,56},{32,0},{40,8},{48,16},{56,24},{64,96... | collective-permute-start | bytes 393224 | tf_op jit(solution)/shard_map/ppermute | solution.py:16
  252.5 4.6 %copy-start = (bf16[2,2048,512]{2,1,0:T(8,128)(2,1)S(1)}, bf16[2,2048,512]{2,1,0:T(8,128)(2,1)}, u32[]{:S(2)}) copy-start(bf16[2,2048,512]{2,1,0:T(8,128)(2,1)} %param.8) | copy-start | bytes 12582916
